TPU v7x, 512 devices: a whole 4x8x8 slice. The times are simulated.
512 devices in a mesh: heads: 8 (over y), ctx: 64 (over z, x, core).
Axes of the slice: x: 4, y: 8, z: 8, core: 2. Of those that a mesh axis runs over, the one named last changes fastest.
Arguments:
- queries: bfloat16 [16384, 4096], P('ctx', 'heads'), may hold values from -6 to 6
- keys: bfloat16 [16384, 1024], P('ctx', 'heads'), may hold values from -6 to 6
- values: bfloat16 [16384, 1024], P('ctx', 'heads'), may hold values from -6 to 6
- out_weight: bfloat16 [4096, 4096], P('heads'), may hold values from -0.09375 to 0.09375
- out_grad: bfloat16 [4096, 16384], P('heads', 'ctx'), may hold values from -6 to 6
- doc_lengths: int32 [16], replicated, may hold values from 1 to 1792, 16384 in all
Outputs:
- out_t: bfloat16 [4096, 16384], P('heads', 'ctx')
- grad_q: bfloat16 [16384, 4096], P('ctx', 'heads')
- grad_k: bfloat16 [16384, 1024], P('ctx', 'heads')
- grad_v: bfloat16 [16384, 1024], P('ctx', 'heads')
Inputs may be any that keep to these rules, and one draw needn't show every extreme that they name: `doc_lengths`: the 16 lengths sum to 16384; the longest document has exactly 1792 tokens.
All inputs are finite; a program needn't handle non-finite values.
Results may differ from a plain program's by a relative error of at most 0.02.
Values may be sent and summed in bfloat16 or wider, within the bound.
No kernel may reach another device: no remote copies, remote signals or barrier semaphores. Data moves between devices by JAX's collectives and lax.ppermute only.
A program may use at most 64 MiB of HBM per device.

v0:
```python
import math

import jax
import jax.numpy as jnp
from jax import lax
from jax.sharding import PartitionSpec as P

REACH = 7


def passed_along(value, axis, steps):
    count = lax.axis_size(axis)
    first, last = (max(0, -steps), min(count, count - steps))
    return lax.ppermute(value, axis, [(source, source + steps) for source in range(first, last)])


def per_device(queries, keys, values, out_weight, out_grad, doc_lengths):
    tok_rows = queries.shape[0]
    head_dim = keys.shape[1]
    group_size = queries.shape[1] // head_dim
    scaling = 1.0 / math.sqrt(head_dim)
    shard = lax.axis_index("ctx")
    doc_ends = jnp.cumsum(doc_lengths)
    starts = doc_ends - doc_lengths
    positions = shard * tok_rows + jnp.arange(tok_rows, dtype=jnp.int32)
    first_key = jnp.max(
        jnp.where(starts[None, :] <= positions[:, None], starts[None, :], 0), axis=1
    )
    stacked = jnp.concatenate([keys, values], axis=1)
    blocks = [stacked[None]]
    for offset in range(1, REACH + 1):
        blocks.append(passed_along(stacked, "ctx", offset)[None])
    window = jnp.concatenate(blocks, axis=0)
    num_blocks = window.shape[0]
    flat_keys = window[:, :, :head_dim].reshape(num_blocks * tok_rows, head_dim)
    flat_values = window[:, :, head_dim:].reshape(num_blocks * tok_rows, head_dim)
    key_pos = (
        (shard - jnp.arange(num_blocks, dtype=jnp.int32))[:, None] * tok_rows
        + jnp.arange(tok_rows, dtype=jnp.int32)[None, :]
    ).reshape(-1)
    visible = (key_pos[None, :] >= first_key[:, None]) & (key_pos[None, :] <= positions[:, None])
    query_heads = queries.reshape(tok_rows, group_size, head_dim)
    scores = (
        jnp.einsum("tgd,kd->gtk", query_heads, flat_keys, preferred_element_type=jnp.float32)
        * scaling
    )
    scores = jnp.where(visible[None], scores, -jnp.inf)
    largest = jnp.max(scores, axis=-1, keepdims=True)
    expons = jnp.exp(scores - largest)
    weights = expons / jnp.sum(expons, axis=-1, keepdims=True)
    probs = weights.astype(jnp.bfloat16)
    attn_heads = jnp.einsum(
        "gtk,kd->tgd", probs, flat_values, preferred_element_type=jnp.float32
    ).astype(jnp.bfloat16)
    attn = attn_heads.reshape(tok_rows, group_size * head_dim)
    columns = out_weight
    out_t = lax.psum_scatter(
        lax.dot_general(
            columns, attn, (((0,), (1,)), ((), ())), preferred_element_type=jnp.float32
        ),
        "heads",
        scatter_dimension=0,
        tiled=True,
    ).astype(jnp.bfloat16)
    columns = out_weight
    grad_attn = jnp.dot(
        columns,
        lax.all_gather(out_grad, "heads", axis=0, tiled=True),
        preferred_element_type=jnp.float32,
    ).astype(jnp.bfloat16)
    grad_heads = grad_attn.reshape(group_size, head_dim, tok_rows)
    delta_sum = jnp.einsum(
        "tgd,gdt->gt", attn_heads, grad_heads, preferred_element_type=jnp.float32
    )
    grad_probs = jnp.einsum(
        "gdt,kd->gtk", grad_heads, flat_values, preferred_element_type=jnp.float32
    )
    dscore = (weights * (grad_probs - delta_sum[:, :, None]) * scaling).astype(jnp.bfloat16)
    grad_q = (
        jnp.einsum("gtk,kd->tgd", dscore, flat_keys, preferred_element_type=jnp.float32)
        .astype(jnp.bfloat16)
        .reshape(tok_rows, group_size * head_dim)
    )
    key_part = jnp.einsum("gtk,tgd->kd", dscore, query_heads, preferred_element_type=jnp.float32)
    value_part = jnp.einsum("gtk,gdt->kd", probs, grad_heads, preferred_element_type=jnp.float32)
    partial_grads = jnp.concatenate([key_part, value_part], axis=1).reshape(
        num_blocks, tok_rows, 2 * head_dim
    )
    summed = partial_grads[0]
    for offset in range(1, num_blocks):
        summed = summed + passed_along(partial_grads[offset], "ctx", -offset)
    grad_k = summed[:, :head_dim].astype(jnp.bfloat16)
    grad_v = summed[:, head_dim:].astype(jnp.bfloat16)
    return (out_t, grad_q, grad_k, grad_v)


def solution(mesh):
    placed = (
        P("ctx", "heads"),
        P("ctx", "heads"),
        P("ctx", "heads"),
        P("heads", None),
        P("heads", "ctx"),
        P(),
    )
    return jax.shard_map(
        per_device,
        mesh=mesh,
        in_specs=placed,
        out_specs=(P("heads", "ctx"), P("ctx", "heads"), P("ctx", "heads"), P("ctx", "heads")),
        check_vma=False,
    )
```

profile of v0, /device:TPU:10, one launch (start us, length us, event | category | flops | bytes accessed | tf_op | source)
XLA Modules:
  0.0 153.6 jit_solution(13572130763276567545)
XLA Ops:
  7.2 0.0 all-gather.2.cloned.1.call-start
  7.2 0.9 constant_dynamic-update-slice_fusion.1
  8.1 0.9 constant_dynamic-update-slice_fusion
  8.9 3.7 %collective-permute-start.6 = (bf16[256,256]{1,0:T(8,128)(2,1)S(1)}, bf16[256,256]{1,0:T(8,128)(2,1)S(1)}, u32[]{:S(2)}, u32[]{:S(2)}) collective-permute-start(bf16[256,256]{1,0:T(8,128)(2,1)S(1)} %constant_dynamic-update-slice_fusion), channel_id=1, source_target_pairs={{0,7},{1,8},{2,9},{3,10},{4,11},{5,12},{6,13},{7,14},{8,15},{9,16}... | collective-permute-start | bytes 393224 | tf_op jit(solution)/shard_map/ppermute | solution.py:14
  12.6 4.7 %collective-permute-start.5 = (bf16[256,256]{1,0:T(8,128)(2,1)S(1)}, bf16[256,256]{1,0:T(8,128)(2,1)S(1)}, u32[]{:S(2)}, u32[]{:S(2)}) collective-permute-start(bf16[256,256]{1,0:T(8,128)(2,1)S(1)} %constant_dynamic-update-slice_fusion), channel_id=1, source_target_pairs={{0,6},{1,7},{2,8},{3,9},{4,10},{5,11},{6,12},{7,13},{8,14},{9,15},... | collective-permute-start | bytes 393224 | tf_op jit(solution)/shard_map/ppermute | solution.py:14
  17.3 3.9 %collective-permute-start.4 = (bf16[256,256]{1,0:T(8,128)(2,1)S(1)}, bf16[256,256]{1,0:T(8,128)(2,1)S(1)}, u32[]{:S(2)}, u32[]{:S(2)}) collective-permute-start(bf16[256,256]{1,0:T(8,128)(2,1)S(1)} %constant_dynamic-update-slice_fusion), channel_id=1, source_target_pairs={{0,5},{1,6},{2,7},{3,8},{4,9},{5,10},{6,11},{7,12},{8,13},{9,14},{... | collective-permute-start | bytes 393224 | tf_op jit(solution)/shard_map/ppermute | solution.py:14
  21.3 4.8 %collective-permute-start.3 = (bf16[256,256]{1,0:T(8,128)(2,1)S(1)}, bf16[256,256]{1,0:T(8,128)(2,1)S(1)}, u32[]{:S(2)}, u32[]{:S(2)}) collective-permute-start(bf16[256,256]{1,0:T(8,128)(2,1)S(1)} %constant_dynamic-update-slice_fusion), channel_id=1, source_target_pairs={{0,4},{1,5},{2,6},{3,7},{4,8},{5,9},{6,10},{7,11},{8,12},{9,13},{1... | collective-permute-start | bytes 393224 | tf_op jit(solution)/shard_map/ppermute | solution.py:14
  26.1 1.9 %collective-permute-start = (bf16[256,256]{1,0:T(8,128)(2,1)S(1)}, bf16[256,256]{1,0:T(8,128)(2,1)S(1)}, u32[]{:S(2)}, u32[]{:S(2)}) collective-permute-start(bf16[256,256]{1,0:T(8,128)(2,1)S(1)} %constant_dynamic-update-slice_fusion), channel_id=1, source_target_pairs={{0,1},{1,2},{2,3},{3,4},{4,5},{5,6},{6,7},{7,8},{8,9},{9,10},{10,1... | collective-permute-start | bytes 393224 | tf_op jit(solution)/shard_map/ppermute | solution.py:14
  28.0 0.0 all-gather.2.cloned.1.call-update
  28.0 0.0 reduce-scatter.2.cloned.1.call-start
  28.1 0.1 add_bitcast_fusion
  28.2 0.7 copy.43
  29.0 0.1 reduce.1
  29.1 0.7 sub.31
  29.8 0.1 select_reduce_fusion
  29.8 0.6 compare_and_fusion
  30.4 1.1 copy.75
  31.5 0.8 collective-permute-done
  32.4 3.4 %collective-permute-start.1 = (bf16[256,256]{1,0:T(8,128)(2,1)S(1)}, bf16[256,256]{1,0:T(8,128)(2,1)S(1)}, u32[]{:S(2)}, u32[]{:S(2)}) collective-permute-start(bf16[256,256]{1,0:T(8,128)(2,1)S(1)} %constant_dynamic-update-slice_fusion), channel_id=1, source_target_pairs={{0,2},{1,3},{2,4},{3,5},{4,6},{5,7},{6,8},{7,9},{8,10},{9,11},{10,... | collective-permute-start | bytes 393224 | tf_op jit(solution)/shard_map/ppermute | solution.py:14
  35.8 4.6 %collective-permute-done.1 = bf16[256,256]{1,0:T(8,128)(2,1)S(1)} collective-permute-done((bf16[256,256]{1,0:T(8,128)(2,1)S(1)}, bf16[256,256]{1,0:T(8,128)(2,1)S(1)}, u32[]{:S(2)}, u32[]{:S(2)}) %collective-permute-start.1) | collective-permute-done | bytes 131104 | tf_op jit(solution)/shard_map/ppermute | solution.py:14
  40.4 2.9 %collective-permute-start.2 = (bf16[256,256]{1,0:T(8,128)(2,1)S(1)}, bf16[256,256]{1,0:T(8,128)(2,1)S(1)}, u32[]{:S(2)}, u32[]{:S(2)}) collective-permute-start(bf16[256,256]{1,0:T(8,128)(2,1)S(1)} %constant_dynamic-update-slice_fusion), channel_id=1, source_target_pairs={{0,3},{1,4},{2,5},{3,6},{4,7},{5,8},{6,9},{7,10},{8,11},{9,12},{10... | collective-permute-start | bytes 393224 | tf_op jit(solution)/shard_map/ppermute | solution.py:14
  43.4 2.5 %collective-permute-done.2 = bf16[256,256]{1,0:T(8,128)(2,1)S(1)} collective-permute-done((bf16[256,256]{1,0:T(8,128)(2,1)S(1)}, bf16[256,256]{1,0:T(8,128)(2,1)S(1)}, u32[]{:S(2)}, u32[]{:S(2)}) %collective-permute-start.2) | collective-permute-done | bytes 131104 | tf_op jit(solution)/shard_map/ppermute | solution.py:14
  45.9 0.0 collective-permute-done.3
  45.9 0.0 collective-permute-done.4
  45.9 0.0 collective-permute-done.5
  46.0 0.0 collective-permute-done.6
  46.0 0.3 fusion.26
  46.3 4.8 %fusion.28 = (f32[4,256]{1,0:T(4,128)S(1)}, f32[4,256,2048]{1,2,0:T(8,128)}) fusion(pred[256,2048]{0,1:T(8,128)(4,1)S(1)} %compare_and_fusion, bf16[2048,128,1]{1,0,2:T(8,128)(2,1)S(1)} %bitcast.79, bf16[256,4,128]{0,2,1:T(8,128)(2,1)S(1)} %bitcast.86), kind=kOutput, calls=%fused_computation.68 | convolution fusion | flops 545261568 | bytes 9703424 | tf_op jit(solution)/shard_map/sub | solution.py:49
  51.1 6.0 %fusion.5 = bf16[4,256,2048]{1,2,0:T(8,128)(2,1)} fusion(f32[4,256,2048]{1,2,0:T(8,128)} %get-tuple-element.28, f32[4,256]{1,0:T(4,128)S(1)} %get-tuple-element.27), kind=kLoop, calls=%fused_computation.24 | loop fusion | flops 4194304 | bytes 12587008 | tf_op jit(solution)/shard_map/convert_element_type | solution.py:51
  57.1 18.4 %all-gather.2.cloned.1.call-done = bf16[4096,256]{1,0:T(8,128)(2,1)} async-done(((bf16[512,256]{1,0:T(8,128)(2,1)}), bf16[4096,256]{1,0:T(8,128)(2,1)}) %all-gather.2.cloned.1.call-update) | async-done | bytes 2097168 | tf_op jit(solution)/shard_map/all_gather | solution.py:68
  75.6 0.0 copy-start
  75.6 4.2 %convolution_convert_fusion = bf16[512,256]{1,0:T(8,128)(2,1)S(1)} fusion(bf16[512,4096]{1,0:T(8,128)(2,1)} %param.9, bf16[4096,256]{1,0:T(8,128)(2,1)} %all-gather.2.cloned.1.call-done), kind=kOutput, calls=%fused_computation.28 | convolution fusion | flops 1073872896 | bytes 6553600 | tf_op jit(solution)/shard_map/dot_general | solution.py:66
  79.8 0.0 copy-start.1
  79.9 0.0 copy-done
  79.9 0.8 fusion.8
  80.7 1.4 copy-done.1
  82.0 3.3 %convolution_bitcast_fusion = f32[4096,256]{0,1:T(8,128)} fusion(bf16[256,512]{0,1:T(8,128)(2,1)S(1)} %bitcast.83, bf16[512,4096]{1,0:T(8,128)(2,1)S(1)} %copy-done.1), kind=kOutput, calls=%fused_computation.5 | convolution fusion | flops 1073741824 | bytes 8650752 | tf_op jit(solution)/shard_map/dot_general | solution.py:58
  85.3 0.0 reduce-scatter.2.cloned.1.call-update
  85.3 3.6 %convolution_bitcast_fusion.1 = f32[2048,128]{0,1:T(8,128)S(1)} fusion(bf16[4,256,2048]{1,2,0:T(8,128)(2,1)} %fusion.5, bf16[4,128,256]{2,1,0:T(8,128)(2,1)S(1)} %bitcast.84), kind=kOutput, calls=%fused_computation.25 | convolution fusion | flops 536870912 | bytes 5505024 | tf_op jit(solution)/shard_map/gtk,gdt->kd/dot_general | solution.py:85
  89.0 4.3 %multiply_convert_fusion = bf16[4,256,2048]{1,2,0:T(8,128)(2,1)S(1)} fusion(bf16[2048,128,1]{1,0,2:T(8,128)(2,1)S(1)} %bitcast.82, bf16[4,128,256]{2,1,0:T(8,128)(2,1)S(1)} %bitcast.85, f32[4,256]{1,0:T(4,128)S(1)} %get-tuple-element.29, f32[4,256,2048]{1,2,0:T(8,128)} %get-tuple-element.28, f32[4,256]{1,0:T(4,128)S(1)} %get-tuple-element.27), kind=kOutput, calls=%fused_computation.2 | convolution fusion | flops 547356672 | bytes 13377536 | tf_op jit(solution)/shard_map/gdt,kd->gtk/dot_general | solution.py:75
  93.3 1.5 convolution_bitcast_fusion.2
  94.8 1.1 fusion.18
  95.9 1.9 %collective-permute-start.7 = (f32[256,256]{0,1:T(8,128)S(1)}, f32[256,256]{0,1:T(8,128)S(1)}, u32[]{:S(2)}, u32[]{:S(2)}) collective-permute-start(f32[256,256]{0,1:T(8,128)S(1)} %get-tuple-element.16), channel_id=1, source_target_pairs={{1,0},{2,1},{3,2},{4,3},{5,4},{6,5},{7,6},{8,7},{9,8},{10,9},{11,1... | collective-permute-start | bytes 786440 | tf_op jit(solution)/shard_map/ppermute | solution.py:14
  97.8 1.9 %collective-permute-start.8 = (f32[256,256]{0,1:T(8,128)S(1)}, f32[256,256]{0,1:T(8,128)S(1)}, u32[]{:S(2)}, u32[]{:S(2)}) collective-permute-start(f32[256,256]{0,1:T(8,128)S(1)} %get-tuple-element.17), channel_id=1, source_target_pairs={{2,0},{3,1},{4,2},{5,3},{6,4},{7,5},{8,6},{9,7},{10,8},{11,9},{12,... | collective-permute-start | bytes 786440 | tf_op jit(solution)/shard_map/ppermute | solution.py:14
  99.7 1.3 collective-permute-start.9
  101.0 1.3 collective-permute-start.10
  102.3 1.3 collective-permute-start.11
  103.6 0.0 collective-permute-done.7
  103.7 1.3 collective-permute-start.13
  105.0 5.1 %collective-permute-done.8 = f32[256,256]{0,1:T(8,128)S(1)} collective-permute-done((f32[256,256]{0,1:T(8,128)S(1)}, f32[256,256]{0,1:T(8,128)S(1)}, u32[]{:S(2)}, u32[]{:S(2)}) %collective-permute-start.8) | collective-permute-done | bytes 262176 | tf_op jit(solution)/shard_map/ppermute | solution.py:14
  110.0 1.3 collective-permute-start.12
  111.3 0.8 convolution_convert_fusion.1
  112.1 0.8 copy.55
  112.9 0.8 collective-permute-done.9
  113.7 8.1 %collective-permute-done.10 = f32[256,256]{0,1:T(8,128)} collective-permute-done((f32[256,256]{0,1:T(8,128)}, f32[256,256]{0,1:T(8,128)}, u32[]{:S(2)}, u32[]{:S(2)}) %collective-permute-start.10) | collective-permute-done | bytes 262176 | tf_op jit(solution)/shard_map/ppermute | solution.py:14
  121.8 2.3 %collective-permute-done.11 = f32[256,256]{0,1:T(8,128)} collective-permute-done((f32[256,256]{0,1:T(8,128)}, f32[256,256]{0,1:T(8,128)}, u32[]{:S(2)}, u32[]{:S(2)}) %collective-permute-start.11) | collective-permute-done | bytes 262176 | tf_op jit(solution)/shard_map/ppermute | solution.py:14
  124.1 11.9 %collective-permute-done.13 = f32[256,256]{0,1:T(8,128)} collective-permute-done((f32[256,256]{0,1:T(8,128)}, f32[256,256]{0,1:T(8,128)}, u32[]{:S(2)}, u32[]{:S(2)}) %collective-permute-start.13) | collective-permute-done | bytes 262176 | tf_op jit(solution)/shard_map/ppermute | solution.py:14
  135.9 6.0 %collective-permute-done.12 = f32[256,256]{0,1:T(8,128)} collective-permute-done((f32[256,256]{0,1:T(8,128)}, f32[256,256]{0,1:T(8,128)}, u32[]{:S(2)}, u32[]{:S(2)}) %collective-permute-start.12) | collective-permute-done | bytes 262176 | tf_op jit(solution)/shard_map/ppermute | solution.py:14
  142.0 1.4 fusion.23
  143.4 0.7 copy.57
  144.1 0.7 copy.56
  144.8 0.0 reduce-scatter.2.cloned.1.call-done
  144.8 1.1 convert_element_type.29
  145.9 0.8 copy.54
  (13 shorter events, 0.1 us)
Async XLA Ops:
  7.2 68.4 %all-gather.2.cloned.1.call-start = ((), (), s32[]{:S(2)}) async-start(), calls=%async_computation.2 | async-start | bytes 2359296 | tf_op jit(solution)/shard_map/all_gather | solution.py:68
  8.9 37.0 %collective-permute-start.6 = (bf16[256,256]{1,0:T(8,128)(2,1)S(1)}, bf16[256,256]{1,0:T(8,128)(2,1)S(1)}, u32[]{:S(2)}, u32[]{:S(2)}) collective-permute-start(bf16[256,256]{1,0:T(8,128)(2,1)S(1)} %constant_dynamic-update-slice_fusion), channel_id=1, source_target_pairs={{0,7},{1,8},{2,9},{3,10},{4,11},{5,12},{6,13},{7,14},{8,15},{9,16}... | collective-permute-start | bytes 393224 | tf_op jit(solution)/shard_map/ppermute | solution.py:14
  12.6 33.3 %collective-permute-start.5 = (bf16[256,256]{1,0:T(8,128)(2,1)S(1)}, bf16[256,256]{1,0:T(8,128)(2,1)S(1)}, u32[]{:S(2)}, u32[]{:S(2)}) collective-permute-start(bf16[256,256]{1,0:T(8,128)(2,1)S(1)} %constant_dynamic-update-slice_fusion), channel_id=1, source_target_pairs={{0,6},{1,7},{2,8},{3,9},{4,10},{5,11},{6,12},{7,13},{8,14},{9,15},... | collective-permute-start | bytes 393224 | tf_op jit(solution)/shard_map/ppermute | solution.py:14
  17.3 28.6 %collective-permute-start.4 = (bf16[256,256]{1,0:T(8,128)(2,1)S(1)}, bf16[256,256]{1,0:T(8,128)(2,1)S(1)}, u32[]{:S(2)}, u32[]{:S(2)}) collective-permute-start(bf16[256,256]{1,0:T(8,128)(2,1)S(1)} %constant_dynamic-update-slice_fusion), channel_id=1, source_target_pairs={{0,5},{1,6},{2,7},{3,8},{4,9},{5,10},{6,11},{7,12},{8,13},{9,14},{... | collective-permute-start | bytes 393224 | tf_op jit(solution)/shard_map/ppermute | solution.py:14
  21.3 24.6 %collective-permute-start.3 = (bf16[256,256]{1,0:T(8,128)(2,1)S(1)}, bf16[256,256]{1,0:T(8,128)(2,1)S(1)}, u32[]{:S(2)}, u32[]{:S(2)}) collective-permute-start(bf16[256,256]{1,0:T(8,128)(2,1)S(1)} %constant_dynamic-update-slice_fusion), channel_id=1, source_target_pairs={{0,4},{1,5},{2,6},{3,7},{4,8},{5,9},{6,10},{7,11},{8,12},{9,13},{1... | collective-permute-start | bytes 393224 | tf_op jit(solution)/shard_map/ppermute | solution.py:14
  26.1 6.3 %collective-permute-start = (bf16[256,256]{1,0:T(8,128)(2,1)S(1)}, bf16[256,256]{1,0:T(8,128)(2,1)S(1)}, u32[]{:S(2)}, u32[]{:S(2)}) collective-permute-start(bf16[256,256]{1,0:T(8,128)(2,1)S(1)} %constant_dynamic-update-slice_fusion), channel_id=1, source_target_pairs={{0,1},{1,2},{2,3},{3,4},{4,5},{5,6},{6,7},{7,8},{8,9},{9,10},{10,1... | collective-permute-start | bytes 393224 | tf_op jit(solution)/shard_map/ppermute | solution.py:14
  28.0 116.8 %reduce-scatter.2.cloned.1.call-start = ((), (), s32[]{:S(2)}) async-start(), calls=%async_computation.1 | async-start | bytes 4718592 | tf_op jit(solution)/shard_map/reduce_scatter | solution.py:57
  32.4 8.1 %collective-permute-start.1 = (bf16[256,256]{1,0:T(8,128)(2,1)S(1)}, bf16[256,256]{1,0:T(8,128)(2,1)S(1)}, u32[]{:S(2)}, u32[]{:S(2)}) collective-permute-start(bf16[256,256]{1,0:T(8,128)(2,1)S(1)} %constant_dynamic-update-slice_fusion), channel_id=1, source_target_pairs={{0,2},{1,3},{2,4},{3,5},{4,6},{5,7},{6,8},{7,9},{8,10},{9,11},{10,... | collective-permute-start | bytes 393224 | tf_op jit(solution)/shard_map/ppermute | solution.py:14
  40.4 5.4 %collective-permute-start.2 = (bf16[256,256]{1,0:T(8,128)(2,1)S(1)}, bf16[256,256]{1,0:T(8,128)(2,1)S(1)}, u32[]{:S(2)}, u32[]{:S(2)}) collective-permute-start(bf16[256,256]{1,0:T(8,128)(2,1)S(1)} %constant_dynamic-update-slice_fusion), channel_id=1, source_target_pairs={{0,3},{1,4},{2,5},{3,6},{4,7},{5,8},{6,9},{7,10},{8,11},{9,12},{10... | collective-permute-start | bytes 393224 | tf_op jit(solution)/shard_map/ppermute | solution.py:14
  75.6 4.3 %copy-start = (bf16[4,256,2048]{1,2,0:T(8,128)(2,1)S(1)}, bf16[4,256,2048]{1,2,0:T(8,128)(2,1)}, u32[]{:S(2)}) copy-start(bf16[4,256,2048]{1,2,0:T(8,128)(2,1)} %fusion.5) | copy-start | bytes 12582916
  79.8 2.2 %copy-start.1 = (bf16[512,4096]{1,0:T(8,128)(2,1)S(1)}, bf16[512,4096]{1,0:T(8,128)(2,1)}, u32[]{:S(2)}) copy-start(bf16[512,4096]{1,0:T(8,128)(2,1)} %param.9) | copy-start | bytes 12582916
  95.9 7.7 %collective-permute-start.7 = (f32[256,256]{0,1:T(8,128)S(1)}, f32[256,256]{0,1:T(8,128)S(1)}, u32[]{:S(2)}, u32[]{:S(2)}) collective-permute-start(f32[256,256]{0,1:T(8,128)S(1)} %get-tuple-element.16), channel_id=1, source_target_pairs={{1,0},{2,1},{3,2},{4,3},{5,4},{6,5},{7,6},{8,7},{9,8},{10,9},{11,1... | collective-permute-start | bytes 786440 | tf_op jit(solution)/shard_map/ppermute | solution.py:14
  97.8 12.2 %collective-permute-start.8 = (f32[256,256]{0,1:T(8,128)S(1)}, f32[256,256]{0,1:T(8,128)S(1)}, u32[]{:S(2)}, u32[]{:S(2)}) collective-permute-start(f32[256,256]{0,1:T(8,128)S(1)} %get-tuple-element.17), channel_id=1, source_target_pairs={{2,0},{3,1},{4,2},{5,3},{6,4},{7,5},{8,6},{9,7},{10,8},{11,9},{12,... | collective-permute-start | bytes 786440 | tf_op jit(solution)/shard_map/ppermute | solution.py:14
  99.7 14.0 %collective-permute-start.9 = (f32[256,256]{0,1:T(8,128)}, f32[256,256]{0,1:T(8,128)}, u32[]{:S(2)}, u32[]{:S(2)}) collective-permute-start(f32[256,256]{0,1:T(8,128)} %get-tuple-element.18), channel_id=1, source_target_pairs={{3,0},{4,1},{5,2},{6,3},{7,4},{8,5},{9,6},{10,7},{11,8},{12,9},{13... | collective-permute-start | bytes 786440 | tf_op jit(solution)/shard_map/ppermute | solution.py:14
  101.0 20.8 %collective-permute-start.10 = (f32[256,256]{0,1:T(8,128)}, f32[256,256]{0,1:T(8,128)}, u32[]{:S(2)}, u32[]{:S(2)}) collective-permute-start(f32[256,256]{0,1:T(8,128)} %get-tuple-element.19), channel_id=1, source_target_pairs={{4,0},{5,1},{6,2},{7,3},{8,4},{9,5},{10,6},{11,7},{12,8},{13,9},{1... | collective-permute-start | bytes 786440 | tf_op jit(solution)/shard_map/ppermute | solution.py:14
  102.3 21.7 %collective-permute-start.11 = (f32[256,256]{0,1:T(8,128)}, f32[256,256]{0,1:T(8,128)}, u32[]{:S(2)}, u32[]{:S(2)}) collective-permute-start(f32[256,256]{0,1:T(8,128)} %get-tuple-element.20), channel_id=1, source_target_pairs={{5,0},{6,1},{7,2},{8,3},{9,4},{10,5},{11,6},{12,7},{13,8},{14,9},{... | collective-permute-start | bytes 786440 | tf_op jit(solution)/shard_map/ppermute | solution.py:14
  103.7 32.3 %collective-permute-start.13 = (f32[256,256]{0,1:T(8,128)}, f32[256,256]{0,1:T(8,128)}, u32[]{:S(2)}, u32[]{:S(2)}) collective-permute-start(f32[256,256]{0,1:T(8,128)} %get-tuple-element.21), channel_id=1, source_target_pairs={{7,0},{8,1},{9,2},{10,3},{11,4},{12,5},{13,6},{14,7},{15,8},{16,9}... | collective-permute-start | bytes 786440 | tf_op jit(solution)/shard_map/ppermute | solution.py:14
  110.0 32.0 %collective-permute-start.12 = (f32[256,256]{0,1:T(8,128)}, f32[256,256]{0,1:T(8,128)}, u32[]{:S(2)}, u32[]{:S(2)}) collective-permute-start(f32[256,256]{0,1:T(8,128)} %get-tuple-element.22), channel_id=1, source_target_pairs={{6,0},{7,1},{8,2},{9,3},{10,4},{11,5},{12,6},{13,7},{14,8},{15,9},... | collective-permute-start | bytes 786440 | tf_op jit(solution)/shard_map/ppermute | solution.py:14
Sparse Core Ops, SparseCore 0:
  28.2 47.3 all-gather.1
  85.5 55.6 reduce-scatter.1
where the time goes:
time: 154 us
  waiting for transfers between devices  60.6 us (39%)
  starting transfers between devices  35.7 us (23%)
  matrix products  23.4 us (15%)
  between operations  14.4 us (9%)
  other arithmetic  11.1 us (7%)
  local copies, waits for them, and re-layouts  8.43 us (5%)
    ppermute x14, waiting for transfers between devices, passed_along(): lax.ppermute(value, axis, [(source, source + steps) for source in range(f...  42.1 us
    ppermute x14, starting transfers between devices, passed_along(): lax.ppermute(value, axis, [(source, source + steps) for source in range(f...  35.6 us
    all_gather x1, waiting for transfers between devices, per_device(): lax.all_gather(out_grad, 'heads', axis=0, tiled=True)  18.4 us
    convert_element_type x1, other arithmetic, per_device(): probs = weights.astype(jnp.bfloat16)  6.04 us
    unnamed x17, local copies, waits for them, and re-layouts  5.47 us
    sub x1, matrix products, per_device(): expons = jnp.exp(scores - largest)  4.84 us
    dot_general x1, matrix products, per_device(): jnp.einsum('gdt,kd->gtk', grad_heads, flat_values, preferred_element_type...  4.34 us
    dot_general x1, matrix products, per_device(): jnp.dot(columns, lax.all_gather(out_grad, 'heads', axis=0, tiled=True), p...  4.25 us
  transfers between devices with their start and end apart: 16, of which 10 were waited for; matrix products, arithmetic and copies ran while one was open for 19% of the time, Pallas kernels for 0%

commit v1 on v0

--- a/solution.py
+++ b/solution.py
@@ -53,19 +53,17 @@
         "gtk,kd->tgd", probs, flat_values, preferred_element_type=jnp.float32
     ).astype(jnp.bfloat16)
     attn = attn_heads.reshape(tok_rows, group_size * head_dim)
-    columns = out_weight
+    out_partial = lax.dot_general(
+        out_weight, attn, (((0,), (1,)), ((), ())), preferred_element_type=jnp.float32
+    ).astype(jnp.bfloat16)
+    gathered = lax.all_gather(out_grad, "heads", axis=0, tiled=True)
     out_t = lax.psum_scatter(
-        lax.dot_general(
-            columns, attn, (((0,), (1,)), ((), ())), preferred_element_type=jnp.float32
-        ),
-        "heads",
-        scatter_dimension=0,
-        tiled=True,
-    ).astype(jnp.bfloat16)
-    columns = out_weight
+        out_partial, "heads", scatter_dimension=0, tiled=True
+    )
+    _, gathered = lax.optimization_barrier((out_partial, gathered))
     grad_attn = jnp.dot(
-        columns,
-        lax.all_gather(out_grad, "heads", axis=0, tiled=True),
+        out_weight,
+        gathered,
         preferred_element_type=jnp.float32,
     ).astype(jnp.bfloat16)
     grad_heads = grad_attn.reshape(group_size, head_dim, tok_rows)
@@ -88,7 +86,8 @@
     )
     summed = partial_grads[0]
     for offset in range(1, num_blocks):
-        summed = summed + passed_along(partial_grads[offset], "ctx", -offset)
+        sent = passed_along(partial_grads[offset].astype(jnp.bfloat16), "ctx", -offset)
+        summed = summed + sent.astype(jnp.float32)
     grad_k = summed[:, :head_dim].astype(jnp.bfloat16)
     grad_v = summed[:, head_dim:].astype(jnp.bfloat16)
     return (out_t, grad_q, grad_k, grad_v)

time: 154 us -> 130 us (0.84)
  the two profiles are of different devices: /device:TPU:10 before, /device:TPU:6 now
where the time goes in v1:
time: 130 us; the launch traced here: 129 us
  starting transfers between devices  44.3 us (34%)
  waiting for transfers between devices  28.1 us (22%)
  matrix products  22.6 us (17%)
  between operations  14.5 us (11%)
  local copies, waits for them, and re-layouts  12.2 us (9%)
  other arithmetic  7.6 us (6%)
    ppermute x14, starting transfers between devices, passed_along(): lax.ppermute(value, axis, [(source, source + steps) for source in range(f...  44.2 us
    all_gather x1, waiting for transfers between devices, per_device(): gathered = lax.all_gather(out_grad, 'heads', axis=0, tiled=True)  14.3 us
    ppermute x14, waiting for transfers between devices, passed_along(): lax.ppermute(value, axis, [(source, source + steps) for source in range(f...  10 us
    unnamed x22, local copies, waits for them, and re-layouts  8.87 us
    sub x1, matrix products, per_device(): expons = jnp.exp(scores - largest)  4.84 us
    dot_general x1, matrix products, per_device(): jnp.einsum('gdt,kd->gtk', grad_heads, flat_values, preferred_element_type...  4.35 us
    convert_element_type x1, other arithmetic, per_device(): probs = weights.astype(jnp.bfloat16)  4.17 us
    dot_general x1, matrix products, per_device(): jnp.dot(out_weight, gathered, preferred_element_type=jnp.float32)  4.12 us
  transfers between devices with their start and end apart: 16, of which 6 were waited for; matrix products, arithmetic and copies ran while one was open for 27% of the time, Pallas kernels for 0%

profile of v1, /device:TPU:6, one launch (start us, length us, event | category | flops | bytes accessed | tf_op | source)
XLA Modules:
  0.0 129.3 jit_solution(3871092937512918961)
XLA Ops:
  7.2 0.0 all-gather.2.cloned.1.call-start
  7.2 0.9 constant_dynamic-update-slice_fusion.1
  8.1 0.9 constant_dynamic-update-slice_fusion
  8.9 1.9 %collective-permute-start = (bf16[256,256]{1,0:T(8,128)(2,1)S(1)}, bf16[256,256]{1,0:T(8,128)(2,1)S(1)}, u32[]{:S(2)}, u32[]{:S(2)}) collective-permute-start(bf16[256,256]{1,0:T(8,128)(2,1)S(1)} %constant_dynamic-update-slice_fusion), channel_id=1, source_target_pairs={{0,1},{1,2},{2,3},{3,4},{4,5},{5,6},{6,7},{7,8},{8,9},{9,10},{10,1... | collective-permute-start | bytes 393224 | tf_op jit(solution)/shard_map/ppermute | solution.py:14
  10.9 4.2 %collective-permute-start.1 = (bf16[256,256]{1,0:T(8,128)(2,1)S(1)}, bf16[256,256]{1,0:T(8,128)(2,1)S(1)}, u32[]{:S(2)}, u32[]{:S(2)}) collective-permute-start(bf16[256,256]{1,0:T(8,128)(2,1)S(1)} %constant_dynamic-update-slice_fusion), channel_id=1, source_target_pairs={{0,2},{1,3},{2,4},{3,5},{4,6},{5,7},{6,8},{7,9},{8,10},{9,11},{10,... | collective-permute-start | bytes 393224 | tf_op jit(solution)/shard_map/ppermute | solution.py:14
  15.1 4.3 %collective-permute-start.2 = (bf16[256,256]{1,0:T(8,128)(2,1)S(1)}, bf16[256,256]{1,0:T(8,128)(2,1)S(1)}, u32[]{:S(2)}, u32[]{:S(2)}) collective-permute-start(bf16[256,256]{1,0:T(8,128)(2,1)S(1)} %constant_dynamic-update-slice_fusion), channel_id=1, source_target_pairs={{0,3},{1,4},{2,5},{3,6},{4,7},{5,8},{6,9},{7,10},{8,11},{9,12},{10... | collective-permute-start | bytes 393224 | tf_op jit(solution)/shard_map/ppermute | solution.py:14
  19.4 4.8 %collective-permute-start.3 = (bf16[256,256]{1,0:T(8,128)(2,1)S(1)}, bf16[256,256]{1,0:T(8,128)(2,1)S(1)}, u32[]{:S(2)}, u32[]{:S(2)}) collective-permute-start(bf16[256,256]{1,0:T(8,128)(2,1)S(1)} %constant_dynamic-update-slice_fusion), channel_id=1, source_target_pairs={{0,4},{1,5},{2,6},{3,7},{4,8},{5,9},{6,10},{7,11},{8,12},{9,13},{1... | collective-permute-start | bytes 393224 | tf_op jit(solution)/shard_map/ppermute | solution.py:14
  24.2 3.8 %collective-permute-start.4 = (bf16[256,256]{1,0:T(8,128)(2,1)S(1)}, bf16[256,256]{1,0:T(8,128)(2,1)S(1)}, u32[]{:S(2)}, u32[]{:S(2)}) collective-permute-start(bf16[256,256]{1,0:T(8,128)(2,1)S(1)} %constant_dynamic-update-slice_fusion), channel_id=1, source_target_pairs={{0,5},{1,6},{2,7},{3,8},{4,9},{5,10},{6,11},{7,12},{8,13},{9,14},{... | collective-permute-start | bytes 393224 | tf_op jit(solution)/shard_map/ppermute | solution.py:14
  28.0 0.0 all-gather.2.cloned.1.call-update
  28.0 0.0 reduce-scatter.2.cloned.1.call-start
  28.1 0.7 copy.45
  28.9 0.1 reduce.1
  29.0 0.7 sub.31
  29.7 0.1 add_bitcast_fusion
  29.7 1.1 copy.77
  30.8 0.1 select_reduce_fusion
  30.9 0.6 compare_and_fusion
  31.5 3.6 %collective-permute-start.5 = (bf16[256,256]{1,0:T(8,128)(2,1)S(1)}, bf16[256,256]{1,0:T(8,128)(2,1)S(1)}, u32[]{:S(2)}, u32[]{:S(2)}) collective-permute-start(bf16[256,256]{1,0:T(8,128)(2,1)S(1)} %constant_dynamic-update-slice_fusion), channel_id=1, source_target_pairs={{0,6},{1,7},{2,8},{3,9},{4,10},{5,11},{6,12},{7,13},{8,14},{9,15},... | collective-permute-start | bytes 393224 | tf_op jit(solution)/shard_map/ppermute | solution.py:14
  35.2 0.0 collective-permute-done.1
  35.2 6.1 %collective-permute-start.6 = (bf16[256,256]{1,0:T(8,128)(2,1)S(1)}, bf16[256,256]{1,0:T(8,128)(2,1)S(1)}, u32[]{:S(2)}, u32[]{:S(2)}) collective-permute-start(bf16[256,256]{1,0:T(8,128)(2,1)S(1)} %constant_dynamic-update-slice_fusion), channel_id=1, source_target_pairs={{0,7},{1,8},{2,9},{3,10},{4,11},{5,12},{6,13},{7,14},{8,15},{9,16}... | collective-permute-start | bytes 393224 | tf_op jit(solution)/shard_map/ppermute | solution.py:14
  41.3 0.0 collective-permute-done.2
  41.4 0.0 collective-permute-done.3
  41.4 0.0 collective-permute-done.5
  41.5 2.6 %collective-permute-done.6 = bf16[256,256]{1,0:T(8,128)(2,1)S(1)} collective-permute-done((bf16[256,256]{1,0:T(8,128)(2,1)S(1)}, bf16[256,256]{1,0:T(8,128)(2,1)S(1)}, u32[]{:S(2)}, u32[]{:S(2)}) %collective-permute-start.6) | collective-permute-done | bytes 131104 | tf_op jit(solution)/shard_map/ppermute | solution.py:14
  44.0 0.3 fusion.23
  44.3 4.8 %fusion.25 = (f32[4,256]{1,0:T(4,128)S(1)}, f32[4,256,2048]{1,2,0:T(8,128)}) fusion(pred[256,2048]{0,1:T(8,128)(4,1)S(1)} %compare_and_fusion, bf16[2048,128,1]{1,0,2:T(8,128)(2,1)S(1)} %bitcast.81, bf16[256,4,128]{0,2,1:T(8,128)(2,1)S(1)} %bitcast.85), kind=kOutput, calls=%fused_computation.54 | convolution fusion | flops 545261568 | bytes 9703424 | tf_op jit(solution)/shard_map/sub | solution.py:49
  49.1 4.2 %fusion.6 = bf16[4,256,2048]{1,2,0:T(8,128)(2,1)S(1)} fusion(f32[4,256,2048]{1,2,0:T(8,128)} %get-tuple-element.30, f32[4,256]{1,0:T(4,128)S(1)} %get-tuple-element.29), kind=kLoop, calls=%fused_computation.11 | loop fusion | flops 4194304 | bytes 12587008 | tf_op jit(solution)/shard_map/convert_element_type | solution.py:51
  53.3 0.0 copy-start.1
  53.3 2.1 %copy-done = bf16[4,256,2048]{1,2,0:T(8,128)(2,1)} copy-done((bf16[4,256,2048]{1,2,0:T(8,128)(2,1)}, bf16[4,256,2048]{1,2,0:T(8,128)(2,1)S(1)}, u32[]{:S(2)}) %copy-start) | copy-done | bytes 4194328
  55.5 0.8 bitcast_convert_fusion
  56.2 0.8 copy-done.1
  57.0 2.6 %fusion.2 = bf16[4096,256]{0,1:T(8,128)(2,1)} fusion(bf16[256,512]{0,1:T(8,128)(2,1)S(1)} %bitcast.88, bf16[512,4096]{1,0:T(8,128)(2,1)S(1)} %copy-done.1), kind=kOutput, calls=%fused_computation.6 | convolution fusion | flops 1074790400 | bytes 6553600 | tf_op jit(solution)/shard_map/dot_general | solution.py:56
  59.7 0.0 reduce-scatter.2.cloned.1.call-update
  59.7 0.2 copy.69
  59.9 14.3 %all-gather.2.cloned.1.call-done = bf16[4096,256]{1,0:T(8,128)(2,1)} async-done(((bf16[512,256]{1,0:T(8,128)(2,1)}), bf16[4096,256]{1,0:T(8,128)(2,1)}) %all-gather.2.cloned.1.call-update) | async-done | bytes 2097168 | tf_op jit(solution)/shard_map/all_gather | solution.py:59
  74.3 4.1 %fusion.8 = bf16[512,256]{0,1:T(8,128)(2,1)S(1)} fusion(bf16[4096,256]{1,0:T(8,128)(2,1)} %all-gather.2.cloned.1.call-done, bf16[512,4096]{1,0:T(8,128)(2,1)} %param.9), kind=kOutput, calls=%fused_computation.22 | convolution fusion | flops 1073872896 | bytes 6553600 | tf_op jit(solution)/shard_map/dot_general | solution.py:64
  78.4 0.1 reshape.157
  78.5 0.2 copy.56
  78.6 0.4 multiply_reduce_fusion
  79.0 0.1 copy.70
  79.1 3.7 %convolution_bitcast_fusion = f32[2048,128]{0,1:T(8,128)S(1)} fusion(bf16[4,256,2048]{1,2,0:T(8,128)(2,1)} %copy-done, bf16[4,128,256]{2,1,0:T(8,128)(2,1)S(1)} %copy.56), kind=kOutput, calls=%fused_computation.15 | convolution fusion | flops 536870912 | bytes 5505024 | tf_op jit(solution)/shard_map/gtk,gdt->kd/dot_general | solution.py:83
  82.7 4.3 %multiply_convert_fusion = bf16[4,256,2048]{1,2,0:T(8,128)(2,1)S(1)} fusion(bf16[2048,128,1]{1,0,2:T(8,128)(2,1)S(1)} %bitcast.84, bf16[4,128,256]{2,1,0:T(8,128)(2,1)S(1)} %copy.56, f32[4,256]{1,0:T(4,128)S(1)} %copy.70, f32[4,256,2048]{1,2,0:T(8,128)} %get-tuple-element.30, f32[4,256]{1,0:T(4,128)S(1)} %get-tuple-element.29), kind=kOutput, calls=%fused_computation.2 | convolution fusion | flops 547356672 | bytes 13377536 | tf_op jit(solution)/shard_map/gdt,kd->gtk/dot_general | solution.py:73
  87.1 1.5 %convolution_bitcast_fusion.1 = f32[2048,128]{0,1:T(8,128)S(1)} fusion(bf16[4,256,2048]{1,2,0:T(8,128)(2,1)S(1)} %multiply_convert_fusion, bf16[256,4,128]{0,2,1:T(8,128)(2,1)S(1)} %bitcast.86), kind=kOutput, calls=%fused_computation.16 | convolution fusion | flops 536870912 | bytes 5505024 | tf_op jit(solution)/shard_map/gtk,tgd->kd/dot_general | solution.py:82
  88.6 0.1 fusion.7
  88.7 0.1 fusion.22
  88.8 3.3 %collective-permute-start.10 = (bf16[256,256]{0,1:T(8,128)(2,1)S(1)}, bf16[256,256]{0,1:T(8,128)(2,1)S(1)}, u32[]{:S(2)}, u32[]{:S(2)}) collective-permute-start(bf16[256,256]{0,1:T(8,128)(2,1)S(1)} %get-tuple-element.22), channel_id=1, source_target_pairs={{4,0},{5,1},{6,2},{7,3},{8,4},{9,5},{10,6},{11,7},{12,8},{13,9},{1... | collective-permute-start | bytes 393224 | tf_op jit(solution)/shard_map/ppermute | solution.py:14
  92.1 1.9 %collective-permute-start.11 = (bf16[256,256]{0,1:T(8,128)(2,1)S(1)}, bf16[256,256]{0,1:T(8,128)(2,1)S(1)}, u32[]{:S(2)}, u32[]{:S(2)}) collective-permute-start(bf16[256,256]{0,1:T(8,128)(2,1)S(1)} %get-tuple-element.21), channel_id=1, source_target_pairs={{5,0},{6,1},{7,2},{8,3},{9,4},{10,5},{11,6},{12,7},{13,8},{14,9},{... | collective-permute-start | bytes 393224 | tf_op jit(solution)/shard_map/ppermute | solution.py:14
  94.1 1.9 %collective-permute-start.12 = (bf16[256,256]{0,1:T(8,128)(2,1)S(1)}, bf16[256,256]{0,1:T(8,128)(2,1)}, u32[]{:S(2)}, u32[]{:S(2)}) collective-permute-start(bf16[256,256]{0,1:T(8,128)(2,1)S(1)} %get-tuple-element.20), channel_id=1, source_target_pairs={{6,0},{7,1},{8,2},{9,3},{10,4},{11,5},{12,6},{13,7},{14,8},{15,9},... | collective-permute-start | bytes 393224 | tf_op jit(solution)/shard_map/ppermute | solution.py:14
  96.0 1.3 collective-permute-start.13
  97.3 1.9 %collective-permute-start.7 = (bf16[256,256]{0,1:T(8,128)(2,1)S(1)}, bf16[256,256]{0,1:T(8,128)(2,1)}, u32[]{:S(2)}, u32[]{:S(2)}) collective-permute-start(bf16[256,256]{0,1:T(8,128)(2,1)S(1)} %get-tuple-element.18), channel_id=1, source_target_pairs={{1,0},{2,1},{3,2},{4,3},{5,4},{6,5},{7,6},{8,7},{9,8},{10,9},{11,1... | collective-permute-start | bytes 393224 | tf_op jit(solution)/shard_map/ppermute | solution.py:14
  99.2 0.0 collective-permute-done.10
  99.2 2.5 %collective-permute-start.8 = (bf16[256,256]{0,1:T(8,128)(2,1)S(1)}, bf16[256,256]{0,1:T(8,128)(2,1)}, u32[]{:S(2)}, u32[]{:S(2)}) collective-permute-start(bf16[256,256]{0,1:T(8,128)(2,1)S(1)} %get-tuple-element.24), channel_id=1, source_target_pairs={{2,0},{3,1},{4,2},{5,3},{6,4},{7,5},{8,6},{9,7},{10,8},{11,9},{12,... | collective-permute-start | bytes 393224 | tf_op jit(solution)/shard_map/ppermute | solution.py:14
  101.7 0.5 collective-permute-done.11
  102.2 0.7 copy-done.3
  102.9 2.6 %collective-permute-start.9 = (bf16[256,256]{0,1:T(8,128)(2,1)S(1)}, bf16[256,256]{0,1:T(8,128)(2,1)}, u32[]{:S(2)}, u32[]{:S(2)}) collective-permute-start(bf16[256,256]{0,1:T(8,128)(2,1)S(1)} %get-tuple-element.23), channel_id=1, source_target_pairs={{3,0},{4,1},{5,2},{6,3},{7,4},{8,5},{9,6},{10,7},{11,8},{12,9},{13... | collective-permute-start | bytes 393224 | tf_op jit(solution)/shard_map/ppermute | solution.py:14
  105.4 0.8 convolution_convert_fusion.2
  106.2 0.8 copy.58
  107.0 6.8 %collective-permute-done.8 = bf16[256,256]{0,1:T(8,128)(2,1)} collective-permute-done((bf16[256,256]{0,1:T(8,128)(2,1)S(1)}, bf16[256,256]{0,1:T(8,128)(2,1)}, u32[]{:S(2)}, u32[]{:S(2)}) %collective-permute-start.8) | collective-permute-done | bytes 131104 | tf_op jit(solution)/shard_map/ppermute | solution.py:14
  113.8 0.2 collective-permute-done.9
  114.0 1.4 %fusion.19 = bf16[256,256]{0,1:T(8,128)(2,1)S(1)} fusion(bf16[256,256]{0,1:T(8,128)(2,1)} %collective-permute-done.13, bf16[256,256]{0,1:T(8,128)(2,1)} %collective-permute-done.12, bf16[256,256]{0,1:T(8,128)(2,1)} %copy-done.3, bf16[256,256]{0,1:T(8,128)(2,1)} %copy-done.2, bf16[256,256]{0,1:T(8,128)(2,1)} %collective-permute-done.9, ...), kind=kLoop, calls=%fused_computation.34 | loop fusion | flops 1048576 | bytes 3145728 | tf_op jit(solution)/shard_map/convert.1
  115.4 0.7 copy.59
  116.2 0.7 copy.60
  116.9 3.7 %reduce-scatter.2.cloned.1.call-done = bf16[512,256]{0,1:T(8,128)(2,1)} async-done(((bf16[4096,256]{0,1:T(8,128)(2,1)}), bf16[512,256]{0,1:T(8,128)(2,1)}) %reduce-scatter.2.cloned.1.call-update) | async-done | bytes 262160 | tf_op jit(solution)/shard_map/reduce_scatter | solution.py:60
  120.6 1.8 %copy.57 = bf16[512,256]{1,0:T(8,128)(2,1)} copy(bf16[512,256]{0,1:T(8,128)(2,1)} %reduce-scatter.2.cloned.1.call-done) | data formatting | bytes 524288
  (22 shorter events, 0.2 us)
Async XLA Ops:
  7.2 67.1 %all-gather.2.cloned.1.call-start = ((), (), s32[]{:S(2)}) async-start(), calls=%async_computation.2 | async-start | bytes 2359296 | tf_op jit(solution)/shard_map/all_gather | solution.py:59
  8.9 22.6 %collective-permute-start = (bf16[256,256]{1,0:T(8,128)(2,1)S(1)}, bf16[256,256]{1,0:T(8,128)(2,1)S(1)}, u32[]{:S(2)}, u32[]{:S(2)}) collective-permute-start(bf16[256,256]{1,0:T(8,128)(2,1)S(1)} %constant_dynamic-update-slice_fusion), channel_id=1, source_target_pairs={{0,1},{1,2},{2,3},{3,4},{4,5},{5,6},{6,7},{7,8},{8,9},{9,10},{10,1... | collective-permute-start | bytes 393224 | tf_op jit(solution)/shard_map/ppermute | solution.py:14
  10.9 24.4 %collective-permute-start.1 = (bf16[256,256]{1,0:T(8,128)(2,1)S(1)}, bf16[256,256]{1,0:T(8,128)(2,1)S(1)}, u32[]{:S(2)}, u32[]{:S(2)}) collective-permute-start(bf16[256,256]{1,0:T(8,128)(2,1)S(1)} %constant_dynamic-update-slice_fusion), channel_id=1, source_target_pairs={{0,2},{1,3},{2,4},{3,5},{4,6},{5,7},{6,8},{7,9},{8,10},{9,11},{10,... | collective-permute-start | bytes 393224 | tf_op jit(solution)/shard_map/ppermute | solution.py:14
  15.1 26.3 %collective-permute-start.2 = (bf16[256,256]{1,0:T(8,128)(2,1)S(1)}, bf16[256,256]{1,0:T(8,128)(2,1)S(1)}, u32[]{:S(2)}, u32[]{:S(2)}) collective-permute-start(bf16[256,256]{1,0:T(8,128)(2,1)S(1)} %constant_dynamic-update-slice_fusion), channel_id=1, source_target_pairs={{0,3},{1,4},{2,5},{3,6},{4,7},{5,8},{6,9},{7,10},{8,11},{9,12},{10... | collective-permute-start | bytes 393224 | tf_op jit(solution)/shard_map/ppermute | solution.py:14
  19.4 22.0 %collective-permute-start.3 = (bf16[256,256]{1,0:T(8,128)(2,1)S(1)}, bf16[256,256]{1,0:T(8,128)(2,1)S(1)}, u32[]{:S(2)}, u32[]{:S(2)}) collective-permute-start(bf16[256,256]{1,0:T(8,128)(2,1)S(1)} %constant_dynamic-update-slice_fusion), channel_id=1, source_target_pairs={{0,4},{1,5},{2,6},{3,7},{4,8},{5,9},{6,10},{7,11},{8,12},{9,13},{1... | collective-permute-start | bytes 393224 | tf_op jit(solution)/shard_map/ppermute | solution.py:14
  24.2 17.2 %collective-permute-start.4 = (bf16[256,256]{1,0:T(8,128)(2,1)S(1)}, bf16[256,256]{1,0:T(8,128)(2,1)S(1)}, u32[]{:S(2)}, u32[]{:S(2)}) collective-permute-start(bf16[256,256]{1,0:T(8,128)(2,1)S(1)} %constant_dynamic-update-slice_fusion), channel_id=1, source_target_pairs={{0,5},{1,6},{2,7},{3,8},{4,9},{5,10},{6,11},{7,12},{8,13},{9,14},{... | collective-permute-start | bytes 393224 | tf_op jit(solution)/shard_map/ppermute | solution.py:14
  28.0 92.6 %reduce-scatter.2.cloned.1.call-start = ((), (), s32[]{:S(2)}) async-start(), calls=%async_computation.1 | async-start | bytes 2359296 | tf_op jit(solution)/shard_map/reduce_scatter | solution.py:60
  31.5 9.9 %collective-permute-start.5 = (bf16[256,256]{1,0:T(8,128)(2,1)S(1)}, bf16[256,256]{1,0:T(8,128)(2,1)S(1)}, u32[]{:S(2)}, u32[]{:S(2)}) collective-permute-start(bf16[256,256]{1,0:T(8,128)(2,1)S(1)} %constant_dynamic-update-slice_fusion), channel_id=1, source_target_pairs={{0,6},{1,7},{2,8},{3,9},{4,10},{5,11},{6,12},{7,13},{8,14},{9,15},... | collective-permute-start | bytes 393224 | tf_op jit(solution)/shard_map/ppermute | solution.py:14
  35.2 8.8 %collective-permute-start.6 = (bf16[256,256]{1,0:T(8,128)(2,1)S(1)}, bf16[256,256]{1,0:T(8,128)(2,1)S(1)}, u32[]{:S(2)}, u32[]{:S(2)}) collective-permute-start(bf16[256,256]{1,0:T(8,128)(2,1)S(1)} %constant_dynamic-update-slice_fusion), channel_id=1, source_target_pairs={{0,7},{1,8},{2,9},{3,10},{4,11},{5,12},{6,13},{7,14},{8,15},{9,16}... | collective-permute-start | bytes 393224 | tf_op jit(solution)/shard_map/ppermute | solution.py:14
  53.3 2.1 %copy-start = (bf16[4,256,2048]{1,2,0:T(8,128)(2,1)}, bf16[4,256,2048]{1,2,0:T(8,128)(2,1)S(1)}, u32[]{:S(2)}) copy-start(bf16[4,256,2048]{1,2,0:T(8,128)(2,1)S(1)} %fusion.6) | copy-start | bytes 12582916
  53.3 3.7 %copy-start.1 = (bf16[512,4096]{1,0:T(8,128)(2,1)S(1)}, bf16[512,4096]{1,0:T(8,128)(2,1)}, u32[]{:S(2)}) copy-start(bf16[512,4096]{1,0:T(8,128)(2,1)} %param.9) | copy-start | bytes 12582916
  88.8 10.4 %collective-permute-start.10 = (bf16[256,256]{0,1:T(8,128)(2,1)S(1)}, bf16[256,256]{0,1:T(8,128)(2,1)S(1)}, u32[]{:S(2)}, u32[]{:S(2)}) collective-permute-start(bf16[256,256]{0,1:T(8,128)(2,1)S(1)} %get-tuple-element.22), channel_id=1, source_target_pairs={{4,0},{5,1},{6,2},{7,3},{8,4},{9,5},{10,6},{11,7},{12,8},{13,9},{1... | collective-permute-start | bytes 393224 | tf_op jit(solution)/shard_map/ppermute | solution.py:14
  92.1 10.1 %collective-permute-start.11 = (bf16[256,256]{0,1:T(8,128)(2,1)S(1)}, bf16[256,256]{0,1:T(8,128)(2,1)S(1)}, u32[]{:S(2)}, u32[]{:S(2)}) collective-permute-start(bf16[256,256]{0,1:T(8,128)(2,1)S(1)} %get-tuple-element.21), channel_id=1, source_target_pairs={{5,0},{6,1},{7,2},{8,3},{9,4},{10,5},{11,6},{12,7},{13,8},{14,9},{... | collective-permute-start | bytes 393224 | tf_op jit(solution)/shard_map/ppermute | solution.py:14
  94.1 13.0 %collective-permute-start.12 = (bf16[256,256]{0,1:T(8,128)(2,1)S(1)}, bf16[256,256]{0,1:T(8,128)(2,1)}, u32[]{:S(2)}, u32[]{:S(2)}) collective-permute-start(bf16[256,256]{0,1:T(8,128)(2,1)S(1)} %get-tuple-element.20), channel_id=1, source_target_pairs={{6,0},{7,1},{8,2},{9,3},{10,4},{11,5},{12,6},{13,7},{14,8},{15,9},... | collective-permute-start | bytes 393224 | tf_op jit(solution)/shard_map/ppermute | solution.py:14
  96.0 11.0 %collective-permute-start.13 = (bf16[256,256]{0,1:T(8,128)(2,1)S(1)}, bf16[256,256]{0,1:T(8,128)(2,1)}, u32[]{:S(2)}, u32[]{:S(2)}) collective-permute-start(bf16[256,256]{0,1:T(8,128)(2,1)S(1)} %get-tuple-element.19), channel_id=1, source_target_pairs={{7,0},{8,1},{9,2},{10,3},{11,4},{12,5},{13,6},{14,7},{15,8},{16,9}... | collective-permute-start | bytes 393224 | tf_op jit(solution)/shard_map/ppermute | solution.py:14
  97.3 9.8 %collective-permute-start.7 = (bf16[256,256]{0,1:T(8,128)(2,1)S(1)}, bf16[256,256]{0,1:T(8,128)(2,1)}, u32[]{:S(2)}, u32[]{:S(2)}) collective-permute-start(bf16[256,256]{0,1:T(8,128)(2,1)S(1)} %get-tuple-element.18), channel_id=1, source_target_pairs={{1,0},{2,1},{3,2},{4,3},{5,4},{6,5},{7,6},{8,7},{9,8},{10,9},{11,1... | collective-permute-start | bytes 393224 | tf_op jit(solution)/shard_map/ppermute | solution.py:14
  99.2 3.0 %copy-start.2 = (bf16[256,256]{0,1:T(8,128)(2,1)}, bf16[256,256]{0,1:T(8,128)(2,1)S(1)}, u32[]{:S(2)}) copy-start(bf16[256,256]{0,1:T(8,128)(2,1)S(1)} %collective-permute-done.10) | copy-start | bytes 393220
  99.2 14.6 %collective-permute-start.8 = (bf16[256,256]{0,1:T(8,128)(2,1)S(1)}, bf16[256,256]{0,1:T(8,128)(2,1)}, u32[]{:S(2)}, u32[]{:S(2)}) collective-permute-start(bf16[256,256]{0,1:T(8,128)(2,1)S(1)} %get-tuple-element.24), channel_id=1, source_target_pairs={{2,0},{3,1},{4,2},{5,3},{6,4},{7,5},{8,6},{9,7},{10,8},{11,9},{12,... | collective-permute-start | bytes 393224 | tf_op jit(solution)/shard_map/ppermute | solution.py:14
  102.2 0.7 copy-start.3
  102.9 11.2 %collective-permute-start.9 = (bf16[256,256]{0,1:T(8,128)(2,1)S(1)}, bf16[256,256]{0,1:T(8,128)(2,1)}, u32[]{:S(2)}, u32[]{:S(2)}) collective-permute-start(bf16[256,256]{0,1:T(8,128)(2,1)S(1)} %get-tuple-element.23), channel_id=1, source_target_pairs={{3,0},{4,1},{5,2},{6,3},{7,4},{8,5},{9,6},{10,7},{11,8},{12,9},{13... | collective-permute-start | bytes 393224 | tf_op jit(solution)/shard_map/ppermute | solution.py:14
Sparse Core Ops, SparseCore 0:
  28.2 46.0 all-gather.1
  77.1 43.4 reduce-scatter.1

commit v2 on v1

--- a/solution.py
+++ b/solution.py
@@ -12,6 +12,69 @@
     count = lax.axis_size(axis)
     first, last = (max(0, -steps), min(count, count - steps))
     return lax.ppermute(value, axis, [(source, source + steps) for source in range(first, last)])
+
+
+def ring_shift(value, axis, steps):
+    count = lax.axis_size(axis)
+    return lax.ppermute(value, axis, [(source, (source + steps) % count) for source in range(count)])
+
+
+def weight_columns(out_weight, index, begin, width):
+    block = out_weight.shape[0]
+    return lax.dynamic_slice_in_dim(out_weight, index * block + begin, width, axis=1)
+
+
+def ring_gather_dot(out_weight, out_grad, axis):
+    count = lax.axis_size(axis)
+    me = lax.axis_index(axis)
+    block = out_grad.shape[0]
+    half = block // 2
+
+    def term(index, begin, width, piece):
+        return jnp.dot(
+            weight_columns(out_weight, index % count, begin, width),
+            piece,
+            preferred_element_type=jnp.float32,
+        )
+
+    total = term(me, 0, block, out_grad)
+    ahead, behind = out_grad, out_grad
+    for step in range(1, count // 2 + 1):
+        if step < count - step:
+            ahead = ring_shift(ahead, axis, 1)
+            behind = ring_shift(behind, axis, -1)
+            total = total + term(me - step, 0, block, ahead)
+            total = total + term(me + step, 0, block, behind)
+        else:
+            low = ring_shift(ahead[:half], axis, 1)
+            high = ring_shift(behind[half:], axis, -1)
+            total = total + term(me - step, 0, half, low)
+            total = total + term(me - step, half, half, high)
+    return total
+
+
+def ring_reduce_scatter_out(out_weight, attn, axis):
+    count = lax.axis_size(axis)
+    me = lax.axis_index(axis)
+    block = out_weight.shape[0]
+    half = block // 2
+
+    def term(index, begin):
+        return lax.dot_general(
+            weight_columns(out_weight, index % count, begin, half),
+            attn,
+            (((0,), (1,)), ((), ())),
+            preferred_element_type=jnp.float32,
+        )
+
+    low = term(me - 1, 0)
+    high = term(me + 1, half)
+    for step in range(1, count):
+        low = ring_shift(low.astype(jnp.bfloat16), axis, 1).astype(jnp.float32) + term(me - 1 - step, 0)
+        high = ring_shift(high.astype(jnp.bfloat16), axis, -1).astype(jnp.float32) + term(
+            me + 1 + step, half
+        )
+    return jnp.concatenate([low, high], axis=0).astype(jnp.bfloat16)
 
 
 def per_device(queries, keys, values, out_weight, out_grad, doc_lengths):
@@ -53,19 +116,8 @@
         "gtk,kd->tgd", probs, flat_values, preferred_element_type=jnp.float32
     ).astype(jnp.bfloat16)
     attn = attn_heads.reshape(tok_rows, group_size * head_dim)
-    out_partial = lax.dot_general(
-        out_weight, attn, (((0,), (1,)), ((), ())), preferred_element_type=jnp.float32
-    ).astype(jnp.bfloat16)
-    gathered = lax.all_gather(out_grad, "heads", axis=0, tiled=True)
-    out_t = lax.psum_scatter(
-        out_partial, "heads", scatter_dimension=0, tiled=True
-    )
-    _, gathered = lax.optimization_barrier((out_partial, gathered))
-    grad_attn = jnp.dot(
-        out_weight,
-        gathered,
-        preferred_element_type=jnp.float32,
-    ).astype(jnp.bfloat16)
+    out_t = ring_reduce_scatter_out(out_weight, attn, "heads")
+    grad_attn = ring_gather_dot(out_weight, out_grad, "heads").astype(jnp.bfloat16)
     grad_heads = grad_attn.reshape(group_size, head_dim, tok_rows)
     delta_sum = jnp.einsum(
         "tgd,gdt->gt", attn_heads, grad_heads, preferred_element_type=jnp.float32

time: 130 us -> 221 us (1.70)
  the two profiles are of different devices: /device:TPU:6 before, /device:TPU:450 now
where the time goes in v2:
time: 221 us; the launch traced here: 219 us
  starting transfers between devices  125 us (57%)
  matrix products  37.8 us (17%)
  waiting for transfers between devices  33.2 us (15%)
  other arithmetic  13.9 us (6%)
  local copies, waits for them, and re-layouts  7.1 us (3%)
    ppermute x22, starting transfers between devices, ring_shift(): lax.ppermute(value, axis, [(source, (source + steps) % count) for source...  80.2 us
    ppermute x14, starting transfers between devices, passed_along(): lax.ppermute(value, axis, [(source, source + steps) for source in range(f...  44.7 us
    dot_general x16, matrix products, term(): lax.dot_general(weight_columns(out_weight, index % count, begin, half), a...  23.1 us
    ppermute x22, waiting for transfers between devices, ring_shift(): lax.ppermute(value, axis, [(source, (source + steps) % count) for source...  18.9 us
    ppermute x14, waiting for transfers between devices, passed_along(): lax.ppermute(value, axis, [(source, source + steps) for source in range(f...  14.3 us
    sub x1, matrix products, per_device(): expons = jnp.exp(scores - largest)  4.83 us
  transfers between devices with their start and end apart: 36, of which 11 were waited for; matrix products, arithmetic and copies ran while one was open for 20% of the time, Pallas kernels for 0%

profile of v2, /device:TPU:450, one launch (start us, length us, event | category | flops | bytes accessed | tf_op | source)
XLA Modules:
  0.0 218.9 jit_solution(4597712773302572207)
XLA Ops:
  2.4 1.3 collective-permute-start.6
  3.7 1.3 collective-permute-start.5
  5.0 3.5 %collective-permute-start.4 = (bf16[256,256]{1,0:T(8,128)(2,1)S(1)}, bf16[256,256]{1,0:T(8,128)(2,1)S(1)}, u32[]{:S(2)}, u32[]{:S(2)}) collective-permute-start(bf16[256,256]{1,0:T(8,128)(2,1)S(1)} %constant_dynamic-update-slice_fusion), channel_id=1, source_target_pairs={{0,5},{1,6},{2,7},{3,8},{4,9},{5,10},{6,11},{7,12},{8,13},{9,14},{... | collective-permute-start | bytes 393224 | tf_op jit(solution)/shard_map/ppermute | solution.py:14
  8.5 1.9 collective-permute-start.3
  10.4 1.9 collective-permute-start
  14.3 1.1 copy.72
  16.2 1.4 fusion.23
  18.1 3.3 %collective-permute-start.1 = (bf16[256,256]{1,0:T(8,128)(2,1)S(1)}, bf16[256,256]{1,0:T(8,128)(2,1)S(1)}, u32[]{:S(2)}, u32[]{:S(2)}) collective-permute-start(bf16[256,256]{1,0:T(8,128)(2,1)S(1)} %constant_dynamic-update-slice_fusion), channel_id=1, source_target_pairs={{0,2},{1,3},{2,4},{3,5},{4,6},{5,7},{6,8},{7,9},{8,10},{9,11},{10,... | collective-permute-start | bytes 393224 | tf_op jit(solution)/shard_map/ppermute | solution.py:14
  21.4 6.3 %collective-permute-done.1 = bf16[256,256]{1,0:T(8,128)(2,1)S(1)} collective-permute-done((bf16[256,256]{1,0:T(8,128)(2,1)S(1)}, bf16[256,256]{1,0:T(8,128)(2,1)S(1)}, u32[]{:S(2)}, u32[]{:S(2)}) %collective-permute-start.1) | collective-permute-done | bytes 131104 | tf_op jit(solution)/shard_map/ppermute | solution.py:14
  27.7 1.9 collective-permute-start.2
  29.7 7.5 %collective-permute-done.2 = bf16[256,256]{1,0:T(8,128)(2,1)S(1)} collective-permute-done((bf16[256,256]{1,0:T(8,128)(2,1)S(1)}, bf16[256,256]{1,0:T(8,128)(2,1)S(1)}, u32[]{:S(2)}, u32[]{:S(2)}) %collective-permute-start.2) | collective-permute-done | bytes 131104 | tf_op jit(solution)/shard_map/ppermute | solution.py:14
  37.2 5.4 %collective-permute-start.22 = (bf16[512,256]{1,0:T(8,128)(2,1)}, bf16[512,256]{1,0:T(8,128)(2,1)S(1)}, u32[]{:S(2)}, u32[]{:S(2)}) collective-permute-start(bf16[512,256]{1,0:T(8,128)(2,1)} %param.10), channel_id=1, source_target_pairs={{0,448},{64,0},{128,64},{192,128},{256,192},{320,256},{384,320},{4... | collective-permute-start | bytes 786440 | tf_op jit(solution)/shard_map/ppermute | solution.py:19
  42.6 1.9 collective-permute-start.21
  44.9 4.8 %fusion.102 = (f32[4,256]{1,0:T(4,128)S(1)}, f32[4,256,2048]{1,2,0:T(8,128)}) fusion(pred[256,2048]{0,1:T(8,128)(4,1)S(1)} %compare_and_fusion, bf16[2048,128,1]{1,0,2:T(8,128)(2,1)S(1)} %bitcast.118, bf16[256,4,128]{0,2,1:T(8,128)(2,1)S(1)} %bitcast.122), kind=kOutput, calls=%fused_computation.145 | convolution fusion | flops 545261568 | bytes 9703424 | tf_op jit(solution)/shard_map/sub | solution.py:112
  49.8 4.3 %fusion.5 = bf16[4,256,2048]{1,2,0:T(8,128)(2,1)S(1)} fusion(f32[4,256,2048]{1,2,0:T(8,128)} %get-tuple-element.28, f32[4,256]{1,0:T(4,128)S(1)} %get-tuple-element.27), kind=kLoop, calls=%fused_computation.9 | loop fusion | flops 4194304 | bytes 12587008 | tf_op jit(solution)/shard_map/convert_element_type | solution.py:114
  54.0 5.1 %collective-permute-start.24 = (bf16[512,256]{1,0:T(8,128)(2,1)S(1)}, bf16[512,256]{1,0:T(8,128)(2,1)S(1)}, u32[]{:S(2)}, u32[]{:S(2)}) collective-permute-start(bf16[512,256]{1,0:T(8,128)(2,1)S(1)} %collective-permute-done.22), channel_id=1, source_target_pairs={{0,448},{64,0},{128,64},{192,128},{256,192},{320,256},{384,320},{4... | collective-permute-start | bytes 786440 | tf_op jit(solution)/shard_map/ppermute | solution.py:19
  59.2 1.9 collective-permute-start.23
  61.8 2.2 collective-permute-done.24
  63.9 5.6 %collective-permute-start.26 = (bf16[512,256]{1,0:T(8,128)(2,1)S(1)}, bf16[512,256]{1,0:T(8,128)(2,1)S(1)}, u32[]{:S(2)}, u32[]{:S(2)}) collective-permute-start(bf16[512,256]{1,0:T(8,128)(2,1)S(1)} %collective-permute-done.24), channel_id=1, source_target_pairs={{0,448},{64,0},{128,64},{192,128},{256,192},{320,256},{384,320},{4... | collective-permute-start | bytes 786440 | tf_op jit(solution)/shard_map/ppermute | solution.py:19
  69.5 1.9 collective-permute-start.25
  72.1 1.3 collective-permute-done.26
  73.4 5.6 %collective-permute-start.28 = (bf16[256,256]{1,0:T(8,128)(2,1)S(1)}, bf16[256,256]{1,0:T(8,128)(2,1)S(1)}, u32[]{:S(2)}, u32[]{:S(2)}) collective-permute-start(bf16[256,256]{1,0:T(8,128)(2,1)S(1)} %slice.76), channel_id=1, source_target_pairs={{0,448},{64,0},{128,64},{192,128},{256,192},{320,256},{384,320},{4... | collective-permute-start | bytes 393224 | tf_op jit(solution)/shard_map/ppermute | solution.py:19
  79.0 1.9 collective-permute-start.27
  81.7 5.4 %collective-permute-done.27 = bf16[256,256]{1,0:T(8,128)(2,1)S(1)} collective-permute-done((bf16[256,256]{1,0:T(8,128)(2,1)S(1)}, bf16[256,256]{1,0:T(8,128)(2,1)S(1)}, u32[]{:S(2)}, u32[]{:S(2)}) %collective-permute-start.27) | collective-permute-done | bytes 131104 | tf_op jit(solution)/shard_map/ppermute | solution.py:19
  88.5 1.5 convolution_bitcast_fusion
  90.7 1.7 multiply_convert_fusion
  93.2 1.5 convolution_bitcast_fusion.1
  97.8 1.2 convolution_convert_fusion.2
  99.1 1.9 collective-permute-start.7
  101.0 5.3 %collective-permute-start.14 = (bf16[256,256]{1,0:T(8,128)(2,1)S(1)}, bf16[256,256]{1,0:T(8,128)(2,1)S(1)}, u32[]{:S(2)}, u32[]{:S(2)}) collective-permute-start(bf16[256,256]{1,0:T(8,128)(2,1)S(1)} %convolution_convert_fusion.2), channel_id=1, source_target_pairs={{0,448},{64,0},{128,64},{192,128},{256,192},{320,256},{384,320},{4... | collective-permute-start | bytes 393224 | tf_op jit(solution)/shard_map/ppermute | solution.py:19
  106.3 1.2 fusion.35
  107.5 1.2 fusion.37
  108.8 1.9 fusion.39
  110.7 1.9 fusion.41
  112.6 1.9 fusion.43
  114.6 1.9 fusion.45
  116.5 1.2 fusion.50
  117.7 1.2 fusion.52
  118.9 1.9 fusion.54
  121.1 1.9 collective-permute-start.29
  123.0 4.5 %collective-permute-start.35 = (bf16[256,256]{0,1:T(8,128)(2,1)S(1)}, bf16[256,256]{0,1:T(8,128)(2,1)S(1)}, u32[]{:S(2)}, u32[]{:S(2)}) collective-permute-start(bf16[256,256]{0,1:T(8,128)(2,1)S(1)} %get-tuple-element.17), channel_id=1, source_target_pairs={{7,0},{8,1},{9,2},{10,3},{11,4},{12,5},{13,6},{14,7},{15,8},{16,9}... | collective-permute-start | bytes 393224 | tf_op jit(solution)/shard_map/ppermute | solution.py:14
  127.6 4.8 %collective-permute-start.34 = (bf16[256,256]{0,1:T(8,128)(2,1)S(1)}, bf16[256,256]{0,1:T(8,128)(2,1)S(1)}, u32[]{:S(2)}, u32[]{:S(2)}) collective-permute-start(bf16[256,256]{0,1:T(8,128)(2,1)S(1)} %get-tuple-element.18), channel_id=1, source_target_pairs={{6,0},{7,1},{8,2},{9,3},{10,4},{11,5},{12,6},{13,7},{14,8},{15,9},... | collective-permute-start | bytes 393224 | tf_op jit(solution)/shard_map/ppermute | solution.py:14
  132.4 1.9 fusion.56
  134.3 5.1 %collective-permute-start.33 = (bf16[256,256]{0,1:T(8,128)(2,1)S(1)}, bf16[256,256]{0,1:T(8,128)(2,1)S(1)}, u32[]{:S(2)}, u32[]{:S(2)}) collective-permute-start(bf16[256,256]{0,1:T(8,128)(2,1)S(1)} %get-tuple-element.19), channel_id=1, source_target_pairs={{5,0},{6,1},{7,2},{8,3},{9,4},{10,5},{11,6},{12,7},{13,8},{14,9},{... | collective-permute-start | bytes 393224 | tf_op jit(solution)/shard_map/ppermute | solution.py:14
  139.4 1.2 add_convert_fusion.13
  140.7 3.9 %collective-permute-start.32 = (bf16[256,256]{0,1:T(8,128)(2,1)S(1)}, bf16[256,256]{0,1:T(8,128)(2,1)S(1)}, u32[]{:S(2)}, u32[]{:S(2)}) collective-permute-start(bf16[256,256]{0,1:T(8,128)(2,1)S(1)} %get-tuple-element.20), channel_id=1, source_target_pairs={{4,0},{5,1},{6,2},{7,3},{8,4},{9,5},{10,6},{11,7},{12,8},{13,9},{1... | collective-permute-start | bytes 393224 | tf_op jit(solution)/shard_map/ppermute | solution.py:14
  144.6 7.4 %collective-permute-start.31 = (bf16[256,256]{0,1:T(8,128)(2,1)S(1)}, bf16[256,256]{0,1:T(8,128)(2,1)S(1)}, u32[]{:S(2)}, u32[]{:S(2)}) collective-permute-start(bf16[256,256]{0,1:T(8,128)(2,1)S(1)} %get-tuple-element.21), channel_id=1, source_target_pairs={{3,0},{4,1},{5,2},{6,3},{7,4},{8,5},{9,6},{10,7},{11,8},{12,9},{13... | collective-permute-start | bytes 393224 | tf_op jit(solution)/shard_map/ppermute | solution.py:14
  152.1 1.9 collective-permute-start.30
  154.0 1.9 add_convert_fusion.6
  155.9 2.0 collective-permute-start.8
  157.9 5.1 %collective-permute-start.15 = (bf16[256,256]{1,0:T(8,128)(2,1)}, bf16[256,256]{1,0:T(8,128)(2,1)}, u32[]{:S(2)}, u32[]{:S(2)}) collective-permute-start(bf16[256,256]{1,0:T(8,128)(2,1)} %add_convert_fusion.6), channel_id=1, source_target_pairs={{0,448},{64,0},{128,64},{192,128},{256,192},{320,256},{384,320},{4... | collective-permute-start | bytes 393224 | tf_op jit(solution)/shard_map/ppermute | solution.py:19
  164.8 2.2 collective-permute-done.15
  167.9 5.6 %collective-permute-start.16 = (bf16[256,256]{1,0:T(8,128)(2,1)S(1)}, bf16[256,256]{1,0:T(8,128)(2,1)S(1)}, u32[]{:S(2)}, u32[]{:S(2)}) collective-permute-start(bf16[256,256]{1,0:T(8,128)(2,1)S(1)} %add_convert_fusion.5), channel_id=1, source_target_pairs={{0,448},{64,0},{128,64},{192,128},{256,192},{320,256},{384,320},{4... | collective-permute-start | bytes 393224 | tf_op jit(solution)/shard_map/ppermute | solution.py:19
  173.5 1.0 add_convert_fusion.12
  174.6 1.9 collective-permute-start.9
  177.5 5.4 %collective-permute-start.17 = (bf16[256,256]{1,0:T(8,128)(2,1)S(1)}, bf16[256,256]{1,0:T(8,128)(2,1)S(1)}, u32[]{:S(2)}, u32[]{:S(2)}) collective-permute-start(bf16[256,256]{1,0:T(8,128)(2,1)S(1)} %add_convert_fusion.4), channel_id=1, source_target_pairs={{0,448},{64,0},{128,64},{192,128},{256,192},{320,256},{384,320},{4... | collective-permute-start | bytes 393224 | tf_op jit(solution)/shard_map/ppermute | solution.py:19
  183.8 1.9 collective-permute-start.10
  186.8 5.1 %collective-permute-start.18 = (bf16[256,256]{1,0:T(8,128)(2,1)S(1)}, bf16[256,256]{1,0:T(8,128)(2,1)S(1)}, u32[]{:S(2)}, u32[]{:S(2)}) collective-permute-start(bf16[256,256]{1,0:T(8,128)(2,1)S(1)} %add_convert_fusion.3), channel_id=1, source_target_pairs={{0,448},{64,0},{128,64},{192,128},{256,192},{320,256},{384,320},{4... | collective-permute-start | bytes 393224 | tf_op jit(solution)/shard_map/ppermute | solution.py:19
  192.0 1.9 collective-permute-start.11
  195.4 5.6 %collective-permute-start.19 = (bf16[256,256]{1,0:T(8,128)(2,1)S(1)}, bf16[256,256]{1,0:T(8,128)(2,1)S(1)}, u32[]{:S(2)}, u32[]{:S(2)}) collective-permute-start(bf16[256,256]{1,0:T(8,128)(2,1)S(1)} %add_convert_fusion.2), channel_id=1, source_target_pairs={{0,448},{64,0},{128,64},{192,128},{256,192},{320,256},{384,320},{4... | collective-permute-start | bytes 393224 | tf_op jit(solution)/shard_map/ppermute | solution.py:19
  202.0 1.9 collective-permute-start.12
  203.9 5.1 %collective-permute-start.20 = (bf16[256,256]{1,0:T(8,128)(2,1)S(1)}, bf16[256,256]{1,0:T(8,128)(2,1)S(1)}, u32[]{:S(2)}, u32[]{:S(2)}) collective-permute-start(bf16[256,256]{1,0:T(8,128)(2,1)S(1)} %add_convert_fusion.1), channel_id=1, source_target_pairs={{0,448},{64,0},{128,64},{192,128},{256,192},{320,256},{384,320},{4... | collective-permute-start | bytes 393224 | tf_op jit(solution)/shard_map/ppermute | solution.py:19
  210.1 1.9 collective-permute-start.13
  212.0 6.1 %collective-permute-done.13 = bf16[256,256]{1,0:T(8,128)(2,1)S(1)} collective-permute-done((bf16[256,256]{1,0:T(8,128)(2,1)S(1)}, bf16[256,256]{1,0:T(8,128)(2,1)S(1)}, u32[]{:S(2)}, u32[]{:S(2)}) %collective-permute-start.13) | collective-permute-done | bytes 131104 | tf_op jit(solution)/shard_map/ppermute | solution.py:19
  (95 shorter events, 22.9 us)
Async XLA Ops:
  0.6 42.0 %copy-start.2 = (bf16[512,256]{1,0:T(8,128)(2,1)S(1)}, bf16[512,256]{1,0:T(8,128)(2,1)}, u32[]{:S(2)}) copy-start(bf16[512,256]{1,0:T(8,128)(2,1)} %param.10) | copy-start | bytes 786436
  2.4 42.2 %collective-permute-start.6 = (bf16[256,256]{1,0:T(8,128)(2,1)S(1)}, bf16[256,256]{1,0:T(8,128)(2,1)S(1)}, u32[]{:S(2)}, u32[]{:S(2)}) collective-permute-start(bf16[256,256]{1,0:T(8,128)(2,1)S(1)} %constant_dynamic-update-slice_fusion), channel_id=1, source_target_pairs={{0,7},{1,8},{2,9},{3,10},{4,11},{5,12},{6,13},{7,14},{8,15},{9,16}... | collective-permute-start | bytes 393224 | tf_op jit(solution)/shard_map/ppermute | solution.py:14
  3.7 40.9 %collective-permute-start.5 = (bf16[256,256]{1,0:T(8,128)(2,1)S(1)}, bf16[256,256]{1,0:T(8,128)(2,1)S(1)}, u32[]{:S(2)}, u32[]{:S(2)}) collective-permute-start(bf16[256,256]{1,0:T(8,128)(2,1)S(1)} %constant_dynamic-update-slice_fusion), channel_id=1, source_target_pairs={{0,6},{1,7},{2,8},{3,9},{4,10},{5,11},{6,12},{7,13},{8,14},{9,15},... | collective-permute-start | bytes 393224 | tf_op jit(solution)/shard_map/ppermute | solution.py:14
  5.0 39.6 %collective-permute-start.4 = (bf16[256,256]{1,0:T(8,128)(2,1)S(1)}, bf16[256,256]{1,0:T(8,128)(2,1)S(1)}, u32[]{:S(2)}, u32[]{:S(2)}) collective-permute-start(bf16[256,256]{1,0:T(8,128)(2,1)S(1)} %constant_dynamic-update-slice_fusion), channel_id=1, source_target_pairs={{0,5},{1,6},{2,7},{3,8},{4,9},{5,10},{6,11},{7,12},{8,13},{9,14},{... | collective-permute-start | bytes 393224 | tf_op jit(solution)/shard_map/ppermute | solution.py:14
  8.5 34.1 %collective-permute-start.3 = (bf16[256,256]{1,0:T(8,128)(2,1)S(1)}, bf16[256,256]{1,0:T(8,128)(2,1)S(1)}, u32[]{:S(2)}, u32[]{:S(2)}) collective-permute-start(bf16[256,256]{1,0:T(8,128)(2,1)S(1)} %constant_dynamic-update-slice_fusion), channel_id=1, source_target_pairs={{0,4},{1,5},{2,6},{3,7},{4,8},{5,9},{6,10},{7,11},{8,12},{9,13},{1... | collective-permute-start | bytes 393224 | tf_op jit(solution)/shard_map/ppermute | solution.py:14
  10.4 7.7 %collective-permute-start = (bf16[256,256]{1,0:T(8,128)(2,1)S(1)}, bf16[256,256]{1,0:T(8,128)(2,1)S(1)}, u32[]{:S(2)}, u32[]{:S(2)}) collective-permute-start(bf16[256,256]{1,0:T(8,128)(2,1)S(1)} %constant_dynamic-update-slice_fusion), channel_id=1, source_target_pairs={{0,1},{1,2},{2,3},{3,4},{4,5},{5,6},{6,7},{7,8},{8,9},{9,10},{10,1... | collective-permute-start | bytes 393224 | tf_op jit(solution)/shard_map/ppermute | solution.py:14
  18.1 9.7 %collective-permute-start.1 = (bf16[256,256]{1,0:T(8,128)(2,1)S(1)}, bf16[256,256]{1,0:T(8,128)(2,1)S(1)}, u32[]{:S(2)}, u32[]{:S(2)}) collective-permute-start(bf16[256,256]{1,0:T(8,128)(2,1)S(1)} %constant_dynamic-update-slice_fusion), channel_id=1, source_target_pairs={{0,2},{1,3},{2,4},{3,5},{4,6},{5,7},{6,8},{7,9},{8,10},{9,11},{10,... | collective-permute-start | bytes 393224 | tf_op jit(solution)/shard_map/ppermute | solution.py:14
  27.7 9.5 %collective-permute-start.2 = (bf16[256,256]{1,0:T(8,128)(2,1)S(1)}, bf16[256,256]{1,0:T(8,128)(2,1)S(1)}, u32[]{:S(2)}, u32[]{:S(2)}) collective-permute-start(bf16[256,256]{1,0:T(8,128)(2,1)S(1)} %constant_dynamic-update-slice_fusion), channel_id=1, source_target_pairs={{0,3},{1,4},{2,5},{3,6},{4,7},{5,8},{6,9},{7,10},{8,11},{9,12},{10... | collective-permute-start | bytes 393224 | tf_op jit(solution)/shard_map/ppermute | solution.py:14
  37.2 16.8 %collective-permute-start.22 = (bf16[512,256]{1,0:T(8,128)(2,1)}, bf16[512,256]{1,0:T(8,128)(2,1)S(1)}, u32[]{:S(2)}, u32[]{:S(2)}) collective-permute-start(bf16[512,256]{1,0:T(8,128)(2,1)} %param.10), channel_id=1, source_target_pairs={{0,448},{64,0},{128,64},{192,128},{256,192},{320,256},{384,320},{4... | collective-permute-start | bytes 786440 | tf_op jit(solution)/shard_map/ppermute | solution.py:19
  42.6 16.5 %collective-permute-start.21 = (bf16[512,256]{1,0:T(8,128)(2,1)S(1)}, bf16[512,256]{1,0:T(8,128)(2,1)S(1)}, u32[]{:S(2)}, u32[]{:S(2)}) collective-permute-start(bf16[512,256]{1,0:T(8,128)(2,1)S(1)} %copy-done.2), channel_id=1, source_target_pairs={{0,64},{64,128},{128,192},{192,256},{256,320},{320,384},{384,448},... | collective-permute-start | bytes 786440 | tf_op jit(solution)/shard_map/ppermute | solution.py:19
  49.8 11.4 %copy-start = (bf16[512,4096]{1,0:T(8,128)(2,1)S(1)}, bf16[512,4096]{1,0:T(8,128)(2,1)}, u32[]{:S(2)}) copy-start(bf16[512,4096]{1,0:T(8,128)(2,1)} %param.9) | copy-start | bytes 12582916
  54.0 9.9 %collective-permute-start.24 = (bf16[512,256]{1,0:T(8,128)(2,1)S(1)}, bf16[512,256]{1,0:T(8,128)(2,1)S(1)}, u32[]{:S(2)}, u32[]{:S(2)}) collective-permute-start(bf16[512,256]{1,0:T(8,128)(2,1)S(1)} %collective-permute-done.22), channel_id=1, source_target_pairs={{0,448},{64,0},{128,64},{192,128},{256,192},{320,256},{384,320},{4... | collective-permute-start | bytes 786440 | tf_op jit(solution)/shard_map/ppermute | solution.py:19
  59.2 10.3 %collective-permute-start.23 = (bf16[512,256]{1,0:T(8,128)(2,1)S(1)}, bf16[512,256]{1,0:T(8,128)(2,1)S(1)}, u32[]{:S(2)}, u32[]{:S(2)}) collective-permute-start(bf16[512,256]{1,0:T(8,128)(2,1)S(1)} %collective-permute-done.21), channel_id=1, source_target_pairs={{0,64},{64,128},{128,192},{192,256},{256,320},{320,384},{384,448},... | collective-permute-start | bytes 786440 | tf_op jit(solution)/shard_map/ppermute | solution.py:19
  63.9 9.5 %collective-permute-start.26 = (bf16[512,256]{1,0:T(8,128)(2,1)S(1)}, bf16[512,256]{1,0:T(8,128)(2,1)S(1)}, u32[]{:S(2)}, u32[]{:S(2)}) collective-permute-start(bf16[512,256]{1,0:T(8,128)(2,1)S(1)} %collective-permute-done.24), channel_id=1, source_target_pairs={{0,448},{64,0},{128,64},{192,128},{256,192},{320,256},{384,320},{4... | collective-permute-start | bytes 786440 | tf_op jit(solution)/shard_map/ppermute | solution.py:19
  69.5 9.5 %collective-permute-start.25 = (bf16[512,256]{1,0:T(8,128)(2,1)S(1)}, bf16[512,256]{1,0:T(8,128)(2,1)S(1)}, u32[]{:S(2)}, u32[]{:S(2)}) collective-permute-start(bf16[512,256]{1,0:T(8,128)(2,1)S(1)} %collective-permute-done.23), channel_id=1, source_target_pairs={{0,64},{64,128},{128,192},{192,256},{256,320},{320,384},{384,448},... | collective-permute-start | bytes 786440 | tf_op jit(solution)/shard_map/ppermute | solution.py:19
  73.4 8.1 %collective-permute-start.28 = (bf16[256,256]{1,0:T(8,128)(2,1)S(1)}, bf16[256,256]{1,0:T(8,128)(2,1)S(1)}, u32[]{:S(2)}, u32[]{:S(2)}) collective-permute-start(bf16[256,256]{1,0:T(8,128)(2,1)S(1)} %slice.76), channel_id=1, source_target_pairs={{0,448},{64,0},{128,64},{192,128},{256,192},{320,256},{384,320},{4... | collective-permute-start | bytes 393224 | tf_op jit(solution)/shard_map/ppermute | solution.py:19
  79.0 8.1 %collective-permute-start.27 = (bf16[256,256]{1,0:T(8,128)(2,1)S(1)}, bf16[256,256]{1,0:T(8,128)(2,1)S(1)}, u32[]{:S(2)}, u32[]{:S(2)}) collective-permute-start(bf16[256,256]{1,0:T(8,128)(2,1)S(1)} %slice.75), channel_id=1, source_target_pairs={{0,64},{64,128},{128,192},{192,256},{256,320},{320,384},{384,448},... | collective-permute-start | bytes 393224 | tf_op jit(solution)/shard_map/ppermute | solution.py:19
  87.1 2.8 %slice-start = ((s8[8388608]{0:T(1024)(128)(4,1)}), s8[4194304]{0:T(1024)(128)(4,1)S(1)}, s32[]{:S(2)}) async-start(s8[8388608]{0:T(1024)(128)(4,1)} %bitcast.114), calls=%async_computation | async-start | bytes 8388608
  87.7 3.0 %slice-start.1 = ((s8[8388608]{0:T(1024)(128)(4,1)}), s8[4194304]{0:T(1024)(128)(4,1)S(1)}, s32[]{:S(2)}) async-start(s8[8388608]{0:T(1024)(128)(4,1)} %bitcast.114), calls=%async_computation.1 | async-start | bytes 8388608
  99.1 35.3 %collective-permute-start.7 = (bf16[256,256]{1,0:T(8,128)(2,1)S(1)}, bf16[256,256]{1,0:T(8,128)(2,1)S(1)}, u32[]{:S(2)}, u32[]{:S(2)}) collective-permute-start(bf16[256,256]{1,0:T(8,128)(2,1)S(1)} %convolution_convert_fusion.3), channel_id=1, source_target_pairs={{0,64},{64,128},{128,192},{192,256},{256,320},{320,384},{384,448},... | collective-permute-start | bytes 393224 | tf_op jit(solution)/shard_map/ppermute | solution.py:19
  101.0 39.7 %collective-permute-start.14 = (bf16[256,256]{1,0:T(8,128)(2,1)S(1)}, bf16[256,256]{1,0:T(8,128)(2,1)S(1)}, u32[]{:S(2)}, u32[]{:S(2)}) collective-permute-start(bf16[256,256]{1,0:T(8,128)(2,1)S(1)} %convolution_convert_fusion.2), channel_id=1, source_target_pairs={{0,448},{64,0},{128,64},{192,128},{256,192},{320,256},{384,320},{4... | collective-permute-start | bytes 393224 | tf_op jit(solution)/shard_map/ppermute | solution.py:19
  121.1 23.5 %collective-permute-start.29 = (bf16[256,256]{0,1:T(8,128)(2,1)S(1)}, bf16[256,256]{0,1:T(8,128)(2,1)S(1)}, u32[]{:S(2)}, u32[]{:S(2)}) collective-permute-start(bf16[256,256]{0,1:T(8,128)(2,1)S(1)} %get-tuple-element.16), channel_id=1, source_target_pairs={{1,0},{2,1},{3,2},{4,3},{5,4},{6,5},{7,6},{8,7},{9,8},{10,9},{11,1... | collective-permute-start | bytes 393224 | tf_op jit(solution)/shard_map/ppermute | solution.py:14
  123.0 29.0 %collective-permute-start.35 = (bf16[256,256]{0,1:T(8,128)(2,1)S(1)}, bf16[256,256]{0,1:T(8,128)(2,1)S(1)}, u32[]{:S(2)}, u32[]{:S(2)}) collective-permute-start(bf16[256,256]{0,1:T(8,128)(2,1)S(1)} %get-tuple-element.17), channel_id=1, source_target_pairs={{7,0},{8,1},{9,2},{10,3},{11,4},{12,5},{13,6},{14,7},{15,8},{16,9}... | collective-permute-start | bytes 393224 | tf_op jit(solution)/shard_map/ppermute | solution.py:14
  127.6 28.3 %collective-permute-start.34 = (bf16[256,256]{0,1:T(8,128)(2,1)S(1)}, bf16[256,256]{0,1:T(8,128)(2,1)S(1)}, u32[]{:S(2)}, u32[]{:S(2)}) collective-permute-start(bf16[256,256]{0,1:T(8,128)(2,1)S(1)} %get-tuple-element.18), channel_id=1, source_target_pairs={{6,0},{7,1},{8,2},{9,3},{10,4},{11,5},{12,6},{13,7},{14,8},{15,9},... | collective-permute-start | bytes 393224 | tf_op jit(solution)/shard_map/ppermute | solution.py:14
  134.3 23.6 %collective-permute-start.33 = (bf16[256,256]{0,1:T(8,128)(2,1)S(1)}, bf16[256,256]{0,1:T(8,128)(2,1)S(1)}, u32[]{:S(2)}, u32[]{:S(2)}) collective-permute-start(bf16[256,256]{0,1:T(8,128)(2,1)S(1)} %get-tuple-element.19), channel_id=1, source_target_pairs={{5,0},{6,1},{7,2},{8,3},{9,4},{10,5},{11,6},{12,7},{13,8},{14,9},{... | collective-permute-start | bytes 393224 | tf_op jit(solution)/shard_map/ppermute | solution.py:14
  140.7 22.4 %collective-permute-start.32 = (bf16[256,256]{0,1:T(8,128)(2,1)S(1)}, bf16[256,256]{0,1:T(8,128)(2,1)S(1)}, u32[]{:S(2)}, u32[]{:S(2)}) collective-permute-start(bf16[256,256]{0,1:T(8,128)(2,1)S(1)} %get-tuple-element.20), channel_id=1, source_target_pairs={{4,0},{5,1},{6,2},{7,3},{8,4},{9,5},{10,6},{11,7},{12,8},{13,9},{1... | collective-permute-start | bytes 393224 | tf_op jit(solution)/shard_map/ppermute | solution.py:14
  144.6 18.5 %collective-permute-start.31 = (bf16[256,256]{0,1:T(8,128)(2,1)S(1)}, bf16[256,256]{0,1:T(8,128)(2,1)S(1)}, u32[]{:S(2)}, u32[]{:S(2)}) collective-permute-start(bf16[256,256]{0,1:T(8,128)(2,1)S(1)} %get-tuple-element.21), channel_id=1, source_target_pairs={{3,0},{4,1},{5,2},{6,3},{7,4},{8,5},{9,6},{10,7},{11,8},{12,9},{13... | collective-permute-start | bytes 393224 | tf_op jit(solution)/shard_map/ppermute | solution.py:14
  152.1 11.0 %collective-permute-start.30 = (bf16[256,256]{0,1:T(8,128)(2,1)S(1)}, bf16[256,256]{0,1:T(8,128)(2,1)S(1)}, u32[]{:S(2)}, u32[]{:S(2)}) collective-permute-start(bf16[256,256]{0,1:T(8,128)(2,1)S(1)} %get-tuple-element.22), channel_id=1, source_target_pairs={{2,0},{3,1},{4,2},{5,3},{6,4},{7,5},{8,6},{9,7},{10,8},{11,9},{12,... | collective-permute-start | bytes 393224 | tf_op jit(solution)/shard_map/ppermute | solution.py:14
  155.9 36.0 %copy-start.1 = (f32[256,256]{1,0:T(8,128)S(1)}, f32[256,256]{1,0:T(8,128)}, u32[]{:S(2)}) copy-start(f32[256,256]{1,0:T(8,128)} %fusion.56) | copy-start | bytes 786436
  155.9 17.6 %collective-permute-start.8 = (bf16[256,256]{1,0:T(8,128)(2,1)S(1)}, bf16[256,256]{1,0:T(8,128)(2,1)}, u32[]{:S(2)}, u32[]{:S(2)}) collective-permute-start(bf16[256,256]{1,0:T(8,128)(2,1)S(1)} %add_convert_fusion.13), channel_id=1, source_target_pairs={{0,64},{64,128},{128,192},{192,256},{256,320},{320,384},{384,448},... | collective-permute-start | bytes 393224 | tf_op jit(solution)/shard_map/ppermute | solution.py:19
  157.9 9.0 %collective-permute-start.15 = (bf16[256,256]{1,0:T(8,128)(2,1)}, bf16[256,256]{1,0:T(8,128)(2,1)}, u32[]{:S(2)}, u32[]{:S(2)}) collective-permute-start(bf16[256,256]{1,0:T(8,128)(2,1)} %add_convert_fusion.6), channel_id=1, source_target_pairs={{0,448},{64,0},{128,64},{192,128},{256,192},{320,256},{384,320},{4... | collective-permute-start | bytes 393224 | tf_op jit(solution)/shard_map/ppermute | solution.py:19
  167.9 8.6 %collective-permute-start.16 = (bf16[256,256]{1,0:T(8,128)(2,1)S(1)}, bf16[256,256]{1,0:T(8,128)(2,1)S(1)}, u32[]{:S(2)}, u32[]{:S(2)}) collective-permute-start(bf16[256,256]{1,0:T(8,128)(2,1)S(1)} %add_convert_fusion.5), channel_id=1, source_target_pairs={{0,448},{64,0},{128,64},{192,128},{256,192},{320,256},{384,320},{4... | collective-permute-start | bytes 393224 | tf_op jit(solution)/shard_map/ppermute | solution.py:19
  174.6 8.3 %collective-permute-start.9 = (bf16[256,256]{1,0:T(8,128)(2,1)S(1)}, bf16[256,256]{1,0:T(8,128)(2,1)S(1)}, u32[]{:S(2)}, u32[]{:S(2)}) collective-permute-start(bf16[256,256]{1,0:T(8,128)(2,1)S(1)} %add_convert_fusion.12), channel_id=1, source_target_pairs={{0,64},{64,128},{128,192},{192,256},{256,320},{320,384},{384,448},... | collective-permute-start | bytes 393224 | tf_op jit(solution)/shard_map/ppermute | solution.py:19
  177.5 8.3 %collective-permute-start.17 = (bf16[256,256]{1,0:T(8,128)(2,1)S(1)}, bf16[256,256]{1,0:T(8,128)(2,1)S(1)}, u32[]{:S(2)}, u32[]{:S(2)}) collective-permute-start(bf16[256,256]{1,0:T(8,128)(2,1)S(1)} %add_convert_fusion.4), channel_id=1, source_target_pairs={{0,448},{64,0},{128,64},{192,128},{256,192},{320,256},{384,320},{4... | collective-permute-start | bytes 393224 | tf_op jit(solution)/shard_map/ppermute | solution.py:19
  183.8 8.1 %collective-permute-start.10 = (bf16[256,256]{1,0:T(8,128)(2,1)S(1)}, bf16[256,256]{1,0:T(8,128)(2,1)S(1)}, u32[]{:S(2)}, u32[]{:S(2)}) collective-permute-start(bf16[256,256]{1,0:T(8,128)(2,1)S(1)} %add_convert_fusion.11), channel_id=1, source_target_pairs={{0,64},{64,128},{128,192},{192,256},{256,320},{320,384},{384,448},... | collective-permute-start | bytes 393224 | tf_op jit(solution)/shard_map/ppermute | solution.py:19
  186.8 7.6 %collective-permute-start.18 = (bf16[256,256]{1,0:T(8,128)(2,1)S(1)}, bf16[256,256]{1,0:T(8,128)(2,1)S(1)}, u32[]{:S(2)}, u32[]{:S(2)}) collective-permute-start(bf16[256,256]{1,0:T(8,128)(2,1)S(1)} %add_convert_fusion.3), channel_id=1, source_target_pairs={{0,448},{64,0},{128,64},{192,128},{256,192},{320,256},{384,320},{4... | collective-permute-start | bytes 393224 | tf_op jit(solution)/shard_map/ppermute | solution.py:19
  192.0 9.0 %collective-permute-start.11 = (bf16[256,256]{1,0:T(8,128)(2,1)S(1)}, bf16[256,256]{1,0:T(8,128)(2,1)S(1)}, u32[]{:S(2)}, u32[]{:S(2)}) collective-permute-start(bf16[256,256]{1,0:T(8,128)(2,1)S(1)} %add_convert_fusion.10), channel_id=1, source_target_pairs={{0,64},{64,128},{128,192},{192,256},{256,320},{320,384},{384,448},... | collective-permute-start | bytes 393224 | tf_op jit(solution)/shard_map/ppermute | solution.py:19
  195.4 8.5 %collective-permute-start.19 = (bf16[256,256]{1,0:T(8,128)(2,1)S(1)}, bf16[256,256]{1,0:T(8,128)(2,1)S(1)}, u32[]{:S(2)}, u32[]{:S(2)}) collective-permute-start(bf16[256,256]{1,0:T(8,128)(2,1)S(1)} %add_convert_fusion.2), channel_id=1, source_target_pairs={{0,448},{64,0},{128,64},{192,128},{256,192},{320,256},{384,320},{4... | collective-permute-start | bytes 393224 | tf_op jit(solution)/shard_map/ppermute | solution.py:19
  202.0 8.1 %collective-permute-start.12 = (bf16[256,256]{1,0:T(8,128)(2,1)S(1)}, bf16[256,256]{1,0:T(8,128)(2,1)S(1)}, u32[]{:S(2)}, u32[]{:S(2)}) collective-permute-start(bf16[256,256]{1,0:T(8,128)(2,1)S(1)} %add_convert_fusion.9), channel_id=1, source_target_pairs={{0,64},{64,128},{128,192},{192,256},{256,320},{320,384},{384,448},... | collective-permute-start | bytes 393224 | tf_op jit(solution)/shard_map/ppermute | solution.py:19
  203.9 8.1 %collective-permute-start.20 = (bf16[256,256]{1,0:T(8,128)(2,1)S(1)}, bf16[256,256]{1,0:T(8,128)(2,1)S(1)}, u32[]{:S(2)}, u32[]{:S(2)}) collective-permute-start(bf16[256,256]{1,0:T(8,128)(2,1)S(1)} %add_convert_fusion.1), channel_id=1, source_target_pairs={{0,448},{64,0},{128,64},{192,128},{256,192},{320,256},{384,320},{4... | collective-permute-start | bytes 393224 | tf_op jit(solution)/shard_map/ppermute | solution.py:19
  210.1 8.1 %collective-permute-start.13 = (bf16[256,256]{1,0:T(8,128)(2,1)S(1)}, bf16[256,256]{1,0:T(8,128)(2,1)S(1)}, u32[]{:S(2)}, u32[]{:S(2)}) collective-permute-start(bf16[256,256]{1,0:T(8,128)(2,1)S(1)} %add_convert_fusion.8), channel_id=1, source_target_pairs={{0,64},{64,128},{128,192},{192,256},{256,320},{320,384},{384,448},... | collective-permute-start | bytes 393224 | tf_op jit(solution)/shard_map/ppermute | solution.py:19

commit v3 on v1

--- a/solution.py
+++ b/solution.py
@@ -27,10 +27,9 @@
         jnp.where(starts[None, :] <= positions[:, None], starts[None, :], 0), axis=1
     )
     stacked = jnp.concatenate([keys, values], axis=1)
-    blocks = [stacked[None]]
-    for offset in range(1, REACH + 1):
-        blocks.append(passed_along(stacked, "ctx", offset)[None])
-    window = jnp.concatenate(blocks, axis=0)
+    window = stacked[None]
+    while window.shape[0] < REACH + 1:
+        window = jnp.concatenate([window, passed_along(window, "ctx", window.shape[0])], axis=0)
     num_blocks = window.shape[0]
     flat_keys = window[:, :, :head_dim].reshape(num_blocks * tok_rows, head_dim)
     flat_values = window[:, :, head_dim:].reshape(num_blocks * tok_rows, head_dim)
@@ -84,10 +83,12 @@
     partial_grads = jnp.concatenate([key_part, value_part], axis=1).reshape(
         num_blocks, tok_rows, 2 * head_dim
     )
-    summed = partial_grads[0]
-    for offset in range(1, num_blocks):
-        sent = passed_along(partial_grads[offset].astype(jnp.bfloat16), "ctx", -offset)
-        summed = summed + sent.astype(jnp.float32)
+    summed = partial_grads
+    while summed.shape[0] > 1:
+        half = summed.shape[0] // 2
+        sent = passed_along(summed[half:].astype(jnp.bfloat16), "ctx", -half)
+        summed = summed[:half] + sent.astype(jnp.float32)
+    summed = summed[0]
     grad_k = summed[:, :head_dim].astype(jnp.bfloat16)
     grad_v = summed[:, head_dim:].astype(jnp.bfloat16)
     return (out_t, grad_q, grad_k, grad_v)

time: 130 us -> 123 us (0.946)
  the two profiles are of different devices: /device:TPU:6 before, /device:TPU:213 now
where the time goes in v3:
time: 123 us
  waiting for transfers between devices  41.5 us (34%)
  matrix products  24.8 us (20%)
  starting transfers between devices  22.3 us (18%)
  between operations  14.3 us (12%)
  local copies, waits for them, and re-layouts  11.2 us (9%)
  other arithmetic  8.57 us (7%)
    ppermute x6, waiting for transfers between devices, passed_along(): lax.ppermute(value, axis, [(source, source + steps) for source in range(f...  41.4 us
    ppermute x6, starting transfers between devices, passed_along(): lax.ppermute(value, axis, [(source, source + steps) for source in range(f...  22.2 us
    unnamed x14, local copies, waits for them, and re-layouts  6.78 us
    sub x1, matrix products, per_device(): expons = jnp.exp(scores - largest)  4.83 us
    dot_general x1, matrix products, per_device(): lax.dot_general(out_weight, attn, (((0,), (1,)), ((), ())), preferred_ele...  4.81 us
    dot_general x1, matrix products, per_device(): jnp.einsum('gdt,kd->gtk', grad_heads, flat_values, preferred_element_type...  4.34 us
    convert_element_type x1, other arithmetic, per_device(): probs = weights.astype(jnp.bfloat16)  4.17 us
    dot_general x1, matrix products, per_device(): jnp.dot(out_weight, gathered, preferred_element_type=jnp.float32)  4.12 us
  transfers between devices with their start and end apart: 8, of which 6 were waited for; matrix products, arithmetic and copies ran while one was open for 31% of the time, Pallas kernels for 0%

profile of v3, /device:TPU:213, one launch (start us, length us, event | category | flops | bytes accessed | tf_op | source)
XLA Modules:
  0.0 122.6 jit_solution(10732032195002310313)
XLA Ops:
  7.2 0.0 all-gather.2.cloned.1.call-start
  7.2 0.9 maximum_bitcast_fusion
  8.1 3.4 %collective-permute-start = (bf16[1,256,256]{2,1,0:T(8,128)(2,1)S(1)}, bf16[1,256,256]{2,1,0:T(8,128)(2,1)S(1)}, u32[]{:S(2)}, u32[]{:S(2)}) collective-permute-start(bf16[1,256,256]{2,1,0:T(8,128)(2,1)S(1)} %maximum_bitcast_fusion), channel_id=1, source_target_pairs={{0,1},{1,2},{2,3},{3,4},{4,5},{5,6},{6,7},{7,8},{8,9},{9,10},{10,1... | collective-permute-start | bytes 393224 | tf_op jit(solution)/shard_map/ppermute | solution.py:14
  11.5 0.0 all-gather.2.cloned.1.call-update
  11.5 0.0 reduce-scatter.2.cloned.1.call-start
  11.6 0.7 copy.45
  12.3 0.1 reduce.1
  12.5 0.7 sub.31
  13.1 0.3 collective-permute-done
  13.5 5.1 %collective-permute-start.1 = (bf16[2,256,256]{2,1,0:T(8,128)(2,1)S(1)}, bf16[2,256,256]{2,1,0:T(8,128)(2,1)S(1)}, u32[]{:S(2)}, u32[]{:S(2)}) collective-permute-start(bf16[2,256,256]{2,1,0:T(8,128)(2,1)S(1)} %pad_maximum_fusion.3), channel_id=1, source_target_pairs={{0,2},{1,3},{2,4},{3,5},{4,6},{5,7},{6,8},{7,9},{8,10},{9,11},{10,... | collective-permute-start | bytes 786440 | tf_op jit(solution)/shard_map/ppermute | solution.py:14
  18.6 0.1 add_bitcast_fusion
  18.7 1.1 copy.79
  19.8 4.7 %collective-permute-done.1 = bf16[2,256,256]{2,1,0:T(8,128)(2,1)S(1)} collective-permute-done((bf16[2,256,256]{2,1,0:T(8,128)(2,1)S(1)}, bf16[2,256,256]{2,1,0:T(8,128)(2,1)S(1)}, u32[]{:S(2)}, u32[]{:S(2)}) %collective-permute-start.1) | collective-permute-done | bytes 262176 | tf_op jit(solution)/shard_map/ppermute | solution.py:14
  24.5 0.1 pad_maximum_fusion.2
  24.5 4.8 %collective-permute-start.2 = (bf16[4,256,256]{2,1,0:T(8,128)(2,1)S(1)}, bf16[4,256,256]{2,1,0:T(8,128)(2,1)S(1)}, u32[]{:S(2)}, u32[]{:S(2)}) collective-permute-start(bf16[4,256,256]{2,1,0:T(8,128)(2,1)S(1)} %pad_maximum_fusion.2), channel_id=1, source_target_pairs={{0,4},{1,5},{2,6},{3,7},{4,8},{5,9},{6,10},{7,11},{8,12},{9,13},{1... | collective-permute-start | bytes 1572872 | tf_op jit(solution)/shard_map/ppermute | solution.py:14
  29.4 0.1 select_reduce_fusion
  29.5 0.6 compare_and_fusion
  30.1 11.2 %collective-permute-done.2 = bf16[4,256,256]{2,1,0:T(8,128)(2,1)S(1)} collective-permute-done((bf16[4,256,256]{2,1,0:T(8,128)(2,1)S(1)}, bf16[4,256,256]{2,1,0:T(8,128)(2,1)S(1)}, u32[]{:S(2)}, u32[]{:S(2)}) %collective-permute-start.2) | collective-permute-done | bytes 524320 | tf_op jit(solution)/shard_map/ppermute | solution.py:14
  41.3 0.1 pad_maximum_fusion.1
  41.4 0.3 fusion.16
  41.7 0.0 copy-start.3
  41.7 4.8 %fusion.18 = (f32[4,256]{1,0:T(4,128)S(1)}, f32[4,256,2048]{1,2,0:T(8,128)}) fusion(pred[256,2048]{0,1:T(8,128)(4,1)S(1)} %compare_and_fusion, bf16[2048,128,1]{1,0,2:T(8,128)(2,1)S(1)} %bitcast.72, bf16[256,4,128]{0,2,1:T(8,128)(2,1)S(1)} %bitcast.76), kind=kOutput, calls=%fused_computation.46 | convolution fusion | flops 545261568 | bytes 9703424 | tf_op jit(solution)/shard_map/sub | solution.py:48
  46.5 0.0 copy-done.3
  46.5 4.2 %fusion.6 = bf16[4,256,2048]{1,2,0:T(8,128)(2,1)S(1)} fusion(f32[4,256,2048]{1,2,0:T(8,128)} %get-tuple-element.23, f32[4,256]{1,0:T(4,128)S(1)} %get-tuple-element.22), kind=kLoop, calls=%fused_computation.11 | loop fusion | flops 4194304 | bytes 12587008 | tf_op jit(solution)/shard_map/convert_element_type | solution.py:50
  50.7 0.0 copy-start
  50.7 2.0 %copy-done = bf16[4,256,2048]{1,2,0:T(8,128)(2,1)} copy-done((bf16[4,256,2048]{1,2,0:T(8,128)(2,1)}, bf16[4,256,2048]{1,2,0:T(8,128)(2,1)S(1)}, u32[]{:S(2)}) %copy-start) | copy-done | bytes 4194328
  52.6 0.8 bitcast_convert_fusion
  53.4 0.2 copy.69
  53.6 4.8 %fusion.2 = bf16[4096,256]{0,1:T(8,128)(2,1)} fusion(bf16[256,512]{0,1:T(8,128)(2,1)S(1)} %bitcast.79, bf16[512,4096]{1,0:T(8,128)(2,1)} %param.9), kind=kOutput, calls=%fused_computation.6 | convolution fusion | flops 1074790400 | bytes 6553600 | tf_op jit(solution)/shard_map/dot_general | solution.py:55
  58.5 0.0 reduce-scatter.2.cloned.1.call-update
  58.5 0.0 all-gather.2.cloned.1.call-done
  58.5 4.1 %fusion.7 = bf16[512,256]{0,1:T(8,128)(2,1)S(1)} fusion(bf16[4096,256]{1,0:T(8,128)(2,1)} %all-gather.2.cloned.1.call-done, bf16[512,4096]{1,0:T(8,128)(2,1)} %param.9), kind=kOutput, calls=%fused_computation.20 | convolution fusion | flops 1073872896 | bytes 6553600 | tf_op jit(solution)/shard_map/dot_general | solution.py:63
  62.6 0.1 reshape.144
  62.7 0.2 copy.56
  62.9 0.4 multiply_reduce_fusion
  63.2 0.1 copy.70
  63.3 3.7 %convolution_bitcast_fusion = f32[2048,128]{0,1:T(8,128)S(1)} fusion(bf16[4,256,2048]{1,2,0:T(8,128)(2,1)} %copy-done, bf16[4,128,256]{2,1,0:T(8,128)(2,1)S(1)} %copy.56), kind=kOutput, calls=%fused_computation.12 | convolution fusion | flops 536870912 | bytes 5505024 | tf_op jit(solution)/shard_map/gtk,gdt->kd/dot_general | solution.py:82
  67.0 4.3 %multiply_convert_fusion = bf16[4,256,2048]{1,2,0:T(8,128)(2,1)S(1)} fusion(bf16[2048,128,1]{1,0,2:T(8,128)(2,1)S(1)} %bitcast.75, bf16[4,128,256]{2,1,0:T(8,128)(2,1)S(1)} %copy.56, f32[4,256]{1,0:T(4,128)S(1)} %copy.70, f32[4,256,2048]{1,2,0:T(8,128)} %get-tuple-element.23, f32[4,256]{1,0:T(4,128)S(1)} %get-tuple-element.22), kind=kOutput, calls=%fused_computation.2 | convolution fusion | flops 547356672 | bytes 13377536 | tf_op jit(solution)/shard_map/gdt,kd->gtk/dot_general | solution.py:72
  71.3 0.0 copy-start.1
  71.3 1.9 %copy-done.1 = bf16[4,256,2048]{1,2,0:T(8,128)(2,1)} copy-done((bf16[4,256,2048]{1,2,0:T(8,128)(2,1)}, bf16[4,256,2048]{1,2,0:T(8,128)(2,1)S(1)}, u32[]{:S(2)}) %copy-start.1) | copy-done | bytes 4194328
  73.3 1.5 %convolution_bitcast_fusion.1 = f32[2048,128]{0,1:T(8,128)S(1)} fusion(bf16[4,256,2048]{1,2,0:T(8,128)(2,1)S(1)} %multiply_convert_fusion, bf16[256,4,128]{0,2,1:T(8,128)(2,1)S(1)} %bitcast.77), kind=kOutput, calls=%fused_computation.13 | convolution fusion | flops 536870912 | bytes 5505024 | tf_op jit(solution)/shard_map/gtk,tgd->kd/dot_general | solution.py:81
  74.8 0.1 fusion.9
  74.8 1.0 copy.78
  75.9 1.9 %collective-permute-start.3 = (bf16[4,256,256]{2,1,0:T(8,128)(2,1)}, bf16[4,256,256]{2,1,0:T(8,128)(2,1)}, u32[]{:S(2)}, u32[]{:S(2)}) collective-permute-start(bf16[4,256,256]{2,1,0:T(8,128)(2,1)} %bitcast.21), channel_id=1, source_target_pairs={{4,0},{5,1},{6,2},{7,3},{8,4},{9,5},{10,6},{11,7},{12,8},{13,9},{1... | collective-permute-start | bytes 1572872 | tf_op jit(solution)/shard_map/ppermute | solution.py:14
  77.8 0.1 fusion.8
  77.9 0.0 copy-start.4
  77.9 0.3 copy.77
  78.3 0.0 copy-start.2
  78.3 15.5 %collective-permute-done.3 = bf16[4,256,256]{2,1,0:T(8,128)(2,1)} collective-permute-done((bf16[4,256,256]{2,1,0:T(8,128)(2,1)}, bf16[4,256,256]{2,1,0:T(8,128)(2,1)}, u32[]{:S(2)}, u32[]{:S(2)}) %collective-permute-start.3) | collective-permute-done | bytes 524320 | tf_op jit(solution)/shard_map/ppermute | solution.py:14
  93.8 1.2 convert_add_fusion
  95.0 1.9 %collective-permute-start.4 = (bf16[2,256,256]{2,1,0:T(8,128)(2,1)S(1)}, bf16[2,256,256]{2,1,0:T(8,128)(2,1)S(1)}, u32[]{:S(2)}, u32[]{:S(2)}) collective-permute-start(bf16[2,256,256]{2,1,0:T(8,128)(2,1)S(1)} %slice.74), channel_id=1, source_target_pairs={{2,0},{3,1},{4,2},{5,3},{6,4},{7,5},{8,6},{9,7},{10,8},{11,9},{12,... | collective-permute-start | bytes 786440 | tf_op jit(solution)/shard_map/ppermute | solution.py:14
  96.9 5.6 %collective-permute-done.4 = bf16[2,256,256]{2,1,0:T(8,128)(2,1)S(1)} collective-permute-done((bf16[2,256,256]{2,1,0:T(8,128)(2,1)S(1)}, bf16[2,256,256]{2,1,0:T(8,128)(2,1)S(1)}, u32[]{:S(2)}, u32[]{:S(2)}) %collective-permute-start.4) | collective-permute-done | bytes 262176 | tf_op jit(solution)/shard_map/ppermute | solution.py:14
  102.5 0.1 slice_add_fusion
  102.6 5.0 %collective-permute-start.5 = (bf16[1,256,256]{2,1,0:T(8,128)(2,1)S(1)}, bf16[1,256,256]{2,1,0:T(8,128)(2,1)S(1)}, u32[]{:S(2)}, u32[]{:S(2)}) collective-permute-start(bf16[1,256,256]{2,1,0:T(8,128)(2,1)S(1)} %slice.75), channel_id=1, source_target_pairs={{1,0},{2,1},{3,2},{4,3},{5,4},{6,5},{7,6},{8,7},{9,8},{10,9},{11,1... | collective-permute-start | bytes 393224 | tf_op jit(solution)/shard_map/ppermute | solution.py:14
  107.6 0.0 copy-done.4
  107.6 0.0 copy-done.2
  107.6 0.8 convolution_convert_fusion.2
  108.4 0.8 copy.60
  109.2 4.1 %collective-permute-done.5 = bf16[1,256,256]{2,1,0:T(8,128)(2,1)S(1)} collective-permute-done((bf16[1,256,256]{2,1,0:T(8,128)(2,1)S(1)}, bf16[1,256,256]{2,1,0:T(8,128)(2,1)S(1)}, u32[]{:S(2)}, u32[]{:S(2)}) %collective-permute-start.5) | collective-permute-done | bytes 131104 | tf_op jit(solution)/shard_map/ppermute | solution.py:14
  113.3 0.7 fusion.17
  114.0 0.0 reduce-scatter.2.cloned.1.call-done
  114.0 1.8 %copy.59 = bf16[512,256]{1,0:T(8,128)(2,1)} copy(bf16[512,256]{0,1:T(8,128)(2,1)} %reduce-scatter.2.cloned.1.call-done) | data formatting | bytes 524288
  (8 shorter events, 0.2 us)
Async XLA Ops:
  7.2 51.3 %all-gather.2.cloned.1.call-start = ((), (), s32[]{:S(2)}) async-start(), calls=%async_computation.2 | async-start | bytes 2359296 | tf_op jit(solution)/shard_map/all_gather | solution.py:58
  8.1 5.3 %collective-permute-start = (bf16[1,256,256]{2,1,0:T(8,128)(2,1)S(1)}, bf16[1,256,256]{2,1,0:T(8,128)(2,1)S(1)}, u32[]{:S(2)}, u32[]{:S(2)}) collective-permute-start(bf16[1,256,256]{2,1,0:T(8,128)(2,1)S(1)} %maximum_bitcast_fusion), channel_id=1, source_target_pairs={{0,1},{1,2},{2,3},{3,4},{4,5},{5,6},{6,7},{7,8},{8,9},{9,10},{10,1... | collective-permute-start | bytes 393224 | tf_op jit(solution)/shard_map/ppermute | solution.py:14
  11.5 102.5 %reduce-scatter.2.cloned.1.call-start = ((), (), s32[]{:S(2)}) async-start(), calls=%async_computation.1 | async-start | bytes 2359296 | tf_op jit(solution)/shard_map/reduce_scatter | solution.py:59
  13.5 11.0 %collective-permute-start.1 = (bf16[2,256,256]{2,1,0:T(8,128)(2,1)S(1)}, bf16[2,256,256]{2,1,0:T(8,128)(2,1)S(1)}, u32[]{:S(2)}, u32[]{:S(2)}) collective-permute-start(bf16[2,256,256]{2,1,0:T(8,128)(2,1)S(1)} %pad_maximum_fusion.3), channel_id=1, source_target_pairs={{0,2},{1,3},{2,4},{3,5},{4,6},{5,7},{6,8},{7,9},{8,10},{9,11},{10,... | collective-permute-start | bytes 786440 | tf_op jit(solution)/shard_map/ppermute | solution.py:14
  24.5 16.7 %collective-permute-start.2 = (bf16[4,256,256]{2,1,0:T(8,128)(2,1)S(1)}, bf16[4,256,256]{2,1,0:T(8,128)(2,1)S(1)}, u32[]{:S(2)}, u32[]{:S(2)}) collective-permute-start(bf16[4,256,256]{2,1,0:T(8,128)(2,1)S(1)} %pad_maximum_fusion.2), channel_id=1, source_target_pairs={{0,4},{1,5},{2,6},{3,7},{4,8},{5,9},{6,10},{7,11},{8,12},{9,13},{1... | collective-permute-start | bytes 1572872 | tf_op jit(solution)/shard_map/ppermute | solution.py:14
  41.7 4.8 %copy-start.3 = (bf16[8,256,128]{2,1,0:T(8,128)(2,1)}, bf16[8,256,128]{2,1,0:T(8,128)(2,1)S(1)}, u32[]{:S(2)}) copy-start(bf16[8,256,128]{2,1,0:T(8,128)(2,1)S(1)} %get-tuple-element.18) | copy-start | bytes 1572868
  50.7 2.0 %copy-start = (bf16[4,256,2048]{1,2,0:T(8,128)(2,1)}, bf16[4,256,2048]{1,2,0:T(8,128)(2,1)S(1)}, u32[]{:S(2)}) copy-start(bf16[4,256,2048]{1,2,0:T(8,128)(2,1)S(1)} %fusion.6) | copy-start | bytes 12582916
  71.3 1.9 %copy-start.1 = (bf16[4,256,2048]{1,2,0:T(8,128)(2,1)}, bf16[4,256,2048]{1,2,0:T(8,128)(2,1)S(1)}, u32[]{:S(2)}) copy-start(bf16[4,256,2048]{1,2,0:T(8,128)(2,1)S(1)} %multiply_convert_fusion) | copy-start | bytes 12582916
  75.9 17.9 %collective-permute-start.3 = (bf16[4,256,256]{2,1,0:T(8,128)(2,1)}, bf16[4,256,256]{2,1,0:T(8,128)(2,1)}, u32[]{:S(2)}, u32[]{:S(2)}) collective-permute-start(bf16[4,256,256]{2,1,0:T(8,128)(2,1)} %bitcast.21), channel_id=1, source_target_pairs={{4,0},{5,1},{6,2},{7,3},{8,4},{9,5},{10,6},{11,7},{12,8},{13,9},{1... | collective-permute-start | bytes 1572872 | tf_op jit(solution)/shard_map/ppermute | solution.py:14
  77.9 29.7 %copy-start.4 = (bf16[8,256,128]{2,1,0:T(8,128)(2,1)S(1)}, bf16[8,256,128]{2,1,0:T(8,128)(2,1)}, u32[]{:S(2)}) copy-start(bf16[8,256,128]{2,1,0:T(8,128)(2,1)} %copy-done.3) | copy-start | bytes 1572868
  78.3 29.3 %copy-start.2 = (bf16[4,256,2048]{1,2,0:T(8,128)(2,1)S(1)}, bf16[4,256,2048]{1,2,0:T(8,128)(2,1)}, u32[]{:S(2)}) copy-start(bf16[4,256,2048]{1,2,0:T(8,128)(2,1)} %copy-done.1) | copy-start | bytes 12582916
  95.0 7.5 %collective-permute-start.4 = (bf16[2,256,256]{2,1,0:T(8,128)(2,1)S(1)}, bf16[2,256,256]{2,1,0:T(8,128)(2,1)S(1)}, u32[]{:S(2)}, u32[]{:S(2)}) collective-permute-start(bf16[2,256,256]{2,1,0:T(8,128)(2,1)S(1)} %slice.74), channel_id=1, source_target_pairs={{2,0},{3,1},{4,2},{5,3},{6,4},{7,5},{8,6},{9,7},{10,8},{11,9},{12,... | collective-permute-start | bytes 786440 | tf_op jit(solution)/shard_map/ppermute | solution.py:14
  102.6 10.7 %collective-permute-start.5 = (bf16[1,256,256]{2,1,0:T(8,128)(2,1)S(1)}, bf16[1,256,256]{2,1,0:T(8,128)(2,1)S(1)}, u32[]{:S(2)}, u32[]{:S(2)}) collective-permute-start(bf16[1,256,256]{2,1,0:T(8,128)(2,1)S(1)} %slice.75), channel_id=1, source_target_pairs={{1,0},{2,1},{3,2},{4,3},{5,4},{6,5},{7,6},{8,7},{9,8},{10,9},{11,1... | collective-permute-start | bytes 393224 | tf_op jit(solution)/shard_map/ppermute | solution.py:14
Sparse Core Ops, SparseCore 0:
  11.6 41.2 all-gather.1
  58.6 42.0 reduce-scatter.1

commit v4 on v3

--- a/solution.py
+++ b/solution.py
@@ -3,6 +3,7 @@
 import jax
 import jax.numpy as jnp
 from jax import lax
+from jax.experimental.layout import Layout, with_layout_constraint
 from jax.sharding import PartitionSpec as P
 
 REACH = 7
@@ -55,6 +56,7 @@
     out_partial = lax.dot_general(
         out_weight, attn, (((0,), (1,)), ((), ())), preferred_element_type=jnp.float32
     ).astype(jnp.bfloat16)
+    out_partial = with_layout_constraint(out_partial, Layout((0, 1)))
     gathered = lax.all_gather(out_grad, "heads", axis=0, tiled=True)
     out_t = lax.psum_scatter(
         out_partial, "heads", scatter_dimension=0, tiled=True

time: 123 us -> 122 us (level)
  the two profiles are of different devices: /device:TPU:213 before, /device:TPU:197 now
where the time goes in v4:
time: 122 us; the launch traced here: 121 us
  waiting for transfers between devices  41.6 us (34%)
  matrix products  25.2 us (21%)
  starting transfers between devices  22.2 us (18%)
  between operations  14.3 us (12%)
  local copies, waits for them, and re-layouts  9.45 us (8%)
  other arithmetic  8.55 us (7%)
    ppermute x6, waiting for transfers between devices, passed_along(): lax.ppermute(value, axis, [(source, source + steps) for source in range(f...  41.5 us
    ppermute x6, starting transfers between devices, passed_along(): lax.ppermute(value, axis, [(source, source + steps) for source in range(f...  22.1 us
    dot_general x1, matrix products, per_device(): lax.dot_general(out_weight, attn, (((0,), (1,)), ((), ())), preferred_ele...  5.28 us
    unnamed x13, local copies, waits for them, and re-layouts  4.99 us
    sub x1, matrix products, per_device(): expons = jnp.exp(scores - largest)  4.83 us
    dot_general x1, matrix products, per_device(): jnp.einsum('gdt,kd->gtk', grad_heads, flat_values, preferred_element_type...  4.34 us
    convert_element_type x1, other arithmetic, per_device(): probs = weights.astype(jnp.bfloat16)  4.15 us
    dot_general x1, matrix products, per_device(): jnp.dot(out_weight, gathered, preferred_element_type=jnp.float32)  4.12 us
  transfers between devices with their start and end apart: 8, of which 6 were waited for; matrix products, arithmetic and copies ran while one was open for 32% of the time, Pallas kernels for 0%

profile of v4, /device:TPU:197, one launch (start us, length us, event | category | flops | bytes accessed | tf_op | source)
XLA Modules:
  0.0 121.3 jit_solution(12127682230862359117)
XLA Ops:
  7.2 0.0 all-gather.2.cloned.1.call-start
  7.2 0.9 maximum_bitcast_fusion
  8.1 3.4 %collective-permute-start = (bf16[1,256,256]{2,1,0:T(8,128)(2,1)S(1)}, bf16[1,256,256]{2,1,0:T(8,128)(2,1)S(1)}, u32[]{:S(2)}, u32[]{:S(2)}) collective-permute-start(bf16[1,256,256]{2,1,0:T(8,128)(2,1)S(1)} %maximum_bitcast_fusion), channel_id=1, source_target_pairs={{0,1},{1,2},{2,3},{3,4},{4,5},{5,6},{6,7},{7,8},{8,9},{9,10},{10,1... | collective-permute-start | bytes 393224 | tf_op jit(solution)/shard_map/ppermute | solution.py:15
  11.5 0.0 all-gather.2.cloned.1.call-update
  11.5 0.0 reduce-scatter.2.cloned.1.call-start
  11.6 0.7 copy.43
  12.3 0.1 reduce.1
  12.5 0.7 sub.31
  13.1 0.3 collective-permute-done
  13.4 5.1 %collective-permute-start.1 = (bf16[2,256,256]{2,1,0:T(8,128)(2,1)S(1)}, bf16[2,256,256]{2,1,0:T(8,128)(2,1)S(1)}, u32[]{:S(2)}, u32[]{:S(2)}) collective-permute-start(bf16[2,256,256]{2,1,0:T(8,128)(2,1)S(1)} %pad_maximum_fusion.3), channel_id=1, source_target_pairs={{0,2},{1,3},{2,4},{3,5},{4,6},{5,7},{6,8},{7,9},{8,10},{9,11},{10,... | collective-permute-start | bytes 786440 | tf_op jit(solution)/shard_map/ppermute | solution.py:15
  18.6 0.1 add_bitcast_fusion
  18.7 1.1 copy.76
  19.8 4.7 %collective-permute-done.1 = bf16[2,256,256]{2,1,0:T(8,128)(2,1)S(1)} collective-permute-done((bf16[2,256,256]{2,1,0:T(8,128)(2,1)S(1)}, bf16[2,256,256]{2,1,0:T(8,128)(2,1)S(1)}, u32[]{:S(2)}, u32[]{:S(2)}) %collective-permute-start.1) | collective-permute-done | bytes 262176 | tf_op jit(solution)/shard_map/ppermute | solution.py:15
  24.5 0.1 pad_maximum_fusion.2
  24.5 4.8 %collective-permute-start.2 = (bf16[4,256,256]{2,1,0:T(8,128)(2,1)S(1)}, bf16[4,256,256]{2,1,0:T(8,128)(2,1)S(1)}, u32[]{:S(2)}, u32[]{:S(2)}) collective-permute-start(bf16[4,256,256]{2,1,0:T(8,128)(2,1)S(1)} %pad_maximum_fusion.2), channel_id=1, source_target_pairs={{0,4},{1,5},{2,6},{3,7},{4,8},{5,9},{6,10},{7,11},{8,12},{9,13},{1... | collective-permute-start | bytes 1572872 | tf_op jit(solution)/shard_map/ppermute | solution.py:15
  29.4 0.1 select_reduce_fusion
  29.5 0.6 compare_and_fusion
  30.1 11.3 %collective-permute-done.2 = bf16[4,256,256]{2,1,0:T(8,128)(2,1)S(1)} collective-permute-done((bf16[4,256,256]{2,1,0:T(8,128)(2,1)S(1)}, bf16[4,256,256]{2,1,0:T(8,128)(2,1)S(1)}, u32[]{:S(2)}, u32[]{:S(2)}) %collective-permute-start.2) | collective-permute-done | bytes 524320 | tf_op jit(solution)/shard_map/ppermute | solution.py:15
  41.4 0.1 pad_maximum_fusion.1
  41.5 0.3 fusion.16
  41.8 0.0 copy-start.3
  41.8 4.8 %fusion.18 = (f32[4,256]{1,0:T(4,128)S(1)}, f32[4,256,2048]{1,2,0:T(8,128)}) fusion(pred[256,2048]{0,1:T(8,128)(4,1)S(1)} %compare_and_fusion, bf16[2048,128,1]{1,0,2:T(8,128)(2,1)S(1)} %bitcast.72, bf16[256,4,128]{0,2,1:T(8,128)(2,1)S(1)} %bitcast.76), kind=kOutput, calls=%fused_computation.46 | convolution fusion | flops 545261568 | bytes 9703424 | tf_op jit(solution)/shard_map/sub | solution.py:49
  46.6 0.0 copy-done.3
  46.6 4.1 %fusion.6 = bf16[4,256,2048]{1,2,0:T(8,128)(2,1)S(1)} fusion(f32[4,256,2048]{1,2,0:T(8,128)} %get-tuple-element.23, f32[4,256]{1,0:T(4,128)S(1)} %get-tuple-element.22), kind=kLoop, calls=%fused_computation.11 | loop fusion | flops 4194304 | bytes 12587008 | tf_op jit(solution)/shard_map/convert_element_type | solution.py:51
  50.8 0.0 copy-start
  50.8 2.0 %copy-done = bf16[4,256,2048]{1,2,0:T(8,128)(2,1)} copy-done((bf16[4,256,2048]{1,2,0:T(8,128)(2,1)}, bf16[4,256,2048]{1,2,0:T(8,128)(2,1)S(1)}, u32[]{:S(2)}) %copy-start) | copy-done | bytes 4194328
  52.7 0.8 bitcast_convert_fusion
  53.5 0.2 copy.66
  53.7 5.3 %fusion.2 = bf16[4096,256]{1,0:T(8,128)(2,1)} fusion(bf16[256,512]{0,1:T(8,128)(2,1)S(1)} %bitcast.79, bf16[512,4096]{1,0:T(8,128)(2,1)} %param.9), kind=kOutput, calls=%fused_computation.6 | convolution fusion | flops 1074790400 | bytes 6553600 | tf_op jit(solution)/shard_map/dot_general | solution.py:56
  59.0 0.0 reduce-scatter.2.cloned.1.call-update
  59.0 0.0 all-gather.2.cloned.1.call-done
  59.1 4.1 %fusion.7 = bf16[512,256]{0,1:T(8,128)(2,1)S(1)} fusion(bf16[4096,256]{1,0:T(8,128)(2,1)} %all-gather.2.cloned.1.call-done, bf16[512,4096]{1,0:T(8,128)(2,1)} %param.9), kind=kOutput, calls=%fused_computation.20 | convolution fusion | flops 1073872896 | bytes 6553600 | tf_op jit(solution)/shard_map/dot_general | solution.py:65
  63.2 0.1 reshape.144
  63.3 0.2 copy.54
  63.4 0.4 multiply_reduce_fusion
  63.8 0.1 copy.67
  63.9 3.7 %convolution_bitcast_fusion = f32[2048,128]{0,1:T(8,128)S(1)} fusion(bf16[4,256,2048]{1,2,0:T(8,128)(2,1)} %copy-done, bf16[4,128,256]{2,1,0:T(8,128)(2,1)S(1)} %copy.54), kind=kOutput, calls=%fused_computation.12 | convolution fusion | flops 536870912 | bytes 5505024 | tf_op jit(solution)/shard_map/gtk,gdt->kd/dot_general | solution.py:84
  67.5 4.3 %multiply_convert_fusion = bf16[4,256,2048]{1,2,0:T(8,128)(2,1)S(1)} fusion(bf16[2048,128,1]{1,0,2:T(8,128)(2,1)S(1)} %bitcast.75, bf16[4,128,256]{2,1,0:T(8,128)(2,1)S(1)} %copy.54, f32[4,256]{1,0:T(4,128)S(1)} %copy.67, f32[4,256,2048]{1,2,0:T(8,128)} %get-tuple-element.23, f32[4,256]{1,0:T(4,128)S(1)} %get-tuple-element.22), kind=kOutput, calls=%fused_computation.2 | convolution fusion | flops 547356672 | bytes 13377536 | tf_op jit(solution)/shard_map/gdt,kd->gtk/dot_general | solution.py:74
  71.9 0.0 copy-start.1
  71.9 1.9 %copy-done.1 = bf16[4,256,2048]{1,2,0:T(8,128)(2,1)} copy-done((bf16[4,256,2048]{1,2,0:T(8,128)(2,1)}, bf16[4,256,2048]{1,2,0:T(8,128)(2,1)S(1)}, u32[]{:S(2)}) %copy-start.1) | copy-done | bytes 4194328
  73.8 1.5 %convolution_bitcast_fusion.1 = f32[2048,128]{0,1:T(8,128)S(1)} fusion(bf16[4,256,2048]{1,2,0:T(8,128)(2,1)S(1)} %multiply_convert_fusion, bf16[256,4,128]{0,2,1:T(8,128)(2,1)S(1)} %bitcast.77), kind=kOutput, calls=%fused_computation.13 | convolution fusion | flops 536870912 | bytes 5505024 | tf_op jit(solution)/shard_map/gtk,tgd->kd/dot_general | solution.py:83
  75.3 0.1 fusion.9
  75.4 1.0 copy.75
  76.4 1.9 %collective-permute-start.3 = (bf16[4,256,256]{2,1,0:T(8,128)(2,1)}, bf16[4,256,256]{2,1,0:T(8,128)(2,1)}, u32[]{:S(2)}, u32[]{:S(2)}) collective-permute-start(bf16[4,256,256]{2,1,0:T(8,128)(2,1)} %bitcast.21), channel_id=1, source_target_pairs={{4,0},{5,1},{6,2},{7,3},{8,4},{9,5},{10,6},{11,7},{12,8},{13,9},{1... | collective-permute-start | bytes 1572872 | tf_op jit(solution)/shard_map/ppermute | solution.py:15
  78.4 0.1 fusion.8
  78.5 0.0 copy-start.4
  78.5 0.3 copy.74
  78.8 0.0 copy-start.2
  78.8 15.6 %collective-permute-done.3 = bf16[4,256,256]{2,1,0:T(8,128)(2,1)} collective-permute-done((bf16[4,256,256]{2,1,0:T(8,128)(2,1)}, bf16[4,256,256]{2,1,0:T(8,128)(2,1)}, u32[]{:S(2)}, u32[]{:S(2)}) %collective-permute-start.3) | collective-permute-done | bytes 524320 | tf_op jit(solution)/shard_map/ppermute | solution.py:15
  94.4 1.2 convert_add_fusion
  95.6 1.9 %collective-permute-start.4 = (bf16[2,256,256]{2,1,0:T(8,128)(2,1)S(1)}, bf16[2,256,256]{2,1,0:T(8,128)(2,1)S(1)}, u32[]{:S(2)}, u32[]{:S(2)}) collective-permute-start(bf16[2,256,256]{2,1,0:T(8,128)(2,1)S(1)} %slice.74), channel_id=1, source_target_pairs={{2,0},{3,1},{4,2},{5,3},{6,4},{7,5},{8,6},{9,7},{10,8},{11,9},{12,... | collective-permute-start | bytes 786440 | tf_op jit(solution)/shard_map/ppermute | solution.py:15
  97.6 5.7 %collective-permute-done.4 = bf16[2,256,256]{2,1,0:T(8,128)(2,1)S(1)} collective-permute-done((bf16[2,256,256]{2,1,0:T(8,128)(2,1)S(1)}, bf16[2,256,256]{2,1,0:T(8,128)(2,1)S(1)}, u32[]{:S(2)}, u32[]{:S(2)}) %collective-permute-start.4) | collective-permute-done | bytes 262176 | tf_op jit(solution)/shard_map/ppermute | solution.py:15
  103.2 0.1 slice_add_fusion
  103.3 4.9 %collective-permute-start.5 = (bf16[1,256,256]{2,1,0:T(8,128)(2,1)S(1)}, bf16[1,256,256]{2,1,0:T(8,128)(2,1)S(1)}, u32[]{:S(2)}, u32[]{:S(2)}) collective-permute-start(bf16[1,256,256]{2,1,0:T(8,128)(2,1)S(1)} %slice.75), channel_id=1, source_target_pairs={{1,0},{2,1},{3,2},{4,3},{5,4},{6,5},{7,6},{8,7},{9,8},{10,9},{11,1... | collective-permute-start | bytes 393224 | tf_op jit(solution)/shard_map/ppermute | solution.py:15
  108.2 0.0 copy-done.4
  108.2 0.0 copy-done.2
  108.3 0.8 convolution_convert_fusion.2
  109.0 0.8 copy.57
  109.9 3.9 %collective-permute-done.5 = bf16[1,256,256]{2,1,0:T(8,128)(2,1)S(1)} collective-permute-done((bf16[1,256,256]{2,1,0:T(8,128)(2,1)S(1)}, bf16[1,256,256]{2,1,0:T(8,128)(2,1)S(1)}, u32[]{:S(2)}, u32[]{:S(2)}) %collective-permute-start.5) | collective-permute-done | bytes 131104 | tf_op jit(solution)/shard_map/ppermute | solution.py:15
  113.8 0.7 fusion.17
  114.5 0.0 reduce-scatter.2.cloned.1.call-done
  (8 shorter events, 0.2 us)
Async XLA Ops:
  7.2 51.9 %all-gather.2.cloned.1.call-start = ((), (), s32[]{:S(2)}) async-start(), calls=%async_computation.2 | async-start | bytes 2359296 | tf_op jit(solution)/shard_map/all_gather | solution.py:60
  8.1 5.3 %collective-permute-start = (bf16[1,256,256]{2,1,0:T(8,128)(2,1)S(1)}, bf16[1,256,256]{2,1,0:T(8,128)(2,1)S(1)}, u32[]{:S(2)}, u32[]{:S(2)}) collective-permute-start(bf16[1,256,256]{2,1,0:T(8,128)(2,1)S(1)} %maximum_bitcast_fusion), channel_id=1, source_target_pairs={{0,1},{1,2},{2,3},{3,4},{4,5},{5,6},{6,7},{7,8},{8,9},{9,10},{10,1... | collective-permute-start | bytes 393224 | tf_op jit(solution)/shard_map/ppermute | solution.py:15
  11.5 102.9 %reduce-scatter.2.cloned.1.call-start = ((), (), s32[]{:S(2)}) async-start(), calls=%async_computation.1 | async-start | bytes 2359296 | tf_op jit(solution)/shard_map/reduce_scatter | solution.py:61
  13.4 11.0 %collective-permute-start.1 = (bf16[2,256,256]{2,1,0:T(8,128)(2,1)S(1)}, bf16[2,256,256]{2,1,0:T(8,128)(2,1)S(1)}, u32[]{:S(2)}, u32[]{:S(2)}) collective-permute-start(bf16[2,256,256]{2,1,0:T(8,128)(2,1)S(1)} %pad_maximum_fusion.3), channel_id=1, source_target_pairs={{0,2},{1,3},{2,4},{3,5},{4,6},{5,7},{6,8},{7,9},{8,10},{9,11},{10,... | collective-permute-start | bytes 786440 | tf_op jit(solution)/shard_map/ppermute | solution.py:15
  24.5 16.8 %collective-permute-start.2 = (bf16[4,256,256]{2,1,0:T(8,128)(2,1)S(1)}, bf16[4,256,256]{2,1,0:T(8,128)(2,1)S(1)}, u32[]{:S(2)}, u32[]{:S(2)}) collective-permute-start(bf16[4,256,256]{2,1,0:T(8,128)(2,1)S(1)} %pad_maximum_fusion.2), channel_id=1, source_target_pairs={{0,4},{1,5},{2,6},{3,7},{4,8},{5,9},{6,10},{7,11},{8,12},{9,13},{1... | collective-permute-start | bytes 1572872 | tf_op jit(solution)/shard_map/ppermute | solution.py:15
  41.8 4.8 %copy-start.3 = (bf16[8,256,128]{2,1,0:T(8,128)(2,1)}, bf16[8,256,128]{2,1,0:T(8,128)(2,1)S(1)}, u32[]{:S(2)}) copy-start(bf16[8,256,128]{2,1,0:T(8,128)(2,1)S(1)} %get-tuple-element.18) | copy-start | bytes 1572868
  50.8 2.0 %copy-start = (bf16[4,256,2048]{1,2,0:T(8,128)(2,1)}, bf16[4,256,2048]{1,2,0:T(8,128)(2,1)S(1)}, u32[]{:S(2)}) copy-start(bf16[4,256,2048]{1,2,0:T(8,128)(2,1)S(1)} %fusion.6) | copy-start | bytes 12582916
  71.9 1.9 %copy-start.1 = (bf16[4,256,2048]{1,2,0:T(8,128)(2,1)}, bf16[4,256,2048]{1,2,0:T(8,128)(2,1)S(1)}, u32[]{:S(2)}) copy-start(bf16[4,256,2048]{1,2,0:T(8,128)(2,1)S(1)} %multiply_convert_fusion) | copy-start | bytes 12582916
  76.4 18.0 %collective-permute-start.3 = (bf16[4,256,256]{2,1,0:T(8,128)(2,1)}, bf16[4,256,256]{2,1,0:T(8,128)(2,1)}, u32[]{:S(2)}, u32[]{:S(2)}) collective-permute-start(bf16[4,256,256]{2,1,0:T(8,128)(2,1)} %bitcast.21), channel_id=1, source_target_pairs={{4,0},{5,1},{6,2},{7,3},{8,4},{9,5},{10,6},{11,7},{12,8},{13,9},{1... | collective-permute-start | bytes 1572872 | tf_op jit(solution)/shard_map/ppermute | solution.py:15
  78.5 29.8 %copy-start.4 = (bf16[8,256,128]{2,1,0:T(8,128)(2,1)S(1)}, bf16[8,256,128]{2,1,0:T(8,128)(2,1)}, u32[]{:S(2)}) copy-start(bf16[8,256,128]{2,1,0:T(8,128)(2,1)} %copy-done.3) | copy-start | bytes 1572868
  78.8 29.4 %copy-start.2 = (bf16[4,256,2048]{1,2,0:T(8,128)(2,1)S(1)}, bf16[4,256,2048]{1,2,0:T(8,128)(2,1)}, u32[]{:S(2)}) copy-start(bf16[4,256,2048]{1,2,0:T(8,128)(2,1)} %copy-done.1) | copy-start | bytes 12582916
  95.6 7.6 %collective-permute-start.4 = (bf16[2,256,256]{2,1,0:T(8,128)(2,1)S(1)}, bf16[2,256,256]{2,1,0:T(8,128)(2,1)S(1)}, u32[]{:S(2)}, u32[]{:S(2)}) collective-permute-start(bf16[2,256,256]{2,1,0:T(8,128)(2,1)S(1)} %slice.74), channel_id=1, source_target_pairs={{2,0},{3,1},{4,2},{5,3},{6,4},{7,5},{8,6},{9,7},{10,8},{11,9},{12,... | collective-permute-start | bytes 786440 | tf_op jit(solution)/shard_map/ppermute | solution.py:15
  103.3 10.4 %collective-permute-start.5 = (bf16[1,256,256]{2,1,0:T(8,128)(2,1)S(1)}, bf16[1,256,256]{2,1,0:T(8,128)(2,1)S(1)}, u32[]{:S(2)}, u32[]{:S(2)}) collective-permute-start(bf16[1,256,256]{2,1,0:T(8,128)(2,1)S(1)} %slice.75), channel_id=1, source_target_pairs={{1,0},{2,1},{3,2},{4,3},{5,4},{6,5},{7,6},{8,7},{9,8},{10,9},{11,1... | collective-permute-start | bytes 393224 | tf_op jit(solution)/shard_map/ppermute | solution.py:15
Sparse Core Ops, SparseCore 0:
  11.6 41.8 all-gather.1
  59.2 43.1 reduce-scatter.1

commit v5 on v1

--- a/solution.py
+++ b/solution.py
@@ -3,6 +3,7 @@
 import jax
 import jax.numpy as jnp
 from jax import lax
+from jax.experimental.layout import Layout, with_layout_constraint
 from jax.sharding import PartitionSpec as P
 
 REACH = 7
@@ -27,10 +28,9 @@
         jnp.where(starts[None, :] <= positions[:, None], starts[None, :], 0), axis=1
     )
     stacked = jnp.concatenate([keys, values], axis=1)
-    blocks = [stacked[None]]
-    for offset in range(1, REACH + 1):
-        blocks.append(passed_along(stacked, "ctx", offset)[None])
-    window = jnp.concatenate(blocks, axis=0)
+    window = stacked[None]
+    while window.shape[0] < REACH + 1:
+        window = jnp.concatenate([window, passed_along(window, "ctx", window.shape[0])], axis=0)
     num_blocks = window.shape[0]
     flat_keys = window[:, :, :head_dim].reshape(num_blocks * tok_rows, head_dim)
     flat_values = window[:, :, head_dim:].reshape(num_blocks * tok_rows, head_dim)
@@ -56,6 +56,7 @@
     out_partial = lax.dot_general(
         out_weight, attn, (((0,), (1,)), ((), ())), preferred_element_type=jnp.float32
     ).astype(jnp.bfloat16)
+    out_partial = with_layout_constraint(out_partial, Layout((0, 1)))
     gathered = lax.all_gather(out_grad, "heads", axis=0, tiled=True)
     out_t = lax.psum_scatter(
         out_partial, "heads", scatter_dimension=0, tiled=True

time: 130 us -> 115 us (0.88)
  starting transfers between devices: 44.3 us -> 27 us
  waiting for transfers between devices: 28.1 us -> 32.6 us
  local copies, waits for them, and re-layouts: 12.2 us -> 7.98 us
    ppermute x14 -> x10, starting transfers between devices: 44.2 us -> 26.9 us  [passed_along(): lax.ppermute(value, axis, [(source, source + steps) for source in range(f...]
    ppermute x14 -> x10, waiting for transfers between devices: 10 us -> 24.1 us  [passed_along(): lax.ppermute(value, axis, [(source, source + steps) for source in range(f...]
    all_gather x1, waiting for transfers between devices: 14.3 us -> 2.14 us  [per_device(): gathered = lax.all_gather(out_grad, 'heads', axis=0, tiled=True)]
    unnamed x22 -> x13, local copies, waits for them, and re-layouts: 8.87 us -> 5.51 us
    reduce_scatter x1, waiting for transfers between devices: 3.75 us -> 6.3 us  [per_device(): lax.psum_scatter(out_partial, 'heads', scatter_dimension=0, tiled=True)]
  transfers between devices with their start and end apart: 16 -> 12, of which waited for: 6 -> 9; matrix products, arithmetic and copies ran while one was open for 27% -> 32% of each run, Pallas kernels for 0% -> 0%
where the time goes in v5:
time: 115 us; the launch traced here: 114 us
  waiting for transfers between devices  32.6 us (28%)
  starting transfers between devices  27 us (23%)
  matrix products  23.1 us (20%)
  between operations  14.3 us (12%)
  other arithmetic  8.66 us (8%)
  local copies, waits for them, and re-layouts  7.98 us (7%)
    ppermute x10, starting transfers between devices, passed_along(): lax.ppermute(value, axis, [(source, source + steps) for source in range(f...  26.9 us
    ppermute x10, waiting for transfers between devices, passed_along(): lax.ppermute(value, axis, [(source, source + steps) for source in range(f...  24.1 us
    reduce_scatter x1, waiting for transfers between devices, per_device(): lax.psum_scatter(out_partial, 'heads', scatter_dimension=0, tiled=True)  6.3 us
    unnamed x13, local copies, waits for them, and re-layouts  5.51 us
    sub x1, matrix products, per_device(): expons = jnp.exp(scores - largest)  4.83 us
    dot_general x1, matrix products, per_device(): jnp.einsum('gdt,kd->gtk', grad_heads, flat_values, preferred_element_type...  4.34 us
    convert_element_type x1, other arithmetic, per_device(): probs = weights.astype(jnp.bfloat16)  4.16 us
    dot_general x1, matrix products, per_device(): jnp.dot(out_weight, gathered, preferred_element_type=jnp.float32)  4.12 us
  transfers between devices with their start and end apart: 12, of which 9 were waited for; matrix products, arithmetic and copies ran while one was open for 32% of the time, Pallas kernels for 0%

profile of v5, /device:TPU:6, one launch (start us, length us, event | category | flops | bytes accessed | tf_op | source)
XLA Modules:
  0.0 113.6 jit_solution(13529946403865456196)
XLA Ops:
  7.2 0.0 all-gather.2.cloned.1.call-start
  7.2 0.9 maximum_bitcast_fusion
  8.1 1.9 %collective-permute-start = (bf16[1,256,256]{2,1,0:T(8,128)(2,1)S(1)}, bf16[1,256,256]{2,1,0:T(8,128)(2,1)S(1)}, u32[]{:S(2)}, u32[]{:S(2)}) collective-permute-start(bf16[1,256,256]{2,1,0:T(8,128)(2,1)S(1)} %maximum_bitcast_fusion), channel_id=1, source_target_pairs={{0,1},{1,2},{2,3},{3,4},{4,5},{5,6},{6,7},{7,8},{8,9},{9,10},{10,1... | collective-permute-start | bytes 393224 | tf_op jit(solution)/shard_map/ppermute | solution.py:15
  10.0 0.0 all-gather.2.cloned.1.call-update
  10.1 0.0 reduce-scatter.2.cloned.1.call-start
  10.1 0.7 copy.43
  10.9 0.1 reduce.1
  11.0 0.7 sub.31
  11.7 2.7 %collective-permute-done = bf16[1,256,256]{2,1,0:T(8,128)(2,1)S(1)} collective-permute-done((bf16[1,256,256]{2,1,0:T(8,128)(2,1)S(1)}, bf16[1,256,256]{2,1,0:T(8,128)(2,1)S(1)}, u32[]{:S(2)}, u32[]{:S(2)}) %collective-permute-start) | collective-permute-done | bytes 131104 | tf_op jit(solution)/shard_map/ppermute | solution.py:15
  14.4 6.3 %collective-permute-start.1 = (bf16[2,256,256]{2,1,0:T(8,128)(2,1)S(1)}, bf16[2,256,256]{2,1,0:T(8,128)(2,1)S(1)}, u32[]{:S(2)}, u32[]{:S(2)}) collective-permute-start(bf16[2,256,256]{2,1,0:T(8,128)(2,1)S(1)} %pad_maximum_fusion.3), channel_id=1, source_target_pairs={{0,2},{1,3},{2,4},{3,5},{4,6},{5,7},{6,8},{7,9},{8,10},{9,11},{10,... | collective-permute-start | bytes 786440 | tf_op jit(solution)/shard_map/ppermute | solution.py:15
  20.7 0.1 add_bitcast_fusion
  20.8 1.1 copy.74
  21.9 2.7 %collective-permute-done.1 = bf16[2,256,256]{2,1,0:T(8,128)(2,1)S(1)} collective-permute-done((bf16[2,256,256]{2,1,0:T(8,128)(2,1)S(1)}, bf16[2,256,256]{2,1,0:T(8,128)(2,1)S(1)}, u32[]{:S(2)}, u32[]{:S(2)}) %collective-permute-start.1) | collective-permute-done | bytes 262176 | tf_op jit(solution)/shard_map/ppermute | solution.py:15
  24.6 0.1 pad_maximum_fusion.2
  24.7 4.2 %collective-permute-start.2 = (bf16[4,256,256]{2,1,0:T(8,128)(2,1)S(1)}, bf16[4,256,256]{2,1,0:T(8,128)(2,1)S(1)}, u32[]{:S(2)}, u32[]{:S(2)}) collective-permute-start(bf16[4,256,256]{2,1,0:T(8,128)(2,1)S(1)} %pad_maximum_fusion.2), channel_id=1, source_target_pairs={{0,4},{1,5},{2,6},{3,7},{4,8},{5,9},{6,10},{7,11},{8,12},{9,13},{1... | collective-permute-start | bytes 1572872 | tf_op jit(solution)/shard_map/ppermute | solution.py:15
  28.9 0.1 select_reduce_fusion
  29.0 0.6 compare_and_fusion
  29.5 11.3 %collective-permute-done.2 = bf16[4,256,256]{2,1,0:T(8,128)(2,1)S(1)} collective-permute-done((bf16[4,256,256]{2,1,0:T(8,128)(2,1)S(1)}, bf16[4,256,256]{2,1,0:T(8,128)(2,1)S(1)}, u32[]{:S(2)}, u32[]{:S(2)}) %collective-permute-start.2) | collective-permute-done | bytes 524320 | tf_op jit(solution)/shard_map/ppermute | solution.py:15
  40.9 0.1 pad_maximum_fusion.1
  41.0 0.3 fusion.23
  41.2 4.8 %fusion.25 = (f32[4,256]{1,0:T(4,128)S(1)}, f32[4,256,2048]{1,2,0:T(8,128)}) fusion(pred[256,2048]{0,1:T(8,128)(4,1)S(1)} %compare_and_fusion, bf16[2048,128,1]{1,0,2:T(8,128)(2,1)S(1)} %bitcast.67, bf16[256,4,128]{0,2,1:T(8,128)(2,1)S(1)} %bitcast.71), kind=kOutput, calls=%fused_computation.48 | convolution fusion | flops 545261568 | bytes 9703424 | tf_op jit(solution)/shard_map/sub | solution.py:49
  46.1 4.2 %fusion.6 = bf16[4,256,2048]{1,2,0:T(8,128)(2,1)S(1)} fusion(f32[4,256,2048]{1,2,0:T(8,128)} %get-tuple-element.30, f32[4,256]{1,0:T(4,128)S(1)} %get-tuple-element.29), kind=kLoop, calls=%fused_computation.11 | loop fusion | flops 4194304 | bytes 12587008 | tf_op jit(solution)/shard_map/convert_element_type | solution.py:51
  50.2 0.0 copy-start
  50.2 0.0 copy-start.1
  50.3 2.1 %copy-done = bf16[4,256,2048]{1,2,0:T(8,128)(2,1)} copy-done((bf16[4,256,2048]{1,2,0:T(8,128)(2,1)}, bf16[4,256,2048]{1,2,0:T(8,128)(2,1)S(1)}, u32[]{:S(2)}) %copy-start) | copy-done | bytes 4194328
  52.4 0.8 bitcast_convert_fusion
  53.1 0.8 copy-done.1
  54.0 3.1 %fusion.2 = bf16[4096,256]{1,0:T(8,128)(2,1)} fusion(bf16[256,512]{0,1:T(8,128)(2,1)S(1)} %bitcast.74, bf16[512,4096]{1,0:T(8,128)(2,1)S(1)} %copy-done.1), kind=kOutput, calls=%fused_computation.6 | convolution fusion | flops 1074790400 | bytes 6553600 | tf_op jit(solution)/shard_map/dot_general | solution.py:56
  57.1 0.0 reduce-scatter.2.cloned.1.call-update
  57.1 0.2 copy.66
  57.4 2.1 %all-gather.2.cloned.1.call-done = bf16[4096,256]{1,0:T(8,128)(2,1)} async-done(((bf16[512,256]{1,0:T(8,128)(2,1)}), bf16[4096,256]{1,0:T(8,128)(2,1)}) %all-gather.2.cloned.1.call-update) | async-done | bytes 2097168 | tf_op jit(solution)/shard_map/all_gather | solution.py:60
  59.5 4.1 %fusion.8 = bf16[512,256]{0,1:T(8,128)(2,1)S(1)} fusion(bf16[4096,256]{1,0:T(8,128)(2,1)} %all-gather.2.cloned.1.call-done, bf16[512,4096]{1,0:T(8,128)(2,1)} %param.9), kind=kOutput, calls=%fused_computation.22 | convolution fusion | flops 1073872896 | bytes 6553600 | tf_op jit(solution)/shard_map/dot_general | solution.py:65
  63.6 0.1 reshape.157
  63.7 0.2 copy.54
  63.9 0.4 multiply_reduce_fusion
  64.2 0.1 copy.67
  64.3 3.7 %convolution_bitcast_fusion = f32[2048,128]{0,1:T(8,128)S(1)} fusion(bf16[4,256,2048]{1,2,0:T(8,128)(2,1)} %copy-done, bf16[4,128,256]{2,1,0:T(8,128)(2,1)S(1)} %copy.54), kind=kOutput, calls=%fused_computation.15 | convolution fusion | flops 536870912 | bytes 5505024 | tf_op jit(solution)/shard_map/gtk,gdt->kd/dot_general | solution.py:84
  68.0 4.3 %multiply_convert_fusion = bf16[4,256,2048]{1,2,0:T(8,128)(2,1)S(1)} fusion(bf16[2048,128,1]{1,0,2:T(8,128)(2,1)S(1)} %bitcast.70, bf16[4,128,256]{2,1,0:T(8,128)(2,1)S(1)} %copy.54, f32[4,256]{1,0:T(4,128)S(1)} %copy.67, f32[4,256,2048]{1,2,0:T(8,128)} %get-tuple-element.30, f32[4,256]{1,0:T(4,128)S(1)} %get-tuple-element.29), kind=kOutput, calls=%fused_computation.2 | convolution fusion | flops 547356672 | bytes 13377536 | tf_op jit(solution)/shard_map/gdt,kd->gtk/dot_general | solution.py:74
  72.3 1.5 %convolution_bitcast_fusion.1 = f32[2048,128]{0,1:T(8,128)S(1)} fusion(bf16[4,256,2048]{1,2,0:T(8,128)(2,1)S(1)} %multiply_convert_fusion, bf16[256,4,128]{0,2,1:T(8,128)(2,1)S(1)} %bitcast.72), kind=kOutput, calls=%fused_computation.16 | convolution fusion | flops 536870912 | bytes 5505024 | tf_op jit(solution)/shard_map/gtk,tgd->kd/dot_general | solution.py:83
  73.8 0.1 fusion.7
  74.0 0.1 fusion.22
  74.0 1.9 %collective-permute-start.3 = (bf16[256,256]{0,1:T(8,128)(2,1)S(1)}, bf16[256,256]{0,1:T(8,128)(2,1)S(1)}, u32[]{:S(2)}, u32[]{:S(2)}) collective-permute-start(bf16[256,256]{0,1:T(8,128)(2,1)S(1)} %get-tuple-element.18), channel_id=1, source_target_pairs={{1,0},{2,1},{3,2},{4,3},{5,4},{6,5},{7,6},{8,7},{9,8},{10,9},{11,1... | collective-permute-start | bytes 393224 | tf_op jit(solution)/shard_map/ppermute | solution.py:15
  76.0 2.8 %collective-permute-start.4 = (bf16[256,256]{0,1:T(8,128)(2,1)S(1)}, bf16[256,256]{0,1:T(8,128)(2,1)S(1)}, u32[]{:S(2)}, u32[]{:S(2)}) collective-permute-start(bf16[256,256]{0,1:T(8,128)(2,1)S(1)} %get-tuple-element.24), channel_id=1, source_target_pairs={{2,0},{3,1},{4,2},{5,3},{6,4},{7,5},{8,6},{9,7},{10,8},{11,9},{12,... | collective-permute-start | bytes 393224 | tf_op jit(solution)/shard_map/ppermute | solution.py:15
  78.8 2.6 %collective-permute-start.5 = (bf16[256,256]{0,1:T(8,128)(2,1)S(1)}, bf16[256,256]{0,1:T(8,128)(2,1)}, u32[]{:S(2)}, u32[]{:S(2)}) collective-permute-start(bf16[256,256]{0,1:T(8,128)(2,1)S(1)} %get-tuple-element.23), channel_id=1, source_target_pairs={{3,0},{4,1},{5,2},{6,3},{7,4},{8,5},{9,6},{10,7},{11,8},{12,9},{13... | collective-permute-start | bytes 393224 | tf_op jit(solution)/shard_map/ppermute | solution.py:15
  81.4 1.9 %collective-permute-start.6 = (bf16[256,256]{0,1:T(8,128)(2,1)S(1)}, bf16[256,256]{0,1:T(8,128)(2,1)}, u32[]{:S(2)}, u32[]{:S(2)}) collective-permute-start(bf16[256,256]{0,1:T(8,128)(2,1)S(1)} %get-tuple-element.22), channel_id=1, source_target_pairs={{4,0},{5,1},{6,2},{7,3},{8,4},{9,5},{10,6},{11,7},{12,8},{13,9},{1... | collective-permute-start | bytes 393224 | tf_op jit(solution)/shard_map/ppermute | solution.py:15
  83.4 1.9 %collective-permute-start.7 = (bf16[256,256]{0,1:T(8,128)(2,1)S(1)}, bf16[256,256]{0,1:T(8,128)(2,1)}, u32[]{:S(2)}, u32[]{:S(2)}) collective-permute-start(bf16[256,256]{0,1:T(8,128)(2,1)S(1)} %get-tuple-element.21), channel_id=1, source_target_pairs={{5,0},{6,1},{7,2},{8,3},{9,4},{10,5},{11,6},{12,7},{13,8},{14,9},{... | collective-permute-start | bytes 393224 | tf_op jit(solution)/shard_map/ppermute | solution.py:15
  85.3 0.0 collective-permute-done.3
  85.3 0.0 copy-start.2
  85.3 1.9 %collective-permute-start.8 = (bf16[256,256]{0,1:T(8,128)(2,1)S(1)}, bf16[256,256]{0,1:T(8,128)(2,1)}, u32[]{:S(2)}, u32[]{:S(2)}) collective-permute-start(bf16[256,256]{0,1:T(8,128)(2,1)S(1)} %get-tuple-element.20), channel_id=1, source_target_pairs={{6,0},{7,1},{8,2},{9,3},{10,4},{11,5},{12,6},{13,7},{14,8},{15,9},... | collective-permute-start | bytes 393224 | tf_op jit(solution)/shard_map/ppermute | solution.py:15
  87.2 0.0 collective-permute-done.4
  87.3 1.3 %collective-permute-start.9 = (bf16[256,256]{0,1:T(8,128)(2,1)S(1)}, bf16[256,256]{0,1:T(8,128)(2,1)}, u32[]{:S(2)}, u32[]{:S(2)}) collective-permute-start(bf16[256,256]{0,1:T(8,128)(2,1)S(1)} %get-tuple-element.19), channel_id=1, source_target_pairs={{7,0},{8,1},{9,2},{10,3},{11,4},{12,5},{13,6},{14,7},{15,8},{16,9}... | collective-permute-start | bytes 393224 | tf_op jit(solution)/shard_map/ppermute | solution.py:15
  88.6 0.8 convolution_convert_fusion.2
  89.3 0.0 copy-done.2
  89.3 0.0 copy-done.3
  89.4 0.8 copy.55
  90.2 0.0 collective-permute-done.5
  90.2 2.4 %collective-permute-done.6 = bf16[256,256]{0,1:T(8,128)(2,1)} collective-permute-done((bf16[256,256]{0,1:T(8,128)(2,1)S(1)}, bf16[256,256]{0,1:T(8,128)(2,1)}, u32[]{:S(2)}, u32[]{:S(2)}) %collective-permute-start.6) | collective-permute-done | bytes 131104 | tf_op jit(solution)/shard_map/ppermute | solution.py:15
  92.6 1.1 collective-permute-done.7
  93.8 1.7 %collective-permute-done.8 = bf16[256,256]{0,1:T(8,128)(2,1)} collective-permute-done((bf16[256,256]{0,1:T(8,128)(2,1)S(1)}, bf16[256,256]{0,1:T(8,128)(2,1)}, u32[]{:S(2)}, u32[]{:S(2)}) %collective-permute-start.8) | collective-permute-done | bytes 131104 | tf_op jit(solution)/shard_map/ppermute | solution.py:15
  95.4 2.2 %collective-permute-done.9 = bf16[256,256]{0,1:T(8,128)(2,1)} collective-permute-done((bf16[256,256]{0,1:T(8,128)(2,1)S(1)}, bf16[256,256]{0,1:T(8,128)(2,1)}, u32[]{:S(2)}, u32[]{:S(2)}) %collective-permute-start.9) | collective-permute-done | bytes 131104 | tf_op jit(solution)/shard_map/ppermute | solution.py:15
  97.6 1.4 %fusion.19 = bf16[256,256]{0,1:T(8,128)(2,1)S(1)} fusion(bf16[256,256]{0,1:T(8,128)(2,1)} %collective-permute-done.9, bf16[256,256]{0,1:T(8,128)(2,1)} %collective-permute-done.8, bf16[256,256]{0,1:T(8,128)(2,1)} %collective-permute-done.7, bf16[256,256]{0,1:T(8,128)(2,1)} %collective-permute-done.6, bf16[256,256]{0,1:T(8,128)(2,1)} %collective-permute-done.5, ...), kind=kLoop, calls=%fused_computation.37 | loop fusion | flops 1048576 | bytes 3145728 | tf_op jit(solution)/shard_map/convert.1
  99.0 0.7 copy.56
  99.7 0.7 copy.57
  100.5 6.3 %reduce-scatter.2.cloned.1.call-done = bf16[512,256]{1,0:T(8,128)(2,1)} async-done(((bf16[4096,256]{1,0:T(8,128)(2,1)}), bf16[512,256]{1,0:T(8,128)(2,1)}) %reduce-scatter.2.cloned.1.call-update) | async-done | bytes 262160 | tf_op jit(solution)/shard_map/reduce_scatter | solution.py:61
  (7 shorter events, 0.1 us)
Async XLA Ops:
  7.2 52.3 %all-gather.2.cloned.1.call-start = ((), (), s32[]{:S(2)}) async-start(), calls=%async_computation.2 | async-start | bytes 2359296 | tf_op jit(solution)/shard_map/all_gather | solution.py:60
  8.1 6.3 %collective-permute-start = (bf16[1,256,256]{2,1,0:T(8,128)(2,1)S(1)}, bf16[1,256,256]{2,1,0:T(8,128)(2,1)S(1)}, u32[]{:S(2)}, u32[]{:S(2)}) collective-permute-start(bf16[1,256,256]{2,1,0:T(8,128)(2,1)S(1)} %maximum_bitcast_fusion), channel_id=1, source_target_pairs={{0,1},{1,2},{2,3},{3,4},{4,5},{5,6},{6,7},{7,8},{8,9},{9,10},{10,1... | collective-permute-start | bytes 393224 | tf_op jit(solution)/shard_map/ppermute | solution.py:15
  10.1 96.7 %reduce-scatter.2.cloned.1.call-start = ((), (), s32[]{:S(2)}) async-start(), calls=%async_computation.1 | async-start | bytes 2359296 | tf_op jit(solution)/shard_map/reduce_scatter | solution.py:61
  14.4 10.2 %collective-permute-start.1 = (bf16[2,256,256]{2,1,0:T(8,128)(2,1)S(1)}, bf16[2,256,256]{2,1,0:T(8,128)(2,1)S(1)}, u32[]{:S(2)}, u32[]{:S(2)}) collective-permute-start(bf16[2,256,256]{2,1,0:T(8,128)(2,1)S(1)} %pad_maximum_fusion.3), channel_id=1, source_target_pairs={{0,2},{1,3},{2,4},{3,5},{4,6},{5,7},{6,8},{7,9},{8,10},{9,11},{10,... | collective-permute-start | bytes 786440 | tf_op jit(solution)/shard_map/ppermute | solution.py:15
  24.7 16.2 %collective-permute-start.2 = (bf16[4,256,256]{2,1,0:T(8,128)(2,1)S(1)}, bf16[4,256,256]{2,1,0:T(8,128)(2,1)S(1)}, u32[]{:S(2)}, u32[]{:S(2)}) collective-permute-start(bf16[4,256,256]{2,1,0:T(8,128)(2,1)S(1)} %pad_maximum_fusion.2), channel_id=1, source_target_pairs={{0,4},{1,5},{2,6},{3,7},{4,8},{5,9},{6,10},{7,11},{8,12},{9,13},{1... | collective-permute-start | bytes 1572872 | tf_op jit(solution)/shard_map/ppermute | solution.py:15
  50.2 2.1 %copy-start = (bf16[4,256,2048]{1,2,0:T(8,128)(2,1)}, bf16[4,256,2048]{1,2,0:T(8,128)(2,1)S(1)}, u32[]{:S(2)}) copy-start(bf16[4,256,2048]{1,2,0:T(8,128)(2,1)S(1)} %fusion.6) | copy-start | bytes 12582916
  50.2 3.7 %copy-start.1 = (bf16[512,4096]{1,0:T(8,128)(2,1)S(1)}, bf16[512,4096]{1,0:T(8,128)(2,1)}, u32[]{:S(2)}) copy-start(bf16[512,4096]{1,0:T(8,128)(2,1)} %param.9) | copy-start | bytes 12582916
  74.0 11.3 %collective-permute-start.3 = (bf16[256,256]{0,1:T(8,128)(2,1)S(1)}, bf16[256,256]{0,1:T(8,128)(2,1)S(1)}, u32[]{:S(2)}, u32[]{:S(2)}) collective-permute-start(bf16[256,256]{0,1:T(8,128)(2,1)S(1)} %get-tuple-element.18), channel_id=1, source_target_pairs={{1,0},{2,1},{3,2},{4,3},{5,4},{6,5},{7,6},{8,7},{9,8},{10,9},{11,1... | collective-permute-start | bytes 393224 | tf_op jit(solution)/shard_map/ppermute | solution.py:15
  76.0 11.3 %collective-permute-start.4 = (bf16[256,256]{0,1:T(8,128)(2,1)S(1)}, bf16[256,256]{0,1:T(8,128)(2,1)S(1)}, u32[]{:S(2)}, u32[]{:S(2)}) collective-permute-start(bf16[256,256]{0,1:T(8,128)(2,1)S(1)} %get-tuple-element.24), channel_id=1, source_target_pairs={{2,0},{3,1},{4,2},{5,3},{6,4},{7,5},{8,6},{9,7},{10,8},{11,9},{12,... | collective-permute-start | bytes 393224 | tf_op jit(solution)/shard_map/ppermute | solution.py:15
  78.8 11.4 %collective-permute-start.5 = (bf16[256,256]{0,1:T(8,128)(2,1)S(1)}, bf16[256,256]{0,1:T(8,128)(2,1)}, u32[]{:S(2)}, u32[]{:S(2)}) collective-permute-start(bf16[256,256]{0,1:T(8,128)(2,1)S(1)} %get-tuple-element.23), channel_id=1, source_target_pairs={{3,0},{4,1},{5,2},{6,3},{7,4},{8,5},{9,6},{10,7},{11,8},{12,9},{13... | collective-permute-start | bytes 393224 | tf_op jit(solution)/shard_map/ppermute | solution.py:15
  81.4 11.2 %collective-permute-start.6 = (bf16[256,256]{0,1:T(8,128)(2,1)S(1)}, bf16[256,256]{0,1:T(8,128)(2,1)}, u32[]{:S(2)}, u32[]{:S(2)}) collective-permute-start(bf16[256,256]{0,1:T(8,128)(2,1)S(1)} %get-tuple-element.22), channel_id=1, source_target_pairs={{4,0},{5,1},{6,2},{7,3},{8,4},{9,5},{10,6},{11,7},{12,8},{13,9},{1... | collective-permute-start | bytes 393224 | tf_op jit(solution)/shard_map/ppermute | solution.py:15
  83.4 10.4 %collective-permute-start.7 = (bf16[256,256]{0,1:T(8,128)(2,1)S(1)}, bf16[256,256]{0,1:T(8,128)(2,1)}, u32[]{:S(2)}, u32[]{:S(2)}) collective-permute-start(bf16[256,256]{0,1:T(8,128)(2,1)S(1)} %get-tuple-element.21), channel_id=1, source_target_pairs={{5,0},{6,1},{7,2},{8,3},{9,4},{10,5},{11,6},{12,7},{13,8},{14,9},{... | collective-permute-start | bytes 393224 | tf_op jit(solution)/shard_map/ppermute | solution.py:15
  85.3 4.0 %copy-start.2 = (bf16[256,256]{0,1:T(8,128)(2,1)}, bf16[256,256]{0,1:T(8,128)(2,1)S(1)}, u32[]{:S(2)}) copy-start(bf16[256,256]{0,1:T(8,128)(2,1)S(1)} %collective-permute-done.3) | copy-start | bytes 393220
  85.3 10.1 %collective-permute-start.8 = (bf16[256,256]{0,1:T(8,128)(2,1)S(1)}, bf16[256,256]{0,1:T(8,128)(2,1)}, u32[]{:S(2)}, u32[]{:S(2)}) collective-permute-start(bf16[256,256]{0,1:T(8,128)(2,1)S(1)} %get-tuple-element.20), channel_id=1, source_target_pairs={{6,0},{7,1},{8,2},{9,3},{10,4},{11,5},{12,6},{13,7},{14,8},{15,9},... | collective-permute-start | bytes 393224 | tf_op jit(solution)/shard_map/ppermute | solution.py:15
  87.3 2.1 %copy-start.3 = (bf16[256,256]{0,1:T(8,128)(2,1)}, bf16[256,256]{0,1:T(8,128)(2,1)S(1)}, u32[]{:S(2)}) copy-start(bf16[256,256]{0,1:T(8,128)(2,1)S(1)} %collective-permute-done.4) | copy-start | bytes 393220
  87.3 10.3 %collective-permute-start.9 = (bf16[256,256]{0,1:T(8,128)(2,1)S(1)}, bf16[256,256]{0,1:T(8,128)(2,1)}, u32[]{:S(2)}, u32[]{:S(2)}) collective-permute-start(bf16[256,256]{0,1:T(8,128)(2,1)S(1)} %get-tuple-element.19), channel_id=1, source_target_pairs={{7,0},{8,1},{9,2},{10,3},{11,4},{12,5},{13,6},{14,7},{15,8},{16,9}... | collective-permute-start | bytes 393224 | tf_op jit(solution)/shard_map/ppermute | solution.py:15
Sparse Core Ops, SparseCore 0:
  10.2 49.2 all-gather.1
  62.9 43.7 reduce-scatter.1

commit v6 on v5

--- a/solution.py
+++ b/solution.py
@@ -29,11 +29,15 @@
     )
     stacked = jnp.concatenate([keys, values], axis=1)
     window = stacked[None]
-    while window.shape[0] < REACH + 1:
+    while 2 * window.shape[0] < REACH + 1:
         window = jnp.concatenate([window, passed_along(window, "ctx", window.shape[0])], axis=0)
-    num_blocks = window.shape[0]
-    flat_keys = window[:, :, :head_dim].reshape(num_blocks * tok_rows, head_dim)
-    flat_values = window[:, :, head_dim:].reshape(num_blocks * tok_rows, head_dim)
+    reach = window.shape[0]
+    key_window = window[:, :, :head_dim]
+    value_window = window[:, :, head_dim:]
+    key_window = jnp.concatenate([key_window, passed_along(key_window, "ctx", reach)], axis=0)
+    value_sent = passed_along(value_window, "ctx", reach)
+    num_blocks = key_window.shape[0]
+    flat_keys = key_window.reshape(num_blocks * tok_rows, head_dim)
     key_pos = (
         (shard - jnp.arange(num_blocks, dtype=jnp.int32))[:, None] * tok_rows
         + jnp.arange(tok_rows, dtype=jnp.int32)[None, :]
@@ -48,6 +52,9 @@
     largest = jnp.max(scores, axis=-1, keepdims=True)
     expons = jnp.exp(scores - largest)
     weights = expons / jnp.sum(expons, axis=-1, keepdims=True)
+    value_sent, weights = lax.optimization_barrier((value_sent, weights))
+    value_window = jnp.concatenate([value_window, value_sent], axis=0)
+    flat_values = value_window.reshape(num_blocks * tok_rows, head_dim)
     probs = weights.astype(jnp.bfloat16)
     attn_heads = jnp.einsum(
         "gtk,kd->tgd", probs, flat_values, preferred_element_type=jnp.float32

time: 115 us -> 113 us (0.983)
  matrix products: 23.1 us -> 30.2 us
  waiting for transfers between devices: 32.6 us -> 26.6 us
  other arithmetic: 8.66 us -> 4.51 us
  starting transfers between devices: 27 us -> 30.7 us
  local copies, waits for them, and re-layouts: 7.98 us -> 5.78 us
    ppermute x10 -> x11, waiting for transfers between devices: 24.1 us -> 15.7 us  [passed_along(): lax.ppermute(value, axis, [(source, source + steps) for source in range(f...]
    div x0 -> x1, matrix products: none -> 6.81 us  [per_device(): weights = expons / jnp.sum(expons, axis=-1, keepdims=True)]
    sub x1 -> x0, matrix products: 4.83 us -> none  [per_device(): expons = jnp.exp(scores - largest)]
    convert_element_type x1 -> x0, other arithmetic: 4.16 us -> none  [per_device(): probs = weights.astype(jnp.bfloat16)]
    ppermute x10 -> x11, starting transfers between devices: 26.9 us -> 30.7 us  [passed_along(): lax.ppermute(value, axis, [(source, source + steps) for source in range(f...]
    dot_general x1, matrix products: 0.76 us -> 4.34 us  [per_device(): jnp.einsum('gtk,kd->tgd', probs, flat_values, preferred_element_type=jnp....]
    all_gather x1, waiting for transfers between devices: 2.14 us -> 5.27 us  [per_device(): gathered = lax.all_gather(out_grad, 'heads', axis=0, tiled=True)]
    unnamed x13 -> x11, local copies, waits for them, and re-layouts: 5.51 us -> 3.49 us
  transfers between devices with their start and end apart: 12 -> 13, of which waited for: 9 -> 8; matrix products, arithmetic and copies ran while one was open for 32% -> 35% of each run, Pallas kernels for 0% -> 0%
where the time goes in v6:
time: 113 us; the launch traced here: 112 us
  starting transfers between devices  30.7 us (27%)
  matrix products  30.2 us (27%)
  waiting for transfers between devices  26.6 us (24%)
  between operations  14.3 us (13%)
  local copies, waits for them, and re-layouts  5.78 us (5%)
  other arithmetic  4.51 us (4%)
    ppermute x11, starting transfers between devices, passed_along(): lax.ppermute(value, axis, [(source, source + steps) for source in range(f...  30.7 us
    ppermute x11, waiting for transfers between devices, passed_along(): lax.ppermute(value, axis, [(source, source + steps) for source in range(f...  15.7 us
    div x1, matrix products, per_device(): weights = expons / jnp.sum(expons, axis=-1, keepdims=True)  6.81 us
    all_gather x1, waiting for transfers between devices, per_device(): gathered = lax.all_gather(out_grad, 'heads', axis=0, tiled=True)  5.27 us
    reduce_scatter x1, waiting for transfers between devices, per_device(): lax.psum_scatter(out_partial, 'heads', scatter_dimension=0, tiled=True)  5 us
    dot_general x1, matrix products, per_device(): jnp.einsum('gtk,gdt->kd', probs, grad_heads, preferred_element_type=jnp.f...  4.87 us
    dot_general x1, matrix products, per_device(): jnp.einsum('gdt,kd->gtk', grad_heads, flat_values, preferred_element_type...  4.63 us
    dot_general x1, matrix products, per_device(): jnp.einsum('gtk,kd->tgd', probs, flat_values, preferred_element_type=jnp....  4.34 us
  transfers between devices with their start and end apart: 13, of which 8 were waited for; matrix products, arithmetic and copies ran while one was open for 35% of the time, Pallas kernels for 0%

profile of v6, /device:TPU:6, one launch (start us, length us, event | category | flops | bytes accessed | tf_op | source)
XLA Modules:
  0.0 112.1 jit_solution(12459241120246296329)
XLA Ops:
  7.2 0.0 all-gather.2.cloned.1.call-start
  7.2 0.7 all-gather.2.cloned.1.call-update
  7.9 0.0 reduce-scatter.2.cloned.1.call-start
  7.9 0.9 maximum_bitcast_fusion
  8.8 1.9 %collective-permute-start = (bf16[1,256,256]{2,1,0:T(8,128)(2,1)S(1)}, bf16[1,256,256]{2,1,0:T(8,128)(2,1)S(1)}, u32[]{:S(2)}, u32[]{:S(2)}) collective-permute-start(bf16[1,256,256]{2,1,0:T(8,128)(2,1)S(1)} %maximum_bitcast_fusion), channel_id=1, source_target_pairs={{0,1},{1,2},{2,3},{3,4},{4,5},{5,6},{6,7},{7,8},{8,9},{9,10},{10,1... | collective-permute-start | bytes 393224 | tf_op jit(solution)/shard_map/ppermute | solution.py:15
  10.8 4.3 %collective-permute-done = bf16[1,256,256]{2,1,0:T(8,128)(2,1)S(1)} collective-permute-done((bf16[1,256,256]{2,1,0:T(8,128)(2,1)S(1)}, bf16[1,256,256]{2,1,0:T(8,128)(2,1)S(1)}, u32[]{:S(2)}, u32[]{:S(2)}) %collective-permute-start) | collective-permute-done | bytes 131104 | tf_op jit(solution)/shard_map/ppermute | solution.py:15
  15.2 6.3 %collective-permute-start.1 = (bf16[2,256,256]{2,1,0:T(8,128)(2,1)S(1)}, bf16[2,256,256]{2,1,0:T(8,128)(2,1)S(1)}, u32[]{:S(2)}, u32[]{:S(2)}) collective-permute-start(bf16[2,256,256]{2,1,0:T(8,128)(2,1)S(1)} %pad_maximum_fusion.4), channel_id=1, source_target_pairs={{0,2},{1,3},{2,4},{3,5},{4,6},{5,7},{6,8},{7,9},{8,10},{9,11},{10,... | collective-permute-start | bytes 786440 | tf_op jit(solution)/shard_map/ppermute | solution.py:15
  21.5 0.1 add_bitcast_fusion
  21.5 0.7 copy.42
  22.3 0.1 reduce.1
  22.4 0.7 sub.31
  23.1 1.1 copy.74
  24.2 0.1 select_reduce_fusion
  24.3 1.1 collective-permute-done.1
  25.3 0.1 pad_maximum_fusion.1
  25.4 0.1 fusion.30
  25.5 4.2 %collective-permute-start.3 = (bf16[4,256,128]{2,1,0:T(8,128)(2,1)S(1)}, bf16[4,256,128]{2,1,0:T(8,128)(2,1)S(1)}, u32[]{:S(2)}, u32[]{:S(2)}) collective-permute-start(bf16[4,256,128]{2,1,0:T(8,128)(2,1)S(1)} %get-tuple-element.29), channel_id=1, source_target_pairs={{0,4},{1,5},{2,6},{3,7},{4,8},{5,9},{6,10},{7,11},{8,12},{9,13},{1... | collective-permute-start | bytes 786440 | tf_op jit(solution)/shard_map/ppermute | solution.py:15
  29.7 0.6 compare_and_fusion
  30.3 4.9 %collective-permute-start.2 = (bf16[4,256,128]{2,1,0:T(8,128)(2,1)S(1)}, bf16[4,256,128]{2,1,0:T(8,128)(2,1)S(1)}, u32[]{:S(2)}, u32[]{:S(2)}) collective-permute-start(bf16[4,256,128]{2,1,0:T(8,128)(2,1)S(1)} %get-tuple-element.30), channel_id=1, source_target_pairs={{0,4},{1,5},{2,6},{3,7},{4,8},{5,9},{6,10},{7,11},{8,12},{9,13},{1... | collective-permute-start | bytes 786440 | tf_op jit(solution)/shard_map/ppermute | solution.py:15
  35.3 2.9 %collective-permute-done.3 = bf16[4,256,128]{2,1,0:T(8,128)(2,1)S(1)} collective-permute-done((bf16[4,256,128]{2,1,0:T(8,128)(2,1)S(1)}, bf16[4,256,128]{2,1,0:T(8,128)(2,1)S(1)}, u32[]{:S(2)}, u32[]{:S(2)}) %collective-permute-start.3) | collective-permute-done | bytes 262176 | tf_op jit(solution)/shard_map/ppermute | solution.py:15
  38.2 6.8 %fusion.7 = f32[4,256,2048]{1,2,0:T(8,128)} fusion(pred[256,2048]{0,1:T(8,128)(4,1)S(1)} %compare_and_fusion, bf16[2048,128,1]{1,0,2:T(8,128)(2,1)S(1)} %bitcast.69, bf16[256,4,128]{0,2,1:T(8,128)(2,1)S(1)} %bitcast.72), kind=kOutput, calls=%fused_computation.11 | convolution fusion | flops 545265664 | bytes 9699328 | tf_op jit(solution)/shard_map/div | solution.py:54
  45.0 0.0 collective-permute-done.2
  45.1 0.0 copy-start
  45.1 4.3 %bitcast_convert_fusion = (f32[4,256,128]{1,2,0:T(8,128)S(1)}, bf16[128,4,256]{2,0,1:T(8,128)(2,1)S(1)}) fusion(bf16[2048,128,1]{1,0,2:T(8,128)(2,1)S(1)} %bitcast.67, f32[4,256,2048]{1,2,0:T(8,128)} %fusion.7), kind=kOutput, calls=%fused_computation.40 | convolution fusion | flops 539230208 | bytes 9699328 | tf_op jit(solution)/shard_map/gtk,kd->tgd/dot_general | solution.py:59
  49.4 0.3 copy-done
  49.7 3.1 %fusion.3 = bf16[4096,256]{1,0:T(8,128)(2,1)} fusion(bf16[256,512]{0,1:T(8,128)(2,1)S(1)} %bitcast.71, bf16[512,4096]{1,0:T(8,128)(2,1)S(1)} %copy-done), kind=kOutput, calls=%fused_computation.7 | convolution fusion | flops 1074790400 | bytes 6553600 | tf_op jit(solution)/shard_map/dot_general | solution.py:63
  52.9 0.0 reduce-scatter.2.cloned.1.call-update
  52.9 0.2 copy.66
  53.1 5.3 %all-gather.2.cloned.1.call-done = bf16[4096,256]{1,0:T(8,128)(2,1)} async-done(((bf16[512,256]{1,0:T(8,128)(2,1)}), bf16[4096,256]{1,0:T(8,128)(2,1)}) %all-gather.2.cloned.1.call-update) | async-done | bytes 2097168 | tf_op jit(solution)/shard_map/all_gather | solution.py:67
  58.4 4.1 %fusion.15 = bf16[512,256]{0,1:T(8,128)(2,1)S(1)} fusion(bf16[4096,256]{1,0:T(8,128)(2,1)} %all-gather.2.cloned.1.call-done, bf16[512,4096]{1,0:T(8,128)(2,1)} %param.9), kind=kOutput, calls=%fused_computation.25 | convolution fusion | flops 1073872896 | bytes 6553600 | tf_op jit(solution)/shard_map/dot_general | solution.py:72
  62.5 0.1 reshape.157
  62.6 0.2 copy.54
  62.8 0.4 multiply_reduce_fusion
  63.2 0.1 copy.67
  63.2 4.6 %multiply_convert_fusion = bf16[4,256,2048]{1,2,0:T(8,128)(2,1)S(1)} fusion(f32[4,256,2048]{1,2,0:T(8,128)} %fusion.7, bf16[2048,128,1]{1,0,2:T(8,128)(2,1)S(1)} %bitcast.68, bf16[4,128,256]{2,1,0:T(8,128)(2,1)S(1)} %copy.54, f32[4,256]{1,0:T(4,128)S(1)} %copy.67), kind=kOutput, calls=%fused_computation.3 | convolution fusion | flops 545259520 | bytes 13373440 | tf_op jit(solution)/shard_map/gdt,kd->gtk/dot_general | solution.py:81
  67.9 1.5 %convolution_bitcast_fusion.1 = f32[2048,128]{0,1:T(8,128)S(1)} fusion(bf16[4,256,2048]{1,2,0:T(8,128)(2,1)S(1)} %multiply_convert_fusion, bf16[256,4,128]{0,2,1:T(8,128)(2,1)S(1)} %bitcast.73), kind=kOutput, calls=%fused_computation.16 | convolution fusion | flops 536870912 | bytes 5505024 | tf_op jit(solution)/shard_map/gtk,tgd->kd/dot_general | solution.py:90
  69.3 4.9 %convolution_bitcast_fusion = f32[2048,128]{0,1:T(8,128)S(1)} fusion(bf16[4,128,256]{2,1,0:T(8,128)(2,1)S(1)} %copy.54, f32[4,256,2048]{1,2,0:T(8,128)} %fusion.7), kind=kOutput, calls=%fused_computation.15 | convolution fusion | flops 538968064 | bytes 9699328 | tf_op jit(solution)/shard_map/gtk,gdt->kd/dot_general | solution.py:91
  74.2 0.1 fusion.8
  74.4 0.1 fusion.29
  74.4 1.3 %collective-permute-start.10 = (bf16[256,256]{0,1:T(8,128)(2,1)S(1)}, bf16[256,256]{0,1:T(8,128)(2,1)S(1)}, u32[]{:S(2)}, u32[]{:S(2)}) collective-permute-start(bf16[256,256]{0,1:T(8,128)(2,1)S(1)} %get-tuple-element.23), channel_id=1, source_target_pairs={{7,0},{8,1},{9,2},{10,3},{11,4},{12,5},{13,6},{14,7},{15,8},{16,9}... | collective-permute-start | bytes 393224 | tf_op jit(solution)/shard_map/ppermute | solution.py:15
  75.7 2.3 %collective-permute-start.9 = (bf16[256,256]{0,1:T(8,128)(2,1)S(1)}, bf16[256,256]{0,1:T(8,128)(2,1)S(1)}, u32[]{:S(2)}, u32[]{:S(2)}) collective-permute-start(bf16[256,256]{0,1:T(8,128)(2,1)S(1)} %get-tuple-element.24), channel_id=1, source_target_pairs={{6,0},{7,1},{8,2},{9,3},{10,4},{11,5},{12,6},{13,7},{14,8},{15,9},... | collective-permute-start | bytes 393224 | tf_op jit(solution)/shard_map/ppermute | solution.py:15
  78.0 1.9 %collective-permute-start.8 = (bf16[256,256]{0,1:T(8,128)(2,1)S(1)}, bf16[256,256]{0,1:T(8,128)(2,1)}, u32[]{:S(2)}, u32[]{:S(2)}) collective-permute-start(bf16[256,256]{0,1:T(8,128)(2,1)S(1)} %get-tuple-element.25), channel_id=1, source_target_pairs={{5,0},{6,1},{7,2},{8,3},{9,4},{10,5},{11,6},{12,7},{13,8},{14,9},{... | collective-permute-start | bytes 393224 | tf_op jit(solution)/shard_map/ppermute | solution.py:15
  80.0 1.9 %collective-permute-start.7 = (bf16[256,256]{0,1:T(8,128)(2,1)S(1)}, bf16[256,256]{0,1:T(8,128)(2,1)}, u32[]{:S(2)}, u32[]{:S(2)}) collective-permute-start(bf16[256,256]{0,1:T(8,128)(2,1)S(1)} %get-tuple-element.26), channel_id=1, source_target_pairs={{4,0},{5,1},{6,2},{7,3},{8,4},{9,5},{10,6},{11,7},{12,8},{13,9},{1... | collective-permute-start | bytes 393224 | tf_op jit(solution)/shard_map/ppermute | solution.py:15
  81.9 1.9 %collective-permute-start.6 = (bf16[256,256]{0,1:T(8,128)(2,1)S(1)}, bf16[256,256]{0,1:T(8,128)(2,1)}, u32[]{:S(2)}, u32[]{:S(2)}) collective-permute-start(bf16[256,256]{0,1:T(8,128)(2,1)S(1)} %get-tuple-element.27), channel_id=1, source_target_pairs={{3,0},{4,1},{5,2},{6,3},{7,4},{8,5},{9,6},{10,7},{11,8},{12,9},{13... | collective-permute-start | bytes 393224 | tf_op jit(solution)/shard_map/ppermute | solution.py:15
  83.8 0.0 collective-permute-done.10
  83.8 0.0 copy-start.1
  83.8 1.9 %collective-permute-start.5 = (bf16[256,256]{0,1:T(8,128)(2,1)S(1)}, bf16[256,256]{0,1:T(8,128)(2,1)}, u32[]{:S(2)}, u32[]{:S(2)}) collective-permute-start(bf16[256,256]{0,1:T(8,128)(2,1)S(1)} %get-tuple-element.28), channel_id=1, source_target_pairs={{2,0},{3,1},{4,2},{5,3},{6,4},{7,5},{8,6},{9,7},{10,8},{11,9},{12,... | collective-permute-start | bytes 393224 | tf_op jit(solution)/shard_map/ppermute | solution.py:15
  85.8 0.0 collective-permute-done.9
  85.8 0.0 copy-start.2
  85.8 0.0 copy-done.1
  85.8 0.6 copy-done.2
  86.4 2.0 %collective-permute-start.4 = (bf16[256,256]{0,1:T(8,128)(2,1)S(1)}, bf16[256,256]{0,1:T(8,128)(2,1)}, u32[]{:S(2)}, u32[]{:S(2)}) collective-permute-start(bf16[256,256]{0,1:T(8,128)(2,1)S(1)} %get-tuple-element.22), channel_id=1, source_target_pairs={{1,0},{2,1},{3,2},{4,3},{5,4},{6,5},{7,6},{8,7},{9,8},{10,9},{11,1... | collective-permute-start | bytes 393224 | tf_op jit(solution)/shard_map/ppermute | solution.py:15
  88.5 0.8 convolution_convert_fusion.2
  89.2 0.8 copy.55
  90.1 0.0 collective-permute-done.8
  90.1 2.2 %collective-permute-done.7 = bf16[256,256]{0,1:T(8,128)(2,1)} collective-permute-done((bf16[256,256]{0,1:T(8,128)(2,1)S(1)}, bf16[256,256]{0,1:T(8,128)(2,1)}, u32[]{:S(2)}, u32[]{:S(2)}) %collective-permute-start.7) | collective-permute-done | bytes 131104 | tf_op jit(solution)/shard_map/ppermute | solution.py:15
  92.2 2.4 %collective-permute-done.6 = bf16[256,256]{0,1:T(8,128)(2,1)} collective-permute-done((bf16[256,256]{0,1:T(8,128)(2,1)S(1)}, bf16[256,256]{0,1:T(8,128)(2,1)}, u32[]{:S(2)}, u32[]{:S(2)}) %collective-permute-start.6) | collective-permute-done | bytes 131104 | tf_op jit(solution)/shard_map/ppermute | solution.py:15
  94.6 2.8 %collective-permute-done.5 = bf16[256,256]{0,1:T(8,128)(2,1)} collective-permute-done((bf16[256,256]{0,1:T(8,128)(2,1)S(1)}, bf16[256,256]{0,1:T(8,128)(2,1)}, u32[]{:S(2)}, u32[]{:S(2)}) %collective-permute-start.5) | collective-permute-done | bytes 131104 | tf_op jit(solution)/shard_map/ppermute | solution.py:15
  97.4 0.0 collective-permute-done.4
  97.4 1.4 %fusion.26 = bf16[256,256]{0,1:T(8,128)(2,1)S(1)} fusion(bf16[256,256]{0,1:T(8,128)(2,1)} %copy-done.1, bf16[256,256]{0,1:T(8,128)(2,1)} %copy-done.2, bf16[256,256]{0,1:T(8,128)(2,1)} %collective-permute-done.8, bf16[256,256]{0,1:T(8,128)(2,1)} %collective-permute-done.7, bf16[256,256]{0,1:T(8,128)(2,1)} %collective-permute-done.6, ...), kind=kLoop, calls=%fused_computation.41 | loop fusion | flops 1048576 | bytes 3145728 | tf_op jit(solution)/shard_map/convert.1
  98.8 0.7 copy.56
  99.6 0.7 copy.57
  100.3 5.0 %reduce-scatter.2.cloned.1.call-done = bf16[512,256]{1,0:T(8,128)(2,1)} async-done(((bf16[4096,256]{1,0:T(8,128)(2,1)}), bf16[512,256]{1,0:T(8,128)(2,1)}) %reduce-scatter.2.cloned.1.call-update) | async-done | bytes 262160 | tf_op jit(solution)/shard_map/reduce_scatter | solution.py:68
  (8 shorter events, 0.2 us)
Async XLA Ops:
  7.2 51.2 %all-gather.2.cloned.1.call-start = ((), (), s32[]{:S(2)}) async-start(), calls=%async_computation.2 | async-start | bytes 2359296 | tf_op jit(solution)/shard_map/all_gather | solution.py:67
  7.9 97.4 %reduce-scatter.2.cloned.1.call-start = ((), (), s32[]{:S(2)}) async-start(), calls=%async_computation.1 | async-start | bytes 2359296 | tf_op jit(solution)/shard_map/reduce_scatter | solution.py:68
  8.8 6.3 %collective-permute-start = (bf16[1,256,256]{2,1,0:T(8,128)(2,1)S(1)}, bf16[1,256,256]{2,1,0:T(8,128)(2,1)S(1)}, u32[]{:S(2)}, u32[]{:S(2)}) collective-permute-start(bf16[1,256,256]{2,1,0:T(8,128)(2,1)S(1)} %maximum_bitcast_fusion), channel_id=1, source_target_pairs={{0,1},{1,2},{2,3},{3,4},{4,5},{5,6},{6,7},{7,8},{8,9},{9,10},{10,1... | collective-permute-start | bytes 393224 | tf_op jit(solution)/shard_map/ppermute | solution.py:15
  15.2 10.2 %collective-permute-start.1 = (bf16[2,256,256]{2,1,0:T(8,128)(2,1)S(1)}, bf16[2,256,256]{2,1,0:T(8,128)(2,1)S(1)}, u32[]{:S(2)}, u32[]{:S(2)}) collective-permute-start(bf16[2,256,256]{2,1,0:T(8,128)(2,1)S(1)} %pad_maximum_fusion.4), channel_id=1, source_target_pairs={{0,2},{1,3},{2,4},{3,5},{4,6},{5,7},{6,8},{7,9},{8,10},{9,11},{10,... | collective-permute-start | bytes 786440 | tf_op jit(solution)/shard_map/ppermute | solution.py:15
  25.5 12.6 %collective-permute-start.3 = (bf16[4,256,128]{2,1,0:T(8,128)(2,1)S(1)}, bf16[4,256,128]{2,1,0:T(8,128)(2,1)S(1)}, u32[]{:S(2)}, u32[]{:S(2)}) collective-permute-start(bf16[4,256,128]{2,1,0:T(8,128)(2,1)S(1)} %get-tuple-element.29), channel_id=1, source_target_pairs={{0,4},{1,5},{2,6},{3,7},{4,8},{5,9},{6,10},{7,11},{8,12},{9,13},{1... | collective-permute-start | bytes 786440 | tf_op jit(solution)/shard_map/ppermute | solution.py:15
  30.3 14.7 %collective-permute-start.2 = (bf16[4,256,128]{2,1,0:T(8,128)(2,1)S(1)}, bf16[4,256,128]{2,1,0:T(8,128)(2,1)S(1)}, u32[]{:S(2)}, u32[]{:S(2)}) collective-permute-start(bf16[4,256,128]{2,1,0:T(8,128)(2,1)S(1)} %get-tuple-element.30), channel_id=1, source_target_pairs={{0,4},{1,5},{2,6},{3,7},{4,8},{5,9},{6,10},{7,11},{8,12},{9,13},{1... | collective-permute-start | bytes 786440 | tf_op jit(solution)/shard_map/ppermute | solution.py:15
  45.1 4.7 %copy-start = (bf16[512,4096]{1,0:T(8,128)(2,1)S(1)}, bf16[512,4096]{1,0:T(8,128)(2,1)}, u32[]{:S(2)}) copy-start(bf16[512,4096]{1,0:T(8,128)(2,1)} %param.9) | copy-start | bytes 12582916
  74.4 9.4 %collective-permute-start.10 = (bf16[256,256]{0,1:T(8,128)(2,1)S(1)}, bf16[256,256]{0,1:T(8,128)(2,1)S(1)}, u32[]{:S(2)}, u32[]{:S(2)}) collective-permute-start(bf16[256,256]{0,1:T(8,128)(2,1)S(1)} %get-tuple-element.23), channel_id=1, source_target_pairs={{7,0},{8,1},{9,2},{10,3},{11,4},{12,5},{13,6},{14,7},{15,8},{16,9}... | collective-permute-start | bytes 393224 | tf_op jit(solution)/shard_map/ppermute | solution.py:15
  75.7 10.0 %collective-permute-start.9 = (bf16[256,256]{0,1:T(8,128)(2,1)S(1)}, bf16[256,256]{0,1:T(8,128)(2,1)S(1)}, u32[]{:S(2)}, u32[]{:S(2)}) collective-permute-start(bf16[256,256]{0,1:T(8,128)(2,1)S(1)} %get-tuple-element.24), channel_id=1, source_target_pairs={{6,0},{7,1},{8,2},{9,3},{10,4},{11,5},{12,6},{13,7},{14,8},{15,9},... | collective-permute-start | bytes 393224 | tf_op jit(solution)/shard_map/ppermute | solution.py:15
  78.0 12.0 %collective-permute-start.8 = (bf16[256,256]{0,1:T(8,128)(2,1)S(1)}, bf16[256,256]{0,1:T(8,128)(2,1)}, u32[]{:S(2)}, u32[]{:S(2)}) collective-permute-start(bf16[256,256]{0,1:T(8,128)(2,1)S(1)} %get-tuple-element.25), channel_id=1, source_target_pairs={{5,0},{6,1},{7,2},{8,3},{9,4},{10,5},{11,6},{12,7},{13,8},{14,9},{... | collective-permute-start | bytes 393224 | tf_op jit(solution)/shard_map/ppermute | solution.py:15
  80.0 12.3 %collective-permute-start.7 = (bf16[256,256]{0,1:T(8,128)(2,1)S(1)}, bf16[256,256]{0,1:T(8,128)(2,1)}, u32[]{:S(2)}, u32[]{:S(2)}) collective-permute-start(bf16[256,256]{0,1:T(8,128)(2,1)S(1)} %get-tuple-element.26), channel_id=1, source_target_pairs={{4,0},{5,1},{6,2},{7,3},{8,4},{9,5},{10,6},{11,7},{12,8},{13,9},{1... | collective-permute-start | bytes 393224 | tf_op jit(solution)/shard_map/ppermute | solution.py:15
  81.9 12.7 %collective-permute-start.6 = (bf16[256,256]{0,1:T(8,128)(2,1)S(1)}, bf16[256,256]{0,1:T(8,128)(2,1)}, u32[]{:S(2)}, u32[]{:S(2)}) collective-permute-start(bf16[256,256]{0,1:T(8,128)(2,1)S(1)} %get-tuple-element.27), channel_id=1, source_target_pairs={{3,0},{4,1},{5,2},{6,3},{7,4},{8,5},{9,6},{10,7},{11,8},{12,9},{13... | collective-permute-start | bytes 393224 | tf_op jit(solution)/shard_map/ppermute | solution.py:15
  83.8 2.0 %copy-start.1 = (bf16[256,256]{0,1:T(8,128)(2,1)}, bf16[256,256]{0,1:T(8,128)(2,1)S(1)}, u32[]{:S(2)}) copy-start(bf16[256,256]{0,1:T(8,128)(2,1)S(1)} %collective-permute-done.10) | copy-start | bytes 393220
  83.8 13.6 %collective-permute-start.5 = (bf16[256,256]{0,1:T(8,128)(2,1)S(1)}, bf16[256,256]{0,1:T(8,128)(2,1)}, u32[]{:S(2)}, u32[]{:S(2)}) collective-permute-start(bf16[256,256]{0,1:T(8,128)(2,1)S(1)} %get-tuple-element.28), channel_id=1, source_target_pairs={{2,0},{3,1},{4,2},{5,3},{6,4},{7,5},{8,6},{9,7},{10,8},{11,9},{12,... | collective-permute-start | bytes 393224 | tf_op jit(solution)/shard_map/ppermute | solution.py:15
  85.8 0.6 copy-start.2
  86.4 11.0 %collective-permute-start.4 = (bf16[256,256]{0,1:T(8,128)(2,1)S(1)}, bf16[256,256]{0,1:T(8,128)(2,1)}, u32[]{:S(2)}, u32[]{:S(2)}) collective-permute-start(bf16[256,256]{0,1:T(8,128)(2,1)S(1)} %get-tuple-element.22), channel_id=1, source_target_pairs={{1,0},{2,1},{3,2},{4,3},{5,4},{6,5},{7,6},{8,7},{9,8},{10,9},{11,1... | collective-permute-start | bytes 393224 | tf_op jit(solution)/shard_map/ppermute | solution.py:15
Sparse Core Ops, SparseCore 0:
  10.1 48.2 all-gather.1
  61.8 43.4 reduce-scatter.1

commit v7 on v6

--- a/solution.py
+++ b/solution.py
@@ -13,6 +13,45 @@
     count = lax.axis_size(axis)
     first, last = (max(0, -steps), min(count, count - steps))
     return lax.ppermute(value, axis, [(source, source + steps) for source in range(first, last)])
+
+
+def ring_shift(value, axis, steps):
+    count = lax.axis_size(axis)
+    return lax.ppermute(value, axis, [(source, (source + steps) % count) for source in range(count)])
+
+
+def weight_columns(out_weight, index, begin, width):
+    block = out_weight.shape[0]
+    return lax.dynamic_slice_in_dim(out_weight, index * block + begin, width, axis=1)
+
+
+def ring_gather_dot(out_weight, out_grad, axis):
+    count = lax.axis_size(axis)
+    me = lax.axis_index(axis)
+    block = out_grad.shape[0]
+    half = block // 2
+
+    def term(index, begin, width, piece):
+        return jnp.dot(
+            weight_columns(out_weight, index % count, begin, width),
+            piece,
+            preferred_element_type=jnp.float32,
+        )
+
+    total = term(me, 0, block, out_grad)
+    ahead, behind = out_grad, out_grad
+    for step in range(1, count // 2 + 1):
+        if step < count - step:
+            ahead = ring_shift(ahead, axis, 1)
+            behind = ring_shift(behind, axis, -1)
+            total = total + term(me - step, 0, block, ahead)
+            total = total + term(me + step, 0, block, behind)
+        else:
+            low = ring_shift(ahead[:half], axis, 1)
+            high = ring_shift(behind[half:], axis, -1)
+            total = total + term(me - step, 0, half, low)
+            total = total + term(me - step, half, half, high)
+    return total
 
 
 def per_device(queries, keys, values, out_weight, out_grad, doc_lengths):
@@ -64,16 +103,10 @@
         out_weight, attn, (((0,), (1,)), ((), ())), preferred_element_type=jnp.float32
     ).astype(jnp.bfloat16)
     out_partial = with_layout_constraint(out_partial, Layout((0, 1)))
-    gathered = lax.all_gather(out_grad, "heads", axis=0, tiled=True)
     out_t = lax.psum_scatter(
         out_partial, "heads", scatter_dimension=0, tiled=True
     )
-    _, gathered = lax.optimization_barrier((out_partial, gathered))
-    grad_attn = jnp.dot(
-        out_weight,
-        gathered,
-        preferred_element_type=jnp.float32,
-    ).astype(jnp.bfloat16)
+    grad_attn = ring_gather_dot(out_weight, out_grad, "heads").astype(jnp.bfloat16)
     grad_heads = grad_attn.reshape(group_size, head_dim, tok_rows)
     delta_sum = jnp.einsum(
         "tgd,gdt->gt", attn_heads, grad_heads, preferred_element_type=jnp.float32

time: 113 us -> 139 us (1.23)
  starting transfers between devices: 30.7 us -> 58.3 us
  waiting for transfers between devices: 26.6 us -> 18.4 us
  matrix products: 30.2 us -> 36.8 us
    ppermute x0 -> x8, starting transfers between devices: none -> 28.8 us  [ring_shift(): lax.ppermute(value, axis, [(source, (source + steps) % count) for source...]
    ppermute x11, waiting for transfers between devices: 15.7 us -> 6.36 us  [passed_along(): lax.ppermute(value, axis, [(source, source + steps) for source in range(f...]
    dot_general x1 -> x9, matrix products: 4.12 us -> 10.9 us  [term(): jnp.dot(weight_columns(out_weight, index % count, begin, width), piece, p...]
    all_gather x1 -> x0, waiting for transfers between devices: 5.27 us -> none  [per_device(): gathered = lax.all_gather(out_grad, 'heads', axis=0, tiled=True)]
    reduce_scatter x1, waiting for transfers between devices: 5 us -> 8.58 us  [per_device(): lax.psum_scatter(out_partial, 'heads', scatter_dimension=0, tiled=True)]
    ppermute x0 -> x8, waiting for transfers between devices: none -> 3.44 us  [ring_shift(): lax.ppermute(value, axis, [(source, (source + steps) % count) for source...]
    unnamed x11 -> x10, local copies, waits for them, and re-layouts: 3.49 us -> 2.97 us
  transfers between devices with their start and end apart: 13 -> 20, of which waited for: 8 -> 5; matrix products, arithmetic and copies ran while one was open for 35% -> 27% of each run, Pallas kernels for 0% -> 0%
where the time goes in v7:
time: 139 us; the launch traced here: 138 us
  starting transfers between devices  58.3 us (42%)
  matrix products  36.8 us (26%)
  waiting for transfers between devices  18.4 us (13%)
  between operations  14.7 us (11%)
  other arithmetic  5.24 us (4%)
  local copies, waits for them, and re-layouts  4.97 us (4%)
    ppermute x11, starting transfers between devices, passed_along(): lax.ppermute(value, axis, [(source, source + steps) for source in range(f...  29.5 us
    ppermute x8, starting transfers between devices, ring_shift(): lax.ppermute(value, axis, [(source, (source + steps) % count) for source...  28.8 us
    dot_general x9, matrix products, term(): jnp.dot(weight_columns(out_weight, index % count, begin, width), piece, p...  10.9 us
    reduce_scatter x1, waiting for transfers between devices, per_device(): lax.psum_scatter(out_partial, 'heads', scatter_dimension=0, tiled=True)  8.58 us
    div x1, matrix products, per_device(): weights = expons / jnp.sum(expons, axis=-1, keepdims=True)  6.83 us
    ppermute x11, waiting for transfers between devices, passed_along(): lax.ppermute(value, axis, [(source, source + steps) for source in range(f...  6.36 us
    dot_general x1, matrix products, per_device(): jnp.einsum('gtk,gdt->kd', probs, grad_heads, preferred_element_type=jnp.f...  4.87 us
    dot_general x1, matrix products, per_device(): jnp.einsum('gdt,kd->gtk', grad_heads, flat_values, preferred_element_type...  4.61 us
  transfers between devices with their start and end apart: 20, of which 5 were waited for; matrix products, arithmetic and copies ran while one was open for 27% of the time, Pallas kernels for 0%

profile of v7, /device:TPU:6, one launch (start us, length us, event | category | flops | bytes accessed | tf_op | source)
XLA Modules:
  0.0 138.4 jit_solution(1126379115423274295)
XLA Ops:
  7.2 0.0 reduce-scatter.2.cloned.1.call-start
  7.2 5.4 %collective-permute-start.5 = (bf16[512,256]{1,0:T(8,128)(2,1)}, bf16[512,256]{1,0:T(8,128)(2,1)S(1)}, u32[]{:S(2)}, u32[]{:S(2)}) collective-permute-start(bf16[512,256]{1,0:T(8,128)(2,1)} %param.10), channel_id=1, source_target_pairs={{0,448},{64,0},{128,64},{192,128},{256,192},{320,256},{384,320},{4... | collective-permute-start | bytes 786440 | tf_op jit(solution)/shard_map/ppermute | solution.py:20
  12.6 1.9 %collective-permute-start.4 = (bf16[512,256]{1,0:T(8,128)(2,1)}, bf16[512,256]{1,0:T(8,128)(2,1)S(1)}, u32[]{:S(2)}, u32[]{:S(2)}) collective-permute-start(bf16[512,256]{1,0:T(8,128)(2,1)} %param.10), channel_id=1, source_target_pairs={{0,64},{64,128},{128,192},{192,256},{256,320},{320,384},{384,448},... | collective-permute-start | bytes 786440 | tf_op jit(solution)/shard_map/ppermute | solution.py:20
  14.5 0.9 maximum_bitcast_fusion
  15.4 1.9 %collective-permute-start = (bf16[1,256,256]{2,1,0:T(8,128)(2,1)S(1)}, bf16[1,256,256]{2,1,0:T(8,128)(2,1)S(1)}, u32[]{:S(2)}, u32[]{:S(2)}) collective-permute-start(bf16[1,256,256]{2,1,0:T(8,128)(2,1)S(1)} %maximum_bitcast_fusion), channel_id=1, source_target_pairs={{0,1},{1,2},{2,3},{3,4},{4,5},{5,6},{6,7},{7,8},{8,9},{9,10},{10,1... | collective-permute-start | bytes 393224 | tf_op jit(solution)/shard_map/ppermute | solution.py:15
  17.5 0.7 copy.40
  18.3 0.1 reduce.1
  18.4 0.7 sub.44
  19.1 0.1 add_bitcast_fusion
  19.1 1.1 copy.72
  20.3 0.1 select_reduce_fusion
  20.4 0.6 compare_and_fusion
  21.0 1.4 %fusion.31 = f32[512,256]{1,0:T(8,128)S(1)} fusion(bf16[512,256]{1,0:T(8,128)(2,1)} %param.10, bf16[512,4096]{1,0:T(8,128)(2,1)} %param.9, s32[]{:T(128)S(6)} %select_n.75), kind=kOutput, calls=%fused_computation.47 | convolution fusion | flops 134217728 | bytes 1310724 | tf_op jit(solution)/shard_map/dot_general | solution.py:35
  22.4 0.0 collective-permute-done
  22.4 5.6 %collective-permute-start.1 = (bf16[2,256,256]{2,1,0:T(8,128)(2,1)S(1)}, bf16[2,256,256]{2,1,0:T(8,128)(2,1)S(1)}, u32[]{:S(2)}, u32[]{:S(2)}) collective-permute-start(bf16[2,256,256]{2,1,0:T(8,128)(2,1)S(1)} %pad_maximum_fusion.4), channel_id=1, source_target_pairs={{0,2},{1,3},{2,4},{3,5},{4,6},{5,7},{6,8},{7,9},{8,10},{9,11},{10,... | collective-permute-start | bytes 786440 | tf_op jit(solution)/shard_map/ppermute | solution.py:15
  28.1 5.1 %collective-permute-start.7 = (bf16[512,256]{1,0:T(8,128)(2,1)S(1)}, bf16[512,256]{1,0:T(8,128)(2,1)}, u32[]{:S(2)}, u32[]{:S(2)}) collective-permute-start(bf16[512,256]{1,0:T(8,128)(2,1)S(1)} %collective-permute-done.5), channel_id=1, source_target_pairs={{0,448},{64,0},{128,64},{192,128},{256,192},{320,256},{384,320},{4... | collective-permute-start | bytes 786440 | tf_op jit(solution)/shard_map/ppermute | solution.py:20
  33.2 0.0 collective-permute-done.4
  33.2 1.9 %collective-permute-start.6 = (bf16[512,256]{1,0:T(8,128)(2,1)S(1)}, bf16[512,256]{1,0:T(8,128)(2,1)}, u32[]{:S(2)}, u32[]{:S(2)}) collective-permute-start(bf16[512,256]{1,0:T(8,128)(2,1)S(1)} %collective-permute-done.4), channel_id=1, source_target_pairs={{0,64},{64,128},{128,192},{192,256},{256,320},{320,384},{384,448},... | collective-permute-start | bytes 786440 | tf_op jit(solution)/shard_map/ppermute | solution.py:20
  35.1 1.3 convolution_add_fusion.3
  36.5 1.3 convolution_add_fusion.2
  37.9 0.1 pad_maximum_fusion.1
  37.9 0.1 fusion.58
  38.0 2.9 %collective-permute-start.2 = (bf16[4,256,128]{2,1,0:T(8,128)(2,1)S(1)}, bf16[4,256,128]{2,1,0:T(8,128)(2,1)}, u32[]{:S(2)}, u32[]{:S(2)}) collective-permute-start(bf16[4,256,128]{2,1,0:T(8,128)(2,1)S(1)} %get-tuple-element.28), channel_id=1, source_target_pairs={{0,4},{1,5},{2,6},{3,7},{4,8},{5,9},{6,10},{7,11},{8,12},{9,13},{1... | collective-permute-start | bytes 786440 | tf_op jit(solution)/shard_map/ppermute | solution.py:15
  40.9 6.3 %collective-permute-start.3 = (bf16[4,256,128]{2,1,0:T(8,128)(2,1)S(1)}, bf16[4,256,128]{2,1,0:T(8,128)(2,1)S(1)}, u32[]{:S(2)}, u32[]{:S(2)}) collective-permute-start(bf16[4,256,128]{2,1,0:T(8,128)(2,1)S(1)} %get-tuple-element.27), channel_id=1, source_target_pairs={{0,4},{1,5},{2,6},{3,7},{4,8},{5,9},{6,10},{7,11},{8,12},{9,13},{1... | collective-permute-start | bytes 786440 | tf_op jit(solution)/shard_map/ppermute | solution.py:15
  47.2 5.1 %collective-permute-start.9 = (bf16[512,256]{1,0:T(8,128)(2,1)}, bf16[512,256]{1,0:T(8,128)(2,1)S(1)}, u32[]{:S(2)}, u32[]{:S(2)}) collective-permute-start(bf16[512,256]{1,0:T(8,128)(2,1)} %collective-permute-done.7), channel_id=1, source_target_pairs={{0,448},{64,0},{128,64},{192,128},{256,192},{320,256},{384,320},{4... | collective-permute-start | bytes 786440 | tf_op jit(solution)/shard_map/ppermute | solution.py:20
  52.3 0.0 collective-permute-done.6
  52.3 1.9 %collective-permute-start.8 = (bf16[512,256]{1,0:T(8,128)(2,1)}, bf16[512,256]{1,0:T(8,128)(2,1)S(1)}, u32[]{:S(2)}, u32[]{:S(2)}) collective-permute-start(bf16[512,256]{1,0:T(8,128)(2,1)} %collective-permute-done.6), channel_id=1, source_target_pairs={{0,64},{64,128},{128,192},{192,256},{256,320},{320,384},{384,448},... | collective-permute-start | bytes 786440 | tf_op jit(solution)/shard_map/ppermute | solution.py:20
  54.3 1.4 %fusion.26 = f32[512,256]{1,0:T(8,128)S(1)} fusion(bf16[512,256]{1,0:T(8,128)(2,1)} %collective-permute-done.7, bf16[512,4096]{1,0:T(8,128)(2,1)} %param.9, s32[]{:T(128)S(6)} %select_n.83), kind=kOutput, calls=%fused_computation.42 | convolution fusion | flops 134217728 | bytes 1310724 | tf_op jit(solution)/shard_map/dot_general | solution.py:35
  55.7 1.4 %fusion.15 = f32[512,256]{1,0:T(8,128)S(1)} fusion(f32[512,256]{1,0:T(8,128)S(1)} %fusion.26, f32[512,256]{1,0:T(8,128)S(1)} %convolution_add_fusion.2, bf16[512,256]{1,0:T(8,128)(2,1)} %collective-permute-done.6, bf16[512,4096]{1,0:T(8,128)(2,1)} %param.9, s32[]{:T(128)S(6)} %select_n.81), kind=kOutput, calls=%fused_computation.27 | convolution fusion | flops 134479872 | bytes 2359300 | tf_op jit(solution)/shard_map/dot_general | solution.py:35
  57.2 6.8 %fusion.7 = f32[4,256,2048]{1,2,0:T(8,128)} fusion(pred[256,2048]{0,1:T(8,128)(4,1)S(1)} %compare_and_fusion, bf16[2048,128,1]{1,0,2:T(8,128)(2,1)S(1)} %bitcast.76, bf16[256,4,128]{0,2,1:T(8,128)(2,1)S(1)} %bitcast.79), kind=kOutput, calls=%fused_computation.11 | convolution fusion | flops 545265664 | bytes 9699328 | tf_op jit(solution)/shard_map/div | solution.py:93
  64.0 0.0 collective-permute-done.2
  64.0 1.1 pad_maximum_fusion.3
  65.2 5.3 %collective-permute-start.11 = (bf16[256,256]{1,0:T(8,128)(2,1)S(1)}, bf16[256,256]{1,0:T(8,128)(2,1)S(1)}, u32[]{:S(2)}, u32[]{:S(2)}) collective-permute-start(bf16[256,256]{1,0:T(8,128)(2,1)S(1)} %slice.76), channel_id=1, source_target_pairs={{0,448},{64,0},{128,64},{192,128},{256,192},{320,256},{384,320},{4... | collective-permute-start | bytes 393224 | tf_op jit(solution)/shard_map/ppermute | solution.py:20
  70.5 2.1 %collective-permute-start.10 = (bf16[256,256]{1,0:T(8,128)(2,1)S(1)}, bf16[256,256]{1,0:T(8,128)(2,1)S(1)}, u32[]{:S(2)}, u32[]{:S(2)}) collective-permute-start(bf16[256,256]{1,0:T(8,128)(2,1)S(1)} %slice.75), channel_id=1, source_target_pairs={{0,64},{64,128},{128,192},{192,256},{256,320},{320,384},{384,448},... | collective-permute-start | bytes 393224 | tf_op jit(solution)/shard_map/ppermute | solution.py:20
  72.6 1.3 fusion.23
  74.0 1.2 fusion.41
  75.1 3.4 %collective-permute-done.10 = bf16[256,256]{1,0:T(8,128)(2,1)S(1)} collective-permute-done((bf16[256,256]{1,0:T(8,128)(2,1)S(1)}, bf16[256,256]{1,0:T(8,128)(2,1)S(1)}, u32[]{:S(2)}, u32[]{:S(2)}) %collective-permute-start.10) | collective-permute-done | bytes 131104 | tf_op jit(solution)/shard_map/ppermute | solution.py:20
  78.6 1.2 fusion.43
  79.8 0.3 fusion.19
  80.1 4.1 %fusion.22 = (f32[4,256]{1,0:T(4,128)S(1)}, bf16[128,4,256]{2,0,1:T(8,128)(2,1)S(1)}) fusion(bf16[512,256]{1,0:T(8,128)(2,1)S(1)} %fusion.19, bf16[2048,128,1]{1,0,2:T(8,128)(2,1)S(1)} %bitcast.72, f32[4,256,2048]{1,2,0:T(8,128)} %fusion.7), kind=kOutput, calls=%fused_computation.38 | convolution fusion | flops 539622400 | bytes 9441280 | tf_op jit(solution)/shard_map/gtk,kd->tgd/dot_general | solution.py:98
  84.2 3.2 %fusion.3 = bf16[4096,256]{1,0:T(8,128)(2,1)} fusion(bf16[256,512]{0,1:T(8,128)(2,1)S(1)} %bitcast.78, bf16[512,4096]{1,0:T(8,128)(2,1)S(1)} %copy-done), kind=kOutput, calls=%fused_computation.7 | convolution fusion | flops 1074790400 | bytes 6553600 | tf_op jit(solution)/shard_map/dot_general | solution.py:102
  87.4 0.0 reduce-scatter.2.cloned.1.call-update
  87.4 4.6 %multiply_convert_fusion = bf16[4,256,2048]{1,2,0:T(8,128)(2,1)S(1)} fusion(f32[4,256,2048]{1,2,0:T(8,128)} %fusion.7, bf16[2048,128,1]{1,0,2:T(8,128)(2,1)S(1)} %bitcast.73, bf16[4,128,256]{2,1,0:T(8,128)(2,1)S(1)} %bitcast.74, f32[4,256]{1,0:T(4,128)S(1)} %get-tuple-element.31), kind=kOutput, calls=%fused_computation.3 | convolution fusion | flops 545259520 | bytes 13373440 | tf_op jit(solution)/shard_map/gdt,kd->gtk/dot_general | solution.py:114
  92.0 1.5 %convolution_bitcast_fusion.1 = f32[2048,128]{0,1:T(8,128)S(1)} fusion(bf16[4,256,2048]{1,2,0:T(8,128)(2,1)S(1)} %multiply_convert_fusion, bf16[256,4,128]{0,2,1:T(8,128)(2,1)S(1)} %bitcast.80), kind=kOutput, calls=%fused_computation.16 | convolution fusion | flops 536870912 | bytes 5505024 | tf_op jit(solution)/shard_map/gtk,tgd->kd/dot_general | solution.py:123
  93.5 4.9 %convolution_bitcast_fusion = f32[2048,128]{0,1:T(8,128)S(1)} fusion(bf16[4,128,256]{2,1,0:T(8,128)(2,1)S(1)} %bitcast.75, f32[4,256,2048]{1,2,0:T(8,128)} %fusion.7), kind=kOutput, calls=%fused_computation.15 | convolution fusion | flops 538968064 | bytes 9699328 | tf_op jit(solution)/shard_map/gtk,gdt->kd/dot_general | solution.py:124
  98.4 0.1 fusion.8
  98.5 0.1 fusion.57
  98.6 1.3 collective-permute-start.18
  99.9 1.9 %collective-permute-start.17 = (bf16[256,256]{0,1:T(8,128)(2,1)S(1)}, bf16[256,256]{0,1:T(8,128)(2,1)S(1)}, u32[]{:S(2)}, u32[]{:S(2)}) collective-permute-start(bf16[256,256]{0,1:T(8,128)(2,1)S(1)} %get-tuple-element.22), channel_id=1, source_target_pairs={{6,0},{7,1},{8,2},{9,3},{10,4},{11,5},{12,6},{13,7},{14,8},{15,9},... | collective-permute-start | bytes 393224 | tf_op jit(solution)/shard_map/ppermute | solution.py:15
  101.8 1.9 %collective-permute-start.16 = (bf16[256,256]{0,1:T(8,128)(2,1)S(1)}, bf16[256,256]{0,1:T(8,128)(2,1)}, u32[]{:S(2)}, u32[]{:S(2)}) collective-permute-start(bf16[256,256]{0,1:T(8,128)(2,1)S(1)} %get-tuple-element.23), channel_id=1, source_target_pairs={{5,0},{6,1},{7,2},{8,3},{9,4},{10,5},{11,6},{12,7},{13,8},{14,9},{... | collective-permute-start | bytes 393224 | tf_op jit(solution)/shard_map/ppermute | solution.py:15
  103.8 1.9 %collective-permute-start.15 = (bf16[256,256]{0,1:T(8,128)(2,1)S(1)}, bf16[256,256]{0,1:T(8,128)(2,1)}, u32[]{:S(2)}, u32[]{:S(2)}) collective-permute-start(bf16[256,256]{0,1:T(8,128)(2,1)S(1)} %get-tuple-element.24), channel_id=1, source_target_pairs={{4,0},{5,1},{6,2},{7,3},{8,4},{9,5},{10,6},{11,7},{12,8},{13,9},{1... | collective-permute-start | bytes 393224 | tf_op jit(solution)/shard_map/ppermute | solution.py:15
  105.7 1.9 %collective-permute-start.14 = (bf16[256,256]{0,1:T(8,128)(2,1)S(1)}, bf16[256,256]{0,1:T(8,128)(2,1)}, u32[]{:S(2)}, u32[]{:S(2)}) collective-permute-start(bf16[256,256]{0,1:T(8,128)(2,1)S(1)} %get-tuple-element.25), channel_id=1, source_target_pairs={{3,0},{4,1},{5,2},{6,3},{7,4},{8,5},{9,6},{10,7},{11,8},{12,9},{13... | collective-permute-start | bytes 393224 | tf_op jit(solution)/shard_map/ppermute | solution.py:15
  107.6 1.9 %collective-permute-start.13 = (bf16[256,256]{0,1:T(8,128)(2,1)S(1)}, bf16[256,256]{0,1:T(8,128)(2,1)}, u32[]{:S(2)}, u32[]{:S(2)}) collective-permute-start(bf16[256,256]{0,1:T(8,128)(2,1)S(1)} %get-tuple-element.26), channel_id=1, source_target_pairs={{2,0},{3,1},{4,2},{5,3},{6,4},{7,5},{8,6},{9,7},{10,8},{11,9},{12,... | collective-permute-start | bytes 393224 | tf_op jit(solution)/shard_map/ppermute | solution.py:15
  109.6 0.6 copy-done.2
  110.2 1.9 %collective-permute-start.12 = (bf16[256,256]{0,1:T(8,128)(2,1)S(1)}, bf16[256,256]{0,1:T(8,128)(2,1)}, u32[]{:S(2)}, u32[]{:S(2)}) collective-permute-start(bf16[256,256]{0,1:T(8,128)(2,1)S(1)} %get-tuple-element.20), channel_id=1, source_target_pairs={{1,0},{2,1},{3,2},{4,3},{5,4},{6,5},{7,6},{8,7},{9,8},{10,9},{11,1... | collective-permute-start | bytes 393224 | tf_op jit(solution)/shard_map/ppermute | solution.py:15
  112.2 0.8 convolution_convert_fusion.1
  112.9 0.8 copy.52
  113.8 1.6 %collective-permute-done.15 = bf16[256,256]{0,1:T(8,128)(2,1)} collective-permute-done((bf16[256,256]{0,1:T(8,128)(2,1)S(1)}, bf16[256,256]{0,1:T(8,128)(2,1)}, u32[]{:S(2)}, u32[]{:S(2)}) %collective-permute-start.15) | collective-permute-done | bytes 131104 | tf_op jit(solution)/shard_map/ppermute | solution.py:15
  115.3 1.4 %collective-permute-done.14 = bf16[256,256]{0,1:T(8,128)(2,1)} collective-permute-done((bf16[256,256]{0,1:T(8,128)(2,1)S(1)}, bf16[256,256]{0,1:T(8,128)(2,1)}, u32[]{:S(2)}, u32[]{:S(2)}) %collective-permute-start.14) | collective-permute-done | bytes 131104 | tf_op jit(solution)/shard_map/ppermute | solution.py:15
  116.7 3.4 %collective-permute-done.13 = bf16[256,256]{0,1:T(8,128)(2,1)} collective-permute-done((bf16[256,256]{0,1:T(8,128)(2,1)S(1)}, bf16[256,256]{0,1:T(8,128)(2,1)}, u32[]{:S(2)}, u32[]{:S(2)}) %collective-permute-start.13) | collective-permute-done | bytes 131104 | tf_op jit(solution)/shard_map/ppermute | solution.py:15
  120.1 1.4 fusion.45
  121.5 0.7 copy.53
  122.2 0.7 copy.54
  123.0 8.6 %reduce-scatter.2.cloned.1.call-done = bf16[512,256]{1,0:T(8,128)(2,1)} async-done(((bf16[4096,256]{1,0:T(8,128)(2,1)}), bf16[512,256]{1,0:T(8,128)(2,1)}) %reduce-scatter.2.cloned.1.call-update) | async-done | bytes 262160 | tf_op jit(solution)/shard_map/reduce_scatter | solution.py:106
  (25 shorter events, 0.2 us)
Async XLA Ops:
  7.2 124.4 %reduce-scatter.2.cloned.1.call-start = ((), (), s32[]{:S(2)}) async-start(), calls=%async_computation.1 | async-start | bytes 2359296 | tf_op jit(solution)/shard_map/reduce_scatter | solution.py:106
  7.2 20.8 %collective-permute-start.5 = (bf16[512,256]{1,0:T(8,128)(2,1)}, bf16[512,256]{1,0:T(8,128)(2,1)S(1)}, u32[]{:S(2)}, u32[]{:S(2)}) collective-permute-start(bf16[512,256]{1,0:T(8,128)(2,1)} %param.10), channel_id=1, source_target_pairs={{0,448},{64,0},{128,64},{192,128},{256,192},{320,256},{384,320},{4... | collective-permute-start | bytes 786440 | tf_op jit(solution)/shard_map/ppermute | solution.py:20
  12.6 20.6 %collective-permute-start.4 = (bf16[512,256]{1,0:T(8,128)(2,1)}, bf16[512,256]{1,0:T(8,128)(2,1)S(1)}, u32[]{:S(2)}, u32[]{:S(2)}) collective-permute-start(bf16[512,256]{1,0:T(8,128)(2,1)} %param.10), channel_id=1, source_target_pairs={{0,64},{64,128},{128,192},{192,256},{256,320},{320,384},{384,448},... | collective-permute-start | bytes 786440 | tf_op jit(solution)/shard_map/ppermute | solution.py:20
  15.4 7.0 %collective-permute-start = (bf16[1,256,256]{2,1,0:T(8,128)(2,1)S(1)}, bf16[1,256,256]{2,1,0:T(8,128)(2,1)S(1)}, u32[]{:S(2)}, u32[]{:S(2)}) collective-permute-start(bf16[1,256,256]{2,1,0:T(8,128)(2,1)S(1)} %maximum_bitcast_fusion), channel_id=1, source_target_pairs={{0,1},{1,2},{2,3},{3,4},{4,5},{5,6},{6,7},{7,8},{8,9},{9,10},{10,1... | collective-permute-start | bytes 393224 | tf_op jit(solution)/shard_map/ppermute | solution.py:15
  22.4 15.4 %collective-permute-start.1 = (bf16[2,256,256]{2,1,0:T(8,128)(2,1)S(1)}, bf16[2,256,256]{2,1,0:T(8,128)(2,1)S(1)}, u32[]{:S(2)}, u32[]{:S(2)}) collective-permute-start(bf16[2,256,256]{2,1,0:T(8,128)(2,1)S(1)} %pad_maximum_fusion.4), channel_id=1, source_target_pairs={{0,2},{1,3},{2,4},{3,5},{4,6},{5,7},{6,8},{7,9},{8,10},{9,11},{10,... | collective-permute-start | bytes 786440 | tf_op jit(solution)/shard_map/ppermute | solution.py:15
  28.1 19.1 %collective-permute-start.7 = (bf16[512,256]{1,0:T(8,128)(2,1)S(1)}, bf16[512,256]{1,0:T(8,128)(2,1)}, u32[]{:S(2)}, u32[]{:S(2)}) collective-permute-start(bf16[512,256]{1,0:T(8,128)(2,1)S(1)} %collective-permute-done.5), channel_id=1, source_target_pairs={{0,448},{64,0},{128,64},{192,128},{256,192},{320,256},{384,320},{4... | collective-permute-start | bytes 786440 | tf_op jit(solution)/shard_map/ppermute | solution.py:20
  33.2 19.1 %collective-permute-start.6 = (bf16[512,256]{1,0:T(8,128)(2,1)S(1)}, bf16[512,256]{1,0:T(8,128)(2,1)}, u32[]{:S(2)}, u32[]{:S(2)}) collective-permute-start(bf16[512,256]{1,0:T(8,128)(2,1)S(1)} %collective-permute-done.4), channel_id=1, source_target_pairs={{0,64},{64,128},{128,192},{192,256},{256,320},{320,384},{384,448},... | collective-permute-start | bytes 786440 | tf_op jit(solution)/shard_map/ppermute | solution.py:20
  38.0 26.0 %collective-permute-start.2 = (bf16[4,256,128]{2,1,0:T(8,128)(2,1)S(1)}, bf16[4,256,128]{2,1,0:T(8,128)(2,1)}, u32[]{:S(2)}, u32[]{:S(2)}) collective-permute-start(bf16[4,256,128]{2,1,0:T(8,128)(2,1)S(1)} %get-tuple-element.28), channel_id=1, source_target_pairs={{0,4},{1,5},{2,6},{3,7},{4,8},{5,9},{6,10},{7,11},{8,12},{9,13},{1... | collective-permute-start | bytes 786440 | tf_op jit(solution)/shard_map/ppermute | solution.py:15
  40.9 16.2 %collective-permute-start.3 = (bf16[4,256,128]{2,1,0:T(8,128)(2,1)S(1)}, bf16[4,256,128]{2,1,0:T(8,128)(2,1)S(1)}, u32[]{:S(2)}, u32[]{:S(2)}) collective-permute-start(bf16[4,256,128]{2,1,0:T(8,128)(2,1)S(1)} %get-tuple-element.27), channel_id=1, source_target_pairs={{0,4},{1,5},{2,6},{3,7},{4,8},{5,9},{6,10},{7,11},{8,12},{9,13},{1... | collective-permute-start | bytes 786440 | tf_op jit(solution)/shard_map/ppermute | solution.py:15
  47.2 18.0 %collective-permute-start.9 = (bf16[512,256]{1,0:T(8,128)(2,1)}, bf16[512,256]{1,0:T(8,128)(2,1)S(1)}, u32[]{:S(2)}, u32[]{:S(2)}) collective-permute-start(bf16[512,256]{1,0:T(8,128)(2,1)} %collective-permute-done.7), channel_id=1, source_target_pairs={{0,448},{64,0},{128,64},{192,128},{256,192},{320,256},{384,320},{4... | collective-permute-start | bytes 786440 | tf_op jit(solution)/shard_map/ppermute | solution.py:20
  52.3 18.1 %collective-permute-start.8 = (bf16[512,256]{1,0:T(8,128)(2,1)}, bf16[512,256]{1,0:T(8,128)(2,1)S(1)}, u32[]{:S(2)}, u32[]{:S(2)}) collective-permute-start(bf16[512,256]{1,0:T(8,128)(2,1)} %collective-permute-done.6), channel_id=1, source_target_pairs={{0,64},{64,128},{128,192},{192,256},{256,320},{320,384},{384,448},... | collective-permute-start | bytes 786440 | tf_op jit(solution)/shard_map/ppermute | solution.py:20
  64.0 15.7 %copy-start = (bf16[512,4096]{1,0:T(8,128)(2,1)S(1)}, bf16[512,4096]{1,0:T(8,128)(2,1)}, u32[]{:S(2)}) copy-start(bf16[512,4096]{1,0:T(8,128)(2,1)} %param.9) | copy-start | bytes 12582916
  65.2 8.8 %collective-permute-start.11 = (bf16[256,256]{1,0:T(8,128)(2,1)S(1)}, bf16[256,256]{1,0:T(8,128)(2,1)S(1)}, u32[]{:S(2)}, u32[]{:S(2)}) collective-permute-start(bf16[256,256]{1,0:T(8,128)(2,1)S(1)} %slice.76), channel_id=1, source_target_pairs={{0,448},{64,0},{128,64},{192,128},{256,192},{320,256},{384,320},{4... | collective-permute-start | bytes 393224 | tf_op jit(solution)/shard_map/ppermute | solution.py:20
  70.5 8.1 %collective-permute-start.10 = (bf16[256,256]{1,0:T(8,128)(2,1)S(1)}, bf16[256,256]{1,0:T(8,128)(2,1)S(1)}, u32[]{:S(2)}, u32[]{:S(2)}) collective-permute-start(bf16[256,256]{1,0:T(8,128)(2,1)S(1)} %slice.75), channel_id=1, source_target_pairs={{0,64},{64,128},{128,192},{192,256},{256,320},{320,384},{384,448},... | collective-permute-start | bytes 393224 | tf_op jit(solution)/shard_map/ppermute | solution.py:20
  98.6 9.0 %collective-permute-start.18 = (bf16[256,256]{0,1:T(8,128)(2,1)S(1)}, bf16[256,256]{0,1:T(8,128)(2,1)S(1)}, u32[]{:S(2)}, u32[]{:S(2)}) collective-permute-start(bf16[256,256]{0,1:T(8,128)(2,1)S(1)} %get-tuple-element.21), channel_id=1, source_target_pairs={{7,0},{8,1},{9,2},{10,3},{11,4},{12,5},{13,6},{14,7},{15,8},{16,9}... | collective-permute-start | bytes 393224 | tf_op jit(solution)/shard_map/ppermute | solution.py:15
  99.9 9.7 %collective-permute-start.17 = (bf16[256,256]{0,1:T(8,128)(2,1)S(1)}, bf16[256,256]{0,1:T(8,128)(2,1)S(1)}, u32[]{:S(2)}, u32[]{:S(2)}) collective-permute-start(bf16[256,256]{0,1:T(8,128)(2,1)S(1)} %get-tuple-element.22), channel_id=1, source_target_pairs={{6,0},{7,1},{8,2},{9,3},{10,4},{11,5},{12,6},{13,7},{14,8},{15,9},... | collective-permute-start | bytes 393224 | tf_op jit(solution)/shard_map/ppermute | solution.py:15
  101.8 11.9 %collective-permute-start.16 = (bf16[256,256]{0,1:T(8,128)(2,1)S(1)}, bf16[256,256]{0,1:T(8,128)(2,1)}, u32[]{:S(2)}, u32[]{:S(2)}) collective-permute-start(bf16[256,256]{0,1:T(8,128)(2,1)S(1)} %get-tuple-element.23), channel_id=1, source_target_pairs={{5,0},{6,1},{7,2},{8,3},{9,4},{10,5},{11,6},{12,7},{13,8},{14,9},{... | collective-permute-start | bytes 393224 | tf_op jit(solution)/shard_map/ppermute | solution.py:15
  103.8 11.6 %collective-permute-start.15 = (bf16[256,256]{0,1:T(8,128)(2,1)S(1)}, bf16[256,256]{0,1:T(8,128)(2,1)}, u32[]{:S(2)}, u32[]{:S(2)}) collective-permute-start(bf16[256,256]{0,1:T(8,128)(2,1)S(1)} %get-tuple-element.24), channel_id=1, source_target_pairs={{4,0},{5,1},{6,2},{7,3},{8,4},{9,5},{10,6},{11,7},{12,8},{13,9},{1... | collective-permute-start | bytes 393224 | tf_op jit(solution)/shard_map/ppermute | solution.py:15
  105.7 11.0 %collective-permute-start.14 = (bf16[256,256]{0,1:T(8,128)(2,1)S(1)}, bf16[256,256]{0,1:T(8,128)(2,1)}, u32[]{:S(2)}, u32[]{:S(2)}) collective-permute-start(bf16[256,256]{0,1:T(8,128)(2,1)S(1)} %get-tuple-element.25), channel_id=1, source_target_pairs={{3,0},{4,1},{5,2},{6,3},{7,4},{8,5},{9,6},{10,7},{11,8},{12,9},{13... | collective-permute-start | bytes 393224 | tf_op jit(solution)/shard_map/ppermute | solution.py:15
  107.6 2.0 %copy-start.1 = (bf16[256,256]{0,1:T(8,128)(2,1)}, bf16[256,256]{0,1:T(8,128)(2,1)S(1)}, u32[]{:S(2)}) copy-start(bf16[256,256]{0,1:T(8,128)(2,1)S(1)} %collective-permute-done.18) | copy-start | bytes 393220
  107.6 12.5 %collective-permute-start.13 = (bf16[256,256]{0,1:T(8,128)(2,1)S(1)}, bf16[256,256]{0,1:T(8,128)(2,1)}, u32[]{:S(2)}, u32[]{:S(2)}) collective-permute-start(bf16[256,256]{0,1:T(8,128)(2,1)S(1)} %get-tuple-element.26), channel_id=1, source_target_pairs={{2,0},{3,1},{4,2},{5,3},{6,4},{7,5},{8,6},{9,7},{10,8},{11,9},{12,... | collective-permute-start | bytes 393224 | tf_op jit(solution)/shard_map/ppermute | solution.py:15
  109.6 0.7 copy-start.2
  110.2 9.9 %collective-permute-start.12 = (bf16[256,256]{0,1:T(8,128)(2,1)S(1)}, bf16[256,256]{0,1:T(8,128)(2,1)}, u32[]{:S(2)}, u32[]{:S(2)}) collective-permute-start(bf16[256,256]{0,1:T(8,128)(2,1)S(1)} %get-tuple-element.20), channel_id=1, source_target_pairs={{1,0},{2,1},{3,2},{4,3},{5,4},{6,5},{7,6},{8,7},{9,8},{10,9},{11,1... | collective-permute-start | bytes 393224 | tf_op jit(solution)/shard_map/ppermute | solution.py:15
Sparse Core Ops, SparseCore 0:
  87.5 43.9 reduce-scatter.1

commit v8 on v6

--- a/solution.py
+++ b/solution.py
@@ -13,6 +13,17 @@
     count = lax.axis_size(axis)
     first, last = (max(0, -steps), min(count, count - steps))
     return lax.ppermute(value, axis, [(source, source + steps) for source in range(first, last)])
+
+
+def softmax_weights(query_heads, flat_keys, visible, scaling):
+    scores = (
+        jnp.einsum("tgd,kd->gtk", query_heads, flat_keys, preferred_element_type=jnp.float32)
+        * scaling
+    )
+    scores = jnp.where(visible[None], scores, -jnp.inf)
+    largest = jnp.max(scores, axis=-1, keepdims=True)
+    expons = jnp.exp(scores - largest)
+    return expons / jnp.sum(expons, axis=-1, keepdims=True)
 
 
 def per_device(queries, keys, values, out_weight, out_grad, doc_lengths):
@@ -44,18 +55,11 @@
     ).reshape(-1)
     visible = (key_pos[None, :] >= first_key[:, None]) & (key_pos[None, :] <= positions[:, None])
     query_heads = queries.reshape(tok_rows, group_size, head_dim)
-    scores = (
-        jnp.einsum("tgd,kd->gtk", query_heads, flat_keys, preferred_element_type=jnp.float32)
-        * scaling
-    )
-    scores = jnp.where(visible[None], scores, -jnp.inf)
-    largest = jnp.max(scores, axis=-1, keepdims=True)
-    expons = jnp.exp(scores - largest)
-    weights = expons / jnp.sum(expons, axis=-1, keepdims=True)
-    value_sent, weights = lax.optimization_barrier((value_sent, weights))
+    weights = softmax_weights(query_heads, flat_keys, visible, scaling)
+    probs = weights.astype(jnp.bfloat16)
+    value_sent, probs = lax.optimization_barrier((value_sent, probs))
     value_window = jnp.concatenate([value_window, value_sent], axis=0)
     flat_values = value_window.reshape(num_blocks * tok_rows, head_dim)
-    probs = weights.astype(jnp.bfloat16)
     attn_heads = jnp.einsum(
         "gtk,kd->tgd", probs, flat_values, preferred_element_type=jnp.float32
     ).astype(jnp.bfloat16)
@@ -68,7 +72,10 @@
     out_t = lax.psum_scatter(
         out_partial, "heads", scatter_dimension=0, tiled=True
     )
-    _, gathered = lax.optimization_barrier((out_partial, gathered))
+    _, gathered, query_again, keys_again = lax.optimization_barrier(
+        (out_partial, gathered, query_heads, flat_keys)
+    )
+    weights = softmax_weights(query_again, keys_again, visible, scaling)
     grad_attn = jnp.dot(
         out_weight,
         gathered,

time: 113 us -> 127 us (1.12)
  matrix products: 30.2 us -> 46 us
  waiting for transfers between devices: 26.6 us -> 25 us
    sub x0 -> x1, matrix products: none -> 7.04 us  [softmax_weights(): expons = jnp.exp(scores - largest)]
    div x1 -> x2, matrix products: 6.81 us -> 13.6 us  [softmax_weights(): return expons / jnp.sum(expons, axis=-1, keepdims=True)]
    reduce_scatter x1, waiting for transfers between devices: 5 us -> 0.01 us  [per_device(): lax.psum_scatter(out_partial, 'heads', scatter_dimension=0, tiled=True)]
    ppermute x11, waiting for transfers between devices: 15.7 us -> 18.4 us  [passed_along(): lax.ppermute(value, axis, [(source, source + steps) for source in range(f...]
    dot_general x1, matrix products: 4.63 us -> 7.09 us  [per_device(): jnp.einsum('gdt,kd->gtk', grad_heads, flat_values, preferred_element_type...]
    dot_general x1, matrix products: 3.15 us -> 5.32 us  [per_device(): lax.dot_general(out_weight, attn, (((0,), (1,)), ((), ())), preferred_ele...]
    dot_general x1, matrix products: 4.34 us -> 2.95 us  [per_device(): jnp.einsum('gtk,kd->tgd', probs, flat_values, preferred_element_type=jnp....]
    unnamed x11 -> x13, local copies, waits for them, and re-layouts: 3.49 us -> 2.56 us
  transfers between devices with their start and end apart: 13 -> 13, of which waited for: 8 -> 8; matrix products, arithmetic and copies ran while one was open for 35% -> 45% of each run, Pallas kernels for 0% -> 0%
where the time goes in v8:
time: 127 us; the launch traced here: 126 us
  matrix products  46 us (36%)
  starting transfers between devices  30.6 us (24%)
  waiting for transfers between devices  25 us (20%)
  between operations  14.3 us (11%)
  local copies, waits for them, and re-layouts  5.67 us (4%)
  other arithmetic  4.49 us (4%)
    ppermute x11, starting transfers between devices, passed_along(): lax.ppermute(value, axis, [(source, source + steps) for source in range(f...  30.5 us
    ppermute x11, waiting for transfers between devices, passed_along(): lax.ppermute(value, axis, [(source, source + steps) for source in range(f...  18.4 us
    div x2, matrix products, softmax_weights(): return expons / jnp.sum(expons, axis=-1, keepdims=True)  13.6 us
    dot_general x1, matrix products, per_device(): jnp.einsum('gdt,kd->gtk', grad_heads, flat_values, preferred_element_type...  7.09 us
    sub x1, matrix products, softmax_weights(): expons = jnp.exp(scores - largest)  7.04 us
    all_gather x1, waiting for transfers between devices, per_device(): gathered = lax.all_gather(out_grad, 'heads', axis=0, tiled=True)  5.9 us
    dot_general x1, matrix products, per_device(): lax.dot_general(out_weight, attn, (((0,), (1,)), ((), ())), preferred_ele...  5.32 us
    dot_general x1, matrix products, per_device(): jnp.dot(out_weight, gathered, preferred_element_type=jnp.float32)  4.12 us
  transfers between devices with their start and end apart: 13, of which 8 were waited for; matrix products, arithmetic and copies ran while one was open for 45% of the time, Pallas kernels for 0%

profile of v8, /device:TPU:6, one launch (start us, length us, event | category | flops | bytes accessed | tf_op | source)
XLA Modules:
  0.0 126.1 jit_solution(8719140261253131101)
XLA Ops:
  7.2 0.0 all-gather.2.cloned.1.call-start
  7.2 0.7 all-gather.2.cloned.1.call-update
  7.9 0.0 reduce-scatter.2.cloned.1.call-start
  7.9 0.9 maximum_bitcast_fusion
  8.8 1.9 %collective-permute-start = (bf16[1,256,256]{2,1,0:T(8,128)(2,1)S(1)}, bf16[1,256,256]{2,1,0:T(8,128)(2,1)S(1)}, u32[]{:S(2)}, u32[]{:S(2)}) collective-permute-start(bf16[1,256,256]{2,1,0:T(8,128)(2,1)S(1)} %maximum_bitcast_fusion), channel_id=1, source_target_pairs={{0,1},{1,2},{2,3},{3,4},{4,5},{5,6},{6,7},{7,8},{8,9},{9,10},{10,1... | collective-permute-start | bytes 393224 | tf_op jit(solution)/shard_map/ppermute | solution.py:15
  10.8 4.3 %collective-permute-done = bf16[1,256,256]{2,1,0:T(8,128)(2,1)S(1)} collective-permute-done((bf16[1,256,256]{2,1,0:T(8,128)(2,1)S(1)}, bf16[1,256,256]{2,1,0:T(8,128)(2,1)S(1)}, u32[]{:S(2)}, u32[]{:S(2)}) %collective-permute-start) | collective-permute-done | bytes 131104 | tf_op jit(solution)/shard_map/ppermute | solution.py:15
  15.2 6.3 %collective-permute-start.1 = (bf16[2,256,256]{2,1,0:T(8,128)(2,1)S(1)}, bf16[2,256,256]{2,1,0:T(8,128)(2,1)S(1)}, u32[]{:S(2)}, u32[]{:S(2)}) collective-permute-start(bf16[2,256,256]{2,1,0:T(8,128)(2,1)S(1)} %pad_maximum_fusion.4), channel_id=1, source_target_pairs={{0,2},{1,3},{2,4},{3,5},{4,6},{5,7},{6,8},{7,9},{8,10},{9,11},{10,... | collective-permute-start | bytes 786440 | tf_op jit(solution)/shard_map/ppermute | solution.py:15
  21.5 0.1 add_bitcast_fusion
  21.5 0.7 copy.44
  22.3 0.1 reduce.1
  22.4 0.7 sub.39
  23.1 1.0 reshape.156
  24.1 0.2 copy.55
  24.3 0.1 select_reduce_fusion
  24.4 0.9 collective-permute-done.1
  25.3 0.1 pad_maximum_fusion.1
  25.4 0.1 fusion.58
  25.5 4.2 %collective-permute-start.3 = (bf16[4,256,128]{2,1,0:T(8,128)(2,1)S(1)}, bf16[4,256,128]{2,1,0:T(8,128)(2,1)S(1)}, u32[]{:S(2)}, u32[]{:S(2)}) collective-permute-start(bf16[4,256,128]{2,1,0:T(8,128)(2,1)S(1)} %get-tuple-element.33), channel_id=1, source_target_pairs={{0,4},{1,5},{2,6},{3,7},{4,8},{5,9},{6,10},{7,11},{8,12},{9,13},{1... | collective-permute-start | bytes 786440 | tf_op jit(solution)/shard_map/ppermute | solution.py:15
  29.7 0.6 compare_and_fusion
  30.3 4.9 %collective-permute-start.2 = (bf16[4,256,128]{2,1,0:T(8,128)(2,1)S(1)}, bf16[4,256,128]{2,1,0:T(8,128)(2,1)S(1)}, u32[]{:S(2)}, u32[]{:S(2)}) collective-permute-start(bf16[4,256,128]{2,1,0:T(8,128)(2,1)S(1)} %get-tuple-element.34), channel_id=1, source_target_pairs={{0,4},{1,5},{2,6},{3,7},{4,8},{5,9},{6,10},{7,11},{8,12},{9,13},{1... | collective-permute-start | bytes 786440 | tf_op jit(solution)/shard_map/ppermute | solution.py:15
  35.3 2.9 %collective-permute-done.3 = bf16[4,256,128]{2,1,0:T(8,128)(2,1)S(1)} collective-permute-done((bf16[4,256,128]{2,1,0:T(8,128)(2,1)S(1)}, bf16[4,256,128]{2,1,0:T(8,128)(2,1)S(1)}, u32[]{:S(2)}, u32[]{:S(2)}) %collective-permute-start.3) | collective-permute-done | bytes 262176 | tf_op jit(solution)/shard_map/ppermute | solution.py:15
  38.2 5.7 %divide_convert_fusion = bf16[4,256,2048]{1,2,0:T(8,128)(2,1)} fusion(pred[256,2048]{0,1:T(8,128)(4,1)S(1)} %compare_and_fusion, bf16[2048,128,1]{1,0,2:T(8,128)(2,1)S(1)} %bitcast.95, bf16[256,4,128]{0,2,1:T(8,128)(2,1)S(1)} %copy.55), kind=kOutput, calls=%fused_computation.8 | convolution fusion | flops 547362816 | bytes 5505024 | tf_op jit(solution)/shard_map/div | solution.py:26
  43.9 0.0 copy-done.1
  43.9 0.0 collective-permute-done.2
  44.0 3.0 %bitcast_convert_fusion = (f32[4,256,128]{1,2,0:T(8,128)S(1)}, bf16[128,4,256]{2,0,1:T(8,128)(2,1)S(1)}) fusion(bf16[2048,128,1]{1,0,2:T(8,128)(2,1)S(1)} %bitcast.99, bf16[4,256,2048]{1,2,0:T(8,128)(2,1)} %divide_convert_fusion), kind=kOutput, calls=%fused_computation.50 | convolution fusion | flops 537133056 | bytes 5505024 | tf_op jit(solution)/shard_map/gtk,kd->tgd/dot_general | solution.py:63
  46.9 0.2 copy.69
  47.2 5.3 %fusion.6 = bf16[4096,256]{1,0:T(8,128)(2,1)} fusion(bf16[256,512]{0,1:T(8,128)(2,1)S(1)} %bitcast.102, bf16[512,4096]{1,0:T(8,128)(2,1)} %param.9), kind=kOutput, calls=%fused_computation.13 | convolution fusion | flops 1074790400 | bytes 6553600 | tf_op jit(solution)/shard_map/dot_general | solution.py:67
  52.5 0.0 reduce-scatter.2.cloned.1.call-update
  52.5 5.9 %all-gather.2.cloned.1.call-done = bf16[4096,256]{1,0:T(8,128)(2,1)} async-done(((bf16[512,256]{1,0:T(8,128)(2,1)}), bf16[4096,256]{1,0:T(8,128)(2,1)}) %all-gather.2.cloned.1.call-update) | async-done | bytes 2097168 | tf_op jit(solution)/shard_map/all_gather | solution.py:71
  58.4 4.1 %fusion.14 = bf16[512,256]{0,1:T(8,128)(2,1)S(1)} fusion(bf16[4096,256]{1,0:T(8,128)(2,1)} %all-gather.2.cloned.1.call-done, bf16[512,4096]{1,0:T(8,128)(2,1)} %param.9), kind=kOutput, calls=%fused_computation.30 | convolution fusion | flops 1073872896 | bytes 6553600 | tf_op jit(solution)/shard_map/dot_general | solution.py:79
  62.5 0.1 reshape.159
  62.6 0.9 copy.57
  63.5 3.7 %convolution_bitcast_fusion = f32[2048,128]{0,1:T(8,128)S(1)} fusion(bf16[4,256,2048]{1,2,0:T(8,128)(2,1)} %divide_convert_fusion, bf16[4,128,256]{2,1,0:T(8,128)(2,1)} %copy.57), kind=kOutput, calls=%fused_computation.23 | convolution fusion | flops 536870912 | bytes 5505024 | tf_op jit(solution)/shard_map/gtk,gdt->kd/dot_general | solution.py:98
  67.2 0.4 multiply_reduce_fusion
  67.5 0.1 copy.70
  67.6 7.9 %fusion = f32[4,256,2048]{1,2,0:T(8,128)} fusion(pred[256,2048]{0,1:T(8,128)(4,1)} %copy-done.1, bf16[2048,128]{1,0:T(8,128)(2,1)S(1)} %bitcast.96, bf16[256,4,128]{2,1,0:T(4,128)(2,1)S(1)} %reshape.156), kind=kOutput, calls=%fused_computation | convolution fusion | flops 543168512 | bytes 9699328 | tf_op jit(solution)/shard_map/div | solution.py:26
  75.5 7.0 %subtract_exponential_fusion = f32[4,256,2048]{1,2,0:T(8,128)} fusion(pred[256,2048]{0,1:T(8,128)(4,1)} %copy-done.1, bf16[2048,128]{1,0:T(8,128)(2,1)S(1)} %bitcast.97, bf16[256,4,128]{2,1,0:T(4,128)(2,1)S(1)} %reshape.156), kind=kOutput, calls=%fused_computation.7 | convolution fusion | flops 543165440 | bytes 9699328 | tf_op jit(solution)/shard_map/sub | solution.py:25
  82.5 0.0 copy-done
  82.5 7.1 %multiply_convert_fusion = bf16[4,256,2048]{1,2,0:T(8,128)(2,1)S(1)} fusion(f32[4,256,2048]{1,2,0:T(8,128)} %subtract_exponential_fusion, f32[4,256,2048]{1,2,0:T(8,128)} %fusion, bf16[2048,128,1]{1,0,2:T(8,128)(2,1)S(1)} %bitcast.100, bf16[4,128,256]{2,1,0:T(8,128)(2,1)S(1)} %copy-done, f32[4,256]{1,0:T(4,128)S(1)} %copy.70), kind=kOutput, calls=%fused_computation.6 | convolution fusion | flops 547356672 | bytes 21762048 | tf_op jit(solution)/shard_map/gdt,kd->gtk/dot_general | solution.py:88
  89.6 1.5 %convolution_bitcast_fusion.1 = f32[2048,128]{0,1:T(8,128)S(1)} fusion(bf16[4,256,2048]{1,2,0:T(8,128)(2,1)S(1)} %multiply_convert_fusion, bf16[256,4,128]{0,2,1:T(8,128)(2,1)S(1)} %copy.55), kind=kOutput, calls=%fused_computation.24 | convolution fusion | flops 536870912 | bytes 5505024 | tf_op jit(solution)/shard_map/gtk,tgd->kd/dot_general | solution.py:97
  91.1 0.1 fusion.13
  91.3 0.1 fusion.57
  91.3 1.9 %collective-permute-start.4 = (bf16[256,256]{0,1:T(8,128)(2,1)S(1)}, bf16[256,256]{0,1:T(8,128)(2,1)S(1)}, u32[]{:S(2)}, u32[]{:S(2)}) collective-permute-start(bf16[256,256]{0,1:T(8,128)(2,1)S(1)} %get-tuple-element.26), channel_id=1, source_target_pairs={{1,0},{2,1},{3,2},{4,3},{5,4},{6,5},{7,6},{8,7},{9,8},{10,9},{11,1... | collective-permute-start | bytes 393224 | tf_op jit(solution)/shard_map/ppermute | solution.py:15
  93.3 1.3 %collective-permute-start.10 = (bf16[256,256]{0,1:T(8,128)(2,1)S(1)}, bf16[256,256]{0,1:T(8,128)(2,1)S(1)}, u32[]{:S(2)}, u32[]{:S(2)}) collective-permute-start(bf16[256,256]{0,1:T(8,128)(2,1)S(1)} %get-tuple-element.27), channel_id=1, source_target_pairs={{7,0},{8,1},{9,2},{10,3},{11,4},{12,5},{13,6},{14,7},{15,8},{16,9}... | collective-permute-start | bytes 393224 | tf_op jit(solution)/shard_map/ppermute | solution.py:15
  94.6 1.9 %collective-permute-start.9 = (bf16[256,256]{0,1:T(8,128)(2,1)S(1)}, bf16[256,256]{0,1:T(8,128)(2,1)}, u32[]{:S(2)}, u32[]{:S(2)}) collective-permute-start(bf16[256,256]{0,1:T(8,128)(2,1)S(1)} %get-tuple-element.28), channel_id=1, source_target_pairs={{6,0},{7,1},{8,2},{9,3},{10,4},{11,5},{12,6},{13,7},{14,8},{15,9},... | collective-permute-start | bytes 393224 | tf_op jit(solution)/shard_map/ppermute | solution.py:15
  96.5 1.9 %collective-permute-start.8 = (bf16[256,256]{0,1:T(8,128)(2,1)S(1)}, bf16[256,256]{0,1:T(8,128)(2,1)}, u32[]{:S(2)}, u32[]{:S(2)}) collective-permute-start(bf16[256,256]{0,1:T(8,128)(2,1)S(1)} %get-tuple-element.29), channel_id=1, source_target_pairs={{5,0},{6,1},{7,2},{8,3},{9,4},{10,5},{11,6},{12,7},{13,8},{14,9},{... | collective-permute-start | bytes 393224 | tf_op jit(solution)/shard_map/ppermute | solution.py:15
  98.4 1.9 %collective-permute-start.7 = (bf16[256,256]{0,1:T(8,128)(2,1)S(1)}, bf16[256,256]{0,1:T(8,128)(2,1)}, u32[]{:S(2)}, u32[]{:S(2)}) collective-permute-start(bf16[256,256]{0,1:T(8,128)(2,1)S(1)} %get-tuple-element.30), channel_id=1, source_target_pairs={{4,0},{5,1},{6,2},{7,3},{8,4},{9,5},{10,6},{11,7},{12,8},{13,9},{1... | collective-permute-start | bytes 393224 | tf_op jit(solution)/shard_map/ppermute | solution.py:15
  100.3 0.0 collective-permute-done.4
  100.4 0.0 copy-start.2
  100.4 1.9 %collective-permute-start.6 = (bf16[256,256]{0,1:T(8,128)(2,1)S(1)}, bf16[256,256]{0,1:T(8,128)(2,1)}, u32[]{:S(2)}, u32[]{:S(2)}) collective-permute-start(bf16[256,256]{0,1:T(8,128)(2,1)S(1)} %get-tuple-element.31), channel_id=1, source_target_pairs={{3,0},{4,1},{5,2},{6,3},{7,4},{8,5},{9,6},{10,7},{11,8},{12,9},{13... | collective-permute-start | bytes 393224 | tf_op jit(solution)/shard_map/ppermute | solution.py:15
  102.3 0.0 collective-permute-done.10
  102.3 0.0 copy-start.3
  102.3 2.2 %collective-permute-start.5 = (bf16[256,256]{0,1:T(8,128)(2,1)S(1)}, bf16[256,256]{0,1:T(8,128)(2,1)}, u32[]{:S(2)}, u32[]{:S(2)}) collective-permute-start(bf16[256,256]{0,1:T(8,128)(2,1)S(1)} %get-tuple-element.32), channel_id=1, source_target_pairs={{2,0},{3,1},{4,2},{5,3},{6,4},{7,5},{8,6},{9,7},{10,8},{11,9},{12,... | collective-permute-start | bytes 393224 | tf_op jit(solution)/shard_map/ppermute | solution.py:15
  104.5 0.8 convolution_convert_fusion.2
  105.3 0.0 copy-done.2
  105.3 0.8 copy.58
  106.2 0.0 collective-permute-done.9
  106.2 2.3 %collective-permute-done.8 = bf16[256,256]{0,1:T(8,128)(2,1)} collective-permute-done((bf16[256,256]{0,1:T(8,128)(2,1)S(1)}, bf16[256,256]{0,1:T(8,128)(2,1)}, u32[]{:S(2)}, u32[]{:S(2)}) %collective-permute-start.8) | collective-permute-done | bytes 131104 | tf_op jit(solution)/shard_map/ppermute | solution.py:15
  108.5 2.3 %collective-permute-done.7 = bf16[256,256]{0,1:T(8,128)(2,1)} collective-permute-done((bf16[256,256]{0,1:T(8,128)(2,1)S(1)}, bf16[256,256]{0,1:T(8,128)(2,1)}, u32[]{:S(2)}, u32[]{:S(2)}) %collective-permute-start.7) | collective-permute-done | bytes 131104 | tf_op jit(solution)/shard_map/ppermute | solution.py:15
  110.8 3.1 %collective-permute-done.6 = bf16[256,256]{0,1:T(8,128)(2,1)} collective-permute-done((bf16[256,256]{0,1:T(8,128)(2,1)S(1)}, bf16[256,256]{0,1:T(8,128)(2,1)}, u32[]{:S(2)}, u32[]{:S(2)}) %collective-permute-start.6) | collective-permute-done | bytes 131104 | tf_op jit(solution)/shard_map/ppermute | solution.py:15
  113.9 2.5 %collective-permute-done.5 = bf16[256,256]{0,1:T(8,128)(2,1)} collective-permute-done((bf16[256,256]{0,1:T(8,128)(2,1)S(1)}, bf16[256,256]{0,1:T(8,128)(2,1)}, u32[]{:S(2)}, u32[]{:S(2)}) %collective-permute-start.5) | collective-permute-done | bytes 131104 | tf_op jit(solution)/shard_map/ppermute | solution.py:15
  116.4 1.4 %fusion.40 = bf16[256,256]{0,1:T(8,128)(2,1)S(1)} fusion(bf16[256,256]{0,1:T(8,128)(2,1)} %copy-done.3, bf16[256,256]{0,1:T(8,128)(2,1)} %collective-permute-done.9, bf16[256,256]{0,1:T(8,128)(2,1)} %collective-permute-done.8, bf16[256,256]{0,1:T(8,128)(2,1)} %collective-permute-done.7, bf16[256,256]{0,1:T(8,128)(2,1)} %collective-permute-done.6, ...), kind=kLoop, calls=%fused_computation.51 | loop fusion | flops 1048576 | bytes 3145728 | tf_op jit(solution)/shard_map/convert.1
  117.8 0.7 copy.60
  118.5 0.7 copy.59
  (12 shorter events, 0.2 us)
Async XLA Ops:
  7.2 51.2 %all-gather.2.cloned.1.call-start = ((), (), s32[]{:S(2)}) async-start(), calls=%async_computation.2 | async-start | bytes 2359296 | tf_op jit(solution)/shard_map/all_gather | solution.py:71
  7.9 111.4 %reduce-scatter.2.cloned.1.call-start = ((), (), s32[]{:S(2)}) async-start(), calls=%async_computation.1 | async-start | bytes 2359296 | tf_op jit(solution)/shard_map/reduce_scatter | solution.py:72
  8.8 6.3 %collective-permute-start = (bf16[1,256,256]{2,1,0:T(8,128)(2,1)S(1)}, bf16[1,256,256]{2,1,0:T(8,128)(2,1)S(1)}, u32[]{:S(2)}, u32[]{:S(2)}) collective-permute-start(bf16[1,256,256]{2,1,0:T(8,128)(2,1)S(1)} %maximum_bitcast_fusion), channel_id=1, source_target_pairs={{0,1},{1,2},{2,3},{3,4},{4,5},{5,6},{6,7},{7,8},{8,9},{9,10},{10,1... | collective-permute-start | bytes 393224 | tf_op jit(solution)/shard_map/ppermute | solution.py:15
  15.2 10.2 %collective-permute-start.1 = (bf16[2,256,256]{2,1,0:T(8,128)(2,1)S(1)}, bf16[2,256,256]{2,1,0:T(8,128)(2,1)S(1)}, u32[]{:S(2)}, u32[]{:S(2)}) collective-permute-start(bf16[2,256,256]{2,1,0:T(8,128)(2,1)S(1)} %pad_maximum_fusion.4), channel_id=1, source_target_pairs={{0,2},{1,3},{2,4},{3,5},{4,6},{5,7},{6,8},{7,9},{8,10},{9,11},{10,... | collective-permute-start | bytes 786440 | tf_op jit(solution)/shard_map/ppermute | solution.py:15
  25.5 12.6 %collective-permute-start.3 = (bf16[4,256,128]{2,1,0:T(8,128)(2,1)S(1)}, bf16[4,256,128]{2,1,0:T(8,128)(2,1)S(1)}, u32[]{:S(2)}, u32[]{:S(2)}) collective-permute-start(bf16[4,256,128]{2,1,0:T(8,128)(2,1)S(1)} %get-tuple-element.33), channel_id=1, source_target_pairs={{0,4},{1,5},{2,6},{3,7},{4,8},{5,9},{6,10},{7,11},{8,12},{9,13},{1... | collective-permute-start | bytes 786440 | tf_op jit(solution)/shard_map/ppermute | solution.py:15
  30.3 13.6 %copy-start.1 = (pred[256,2048]{0,1:T(8,128)(4,1)}, pred[256,2048]{0,1:T(8,128)(4,1)S(1)}, u32[]{:S(2)}) copy-start(pred[256,2048]{0,1:T(8,128)(4,1)S(1)} %compare_and_fusion) | copy-start | bytes 1572868
  30.3 13.6 %collective-permute-start.2 = (bf16[4,256,128]{2,1,0:T(8,128)(2,1)S(1)}, bf16[4,256,128]{2,1,0:T(8,128)(2,1)S(1)}, u32[]{:S(2)}, u32[]{:S(2)}) collective-permute-start(bf16[4,256,128]{2,1,0:T(8,128)(2,1)S(1)} %get-tuple-element.34), channel_id=1, source_target_pairs={{0,4},{1,5},{2,6},{3,7},{4,8},{5,9},{6,10},{7,11},{8,12},{9,13},{1... | collective-permute-start | bytes 786440 | tf_op jit(solution)/shard_map/ppermute | solution.py:15
  75.5 7.0 %copy-start = (bf16[4,128,256]{2,1,0:T(8,128)(2,1)S(1)}, bf16[4,128,256]{2,1,0:T(8,128)(2,1)}, u32[]{:S(2)}) copy-start(bf16[4,128,256]{2,1,0:T(8,128)(2,1)} %copy.57) | copy-start | bytes 786436
  91.3 9.0 %collective-permute-start.4 = (bf16[256,256]{0,1:T(8,128)(2,1)S(1)}, bf16[256,256]{0,1:T(8,128)(2,1)S(1)}, u32[]{:S(2)}, u32[]{:S(2)}) collective-permute-start(bf16[256,256]{0,1:T(8,128)(2,1)S(1)} %get-tuple-element.26), channel_id=1, source_target_pairs={{1,0},{2,1},{3,2},{4,3},{5,4},{6,5},{7,6},{8,7},{9,8},{10,9},{11,1... | collective-permute-start | bytes 393224 | tf_op jit(solution)/shard_map/ppermute | solution.py:15
  93.3 9.0 %collective-permute-start.10 = (bf16[256,256]{0,1:T(8,128)(2,1)S(1)}, bf16[256,256]{0,1:T(8,128)(2,1)S(1)}, u32[]{:S(2)}, u32[]{:S(2)}) collective-permute-start(bf16[256,256]{0,1:T(8,128)(2,1)S(1)} %get-tuple-element.27), channel_id=1, source_target_pairs={{7,0},{8,1},{9,2},{10,3},{11,4},{12,5},{13,6},{14,7},{15,8},{16,9}... | collective-permute-start | bytes 393224 | tf_op jit(solution)/shard_map/ppermute | solution.py:15
  94.6 11.6 %collective-permute-start.9 = (bf16[256,256]{0,1:T(8,128)(2,1)S(1)}, bf16[256,256]{0,1:T(8,128)(2,1)}, u32[]{:S(2)}, u32[]{:S(2)}) collective-permute-start(bf16[256,256]{0,1:T(8,128)(2,1)S(1)} %get-tuple-element.28), channel_id=1, source_target_pairs={{6,0},{7,1},{8,2},{9,3},{10,4},{11,5},{12,6},{13,7},{14,8},{15,9},... | collective-permute-start | bytes 393224 | tf_op jit(solution)/shard_map/ppermute | solution.py:15
  96.5 12.0 %collective-permute-start.8 = (bf16[256,256]{0,1:T(8,128)(2,1)S(1)}, bf16[256,256]{0,1:T(8,128)(2,1)}, u32[]{:S(2)}, u32[]{:S(2)}) collective-permute-start(bf16[256,256]{0,1:T(8,128)(2,1)S(1)} %get-tuple-element.29), channel_id=1, source_target_pairs={{5,0},{6,1},{7,2},{8,3},{9,4},{10,5},{11,6},{12,7},{13,8},{14,9},{... | collective-permute-start | bytes 393224 | tf_op jit(solution)/shard_map/ppermute | solution.py:15
  98.4 12.4 %collective-permute-start.7 = (bf16[256,256]{0,1:T(8,128)(2,1)S(1)}, bf16[256,256]{0,1:T(8,128)(2,1)}, u32[]{:S(2)}, u32[]{:S(2)}) collective-permute-start(bf16[256,256]{0,1:T(8,128)(2,1)S(1)} %get-tuple-element.30), channel_id=1, source_target_pairs={{4,0},{5,1},{6,2},{7,3},{8,4},{9,5},{10,6},{11,7},{12,8},{13,9},{1... | collective-permute-start | bytes 393224 | tf_op jit(solution)/shard_map/ppermute | solution.py:15
  100.4 5.0 %copy-start.2 = (bf16[256,256]{0,1:T(8,128)(2,1)}, bf16[256,256]{0,1:T(8,128)(2,1)S(1)}, u32[]{:S(2)}) copy-start(bf16[256,256]{0,1:T(8,128)(2,1)S(1)} %collective-permute-done.4) | copy-start | bytes 393220
  100.4 13.5 %collective-permute-start.6 = (bf16[256,256]{0,1:T(8,128)(2,1)S(1)}, bf16[256,256]{0,1:T(8,128)(2,1)}, u32[]{:S(2)}, u32[]{:S(2)}) collective-permute-start(bf16[256,256]{0,1:T(8,128)(2,1)S(1)} %get-tuple-element.31), channel_id=1, source_target_pairs={{3,0},{4,1},{5,2},{6,3},{7,4},{8,5},{9,6},{10,7},{11,8},{12,9},{13... | collective-permute-start | bytes 393224 | tf_op jit(solution)/shard_map/ppermute | solution.py:15
  102.3 3.0 %copy-start.3 = (bf16[256,256]{0,1:T(8,128)(2,1)}, bf16[256,256]{0,1:T(8,128)(2,1)S(1)}, u32[]{:S(2)}) copy-start(bf16[256,256]{0,1:T(8,128)(2,1)S(1)} %collective-permute-done.10) | copy-start | bytes 393220
  102.3 14.1 %collective-permute-start.5 = (bf16[256,256]{0,1:T(8,128)(2,1)S(1)}, bf16[256,256]{0,1:T(8,128)(2,1)}, u32[]{:S(2)}, u32[]{:S(2)}) collective-permute-start(bf16[256,256]{0,1:T(8,128)(2,1)S(1)} %get-tuple-element.32), channel_id=1, source_target_pairs={{2,0},{3,1},{4,2},{5,3},{6,4},{7,5},{8,6},{9,7},{10,8},{11,9},{12,... | collective-permute-start | bytes 393224 | tf_op jit(solution)/shard_map/ppermute | solution.py:15
Sparse Core Ops, SparseCore 0:
  10.1 48.2 all-gather.1
  61.8 43.4 reduce-scatter.1

commit v9 on v6

--- a/solution.py
+++ b/solution.py
@@ -52,10 +52,10 @@
     largest = jnp.max(scores, axis=-1, keepdims=True)
     expons = jnp.exp(scores - largest)
     weights = expons / jnp.sum(expons, axis=-1, keepdims=True)
-    value_sent, weights = lax.optimization_barrier((value_sent, weights))
+    probs = weights.astype(jnp.bfloat16)
+    value_sent, probs = lax.optimization_barrier((value_sent, probs))
     value_window = jnp.concatenate([value_window, value_sent], axis=0)
     flat_values = value_window.reshape(num_blocks * tok_rows, head_dim)
-    probs = weights.astype(jnp.bfloat16)
     attn_heads = jnp.einsum(
         "gtk,kd->tgd", probs, flat_values, preferred_element_type=jnp.float32
     ).astype(jnp.bfloat16)

time: 113 us -> 113 us (level)
  starting transfers between devices: 30.7 us -> 31.9 us
    div x1, matrix products: 6.81 us -> 8.59 us  [per_device(): weights = expons / jnp.sum(expons, axis=-1, keepdims=True)]
    dot_general x1, matrix products: 4.34 us -> 3.12 us  [per_device(): jnp.einsum('gtk,kd->tgd', probs, flat_values, preferred_element_type=jnp....]
    dot_general x1, matrix products: 4.87 us -> 3.67 us  [per_device(): jnp.einsum('gtk,gdt->kd', probs, grad_heads, preferred_element_type=jnp.f...]
where the time goes in v9:
time: 113 us; the launch traced here: 112 us
  starting transfers between devices  31.9 us (28%)
  matrix products  29.5 us (26%)
  waiting for transfers between devices  26 us (23%)
  between operations  14.3 us (13%)
  local copies, waits for them, and re-layouts  5.8 us (5%)
  other arithmetic  4.5 us (4%)
    ppermute x11, starting transfers between devices, passed_along(): lax.ppermute(value, axis, [(source, source + steps) for source in range(f...  31.8 us
    ppermute x11, waiting for transfers between devices, passed_along(): lax.ppermute(value, axis, [(source, source + steps) for source in range(f...  15.1 us
    div x1, matrix products, per_device(): weights = expons / jnp.sum(expons, axis=-1, keepdims=True)  8.59 us
    reduce_scatter x1, waiting for transfers between devices, per_device(): lax.psum_scatter(out_partial, 'heads', scatter_dimension=0, tiled=True)  5.4 us
    all_gather x1, waiting for transfers between devices, per_device(): gathered = lax.all_gather(out_grad, 'heads', axis=0, tiled=True)  4.76 us
    dot_general x1, matrix products, per_device(): jnp.einsum('gdt,kd->gtk', grad_heads, flat_values, preferred_element_type...  4.61 us
    dot_general x1, matrix products, per_device(): jnp.dot(out_weight, gathered, preferred_element_type=jnp.float32)  4.12 us
    dot_general x1, matrix products, per_device(): jnp.einsum('gtk,gdt->kd', probs, grad_heads, preferred_element_type=jnp.f...  3.67 us
  transfers between devices with their start and end apart: 13, of which 8 were waited for; matrix products, arithmetic and copies ran while one was open for 35% of the time, Pallas kernels for 0%

profile of v9, /device:TPU:6, one launch (start us, length us, event | category | flops | bytes accessed | tf_op | source)
XLA Modules:
  0.0 111.9 jit_solution(16629074882983437488)
XLA Ops:
  7.2 0.0 all-gather.2.cloned.1.call-start
  7.2 0.7 all-gather.2.cloned.1.call-update
  7.9 0.0 reduce-scatter.2.cloned.1.call-start
  7.9 0.9 maximum_bitcast_fusion
  8.8 1.9 %collective-permute-start = (bf16[1,256,256]{2,1,0:T(8,128)(2,1)S(1)}, bf16[1,256,256]{2,1,0:T(8,128)(2,1)S(1)}, u32[]{:S(2)}, u32[]{:S(2)}) collective-permute-start(bf16[1,256,256]{2,1,0:T(8,128)(2,1)S(1)} %maximum_bitcast_fusion), channel_id=1, source_target_pairs={{0,1},{1,2},{2,3},{3,4},{4,5},{5,6},{6,7},{7,8},{8,9},{9,10},{10,1... | collective-permute-start | bytes 393224 | tf_op jit(solution)/shard_map/ppermute | solution.py:15
  10.8 4.3 %collective-permute-done = bf16[1,256,256]{2,1,0:T(8,128)(2,1)S(1)} collective-permute-done((bf16[1,256,256]{2,1,0:T(8,128)(2,1)S(1)}, bf16[1,256,256]{2,1,0:T(8,128)(2,1)S(1)}, u32[]{:S(2)}, u32[]{:S(2)}) %collective-permute-start) | collective-permute-done | bytes 131104 | tf_op jit(solution)/shard_map/ppermute | solution.py:15
  15.2 6.3 %collective-permute-start.1 = (bf16[2,256,256]{2,1,0:T(8,128)(2,1)S(1)}, bf16[2,256,256]{2,1,0:T(8,128)(2,1)S(1)}, u32[]{:S(2)}, u32[]{:S(2)}) collective-permute-start(bf16[2,256,256]{2,1,0:T(8,128)(2,1)S(1)} %pad_maximum_fusion.4), channel_id=1, source_target_pairs={{0,2},{1,3},{2,4},{3,5},{4,6},{5,7},{6,8},{7,9},{8,10},{9,11},{10,... | collective-permute-start | bytes 786440 | tf_op jit(solution)/shard_map/ppermute | solution.py:15
  21.5 0.1 add_bitcast_fusion
  21.5 0.7 copy.42
  22.3 0.1 reduce.1
  22.4 0.7 sub.31
  23.1 1.1 copy.74
  24.2 0.1 select_reduce_fusion
  24.3 1.1 collective-permute-done.1
  25.3 0.1 pad_maximum_fusion.1
  25.4 0.1 fusion.24
  25.5 4.2 %collective-permute-start.3 = (bf16[4,256,128]{2,1,0:T(8,128)(2,1)S(1)}, bf16[4,256,128]{2,1,0:T(8,128)(2,1)S(1)}, u32[]{:S(2)}, u32[]{:S(2)}) collective-permute-start(bf16[4,256,128]{2,1,0:T(8,128)(2,1)S(1)} %get-tuple-element.29), channel_id=1, source_target_pairs={{0,4},{1,5},{2,6},{3,7},{4,8},{5,9},{6,10},{7,11},{8,12},{9,13},{1... | collective-permute-start | bytes 786440 | tf_op jit(solution)/shard_map/ppermute | solution.py:15
  29.7 0.6 compare_and_fusion
  30.3 4.9 %collective-permute-start.2 = (bf16[4,256,128]{2,1,0:T(8,128)(2,1)S(1)}, bf16[4,256,128]{2,1,0:T(8,128)(2,1)S(1)}, u32[]{:S(2)}, u32[]{:S(2)}) collective-permute-start(bf16[4,256,128]{2,1,0:T(8,128)(2,1)S(1)} %get-tuple-element.30), channel_id=1, source_target_pairs={{0,4},{1,5},{2,6},{3,7},{4,8},{5,9},{6,10},{7,11},{8,12},{9,13},{1... | collective-permute-start | bytes 786440 | tf_op jit(solution)/shard_map/ppermute | solution.py:15
  35.3 2.9 %collective-permute-done.3 = bf16[4,256,128]{2,1,0:T(8,128)(2,1)S(1)} collective-permute-done((bf16[4,256,128]{2,1,0:T(8,128)(2,1)S(1)}, bf16[4,256,128]{2,1,0:T(8,128)(2,1)S(1)}, u32[]{:S(2)}, u32[]{:S(2)}) %collective-permute-start.3) | collective-permute-done | bytes 262176 | tf_op jit(solution)/shard_map/ppermute | solution.py:15
  38.2 8.6 %fusion.26 = (bf16[4,256,2048]{1,2,0:T(8,128)(2,1)}, f32[4,256,2048]{1,2,0:T(8,128)}) fusion(pred[256,2048]{0,1:T(8,128)(4,1)S(1)} %compare_and_fusion, bf16[2048,128,1]{1,0,2:T(8,128)(2,1)S(1)} %bitcast.71, bf16[256,4,128]{0,2,1:T(8,128)(2,1)S(1)} %bitcast.73), kind=kOutput, calls=%fused_computation.49 | convolution fusion | flops 547362816 | bytes 13893632 | tf_op jit(solution)/shard_map/div | solution.py:54
  46.8 0.0 copy-start
  46.8 0.0 collective-permute-done.2
  46.8 3.1 %bitcast_convert_fusion = (f32[4,256,128]{1,2,0:T(8,128)S(1)}, bf16[128,4,256]{2,0,1:T(8,128)(2,1)S(1)}) fusion(bf16[2048,128,1]{1,0,2:T(8,128)(2,1)S(1)} %bitcast.69, bf16[4,256,2048]{1,2,0:T(8,128)(2,1)} %get-tuple-element.8), kind=kOutput, calls=%fused_computation.37 | convolution fusion | flops 537133056 | bytes 5505024 | tf_op jit(solution)/shard_map/gtk,kd->tgd/dot_general | solution.py:59
  50.0 0.3 copy-done
  50.3 3.1 %fusion.3 = bf16[4096,256]{1,0:T(8,128)(2,1)} fusion(bf16[256,512]{0,1:T(8,128)(2,1)S(1)} %bitcast.76, bf16[512,4096]{1,0:T(8,128)(2,1)S(1)} %copy-done), kind=kOutput, calls=%fused_computation.7 | convolution fusion | flops 1074790400 | bytes 6553600 | tf_op jit(solution)/shard_map/dot_general | solution.py:63
  53.4 0.0 reduce-scatter.2.cloned.1.call-update
  53.4 0.2 copy.66
  53.7 4.8 %all-gather.2.cloned.1.call-done = bf16[4096,256]{1,0:T(8,128)(2,1)} async-done(((bf16[512,256]{1,0:T(8,128)(2,1)}), bf16[4096,256]{1,0:T(8,128)(2,1)}) %all-gather.2.cloned.1.call-update) | async-done | bytes 2097168 | tf_op jit(solution)/shard_map/all_gather | solution.py:67
  58.4 4.1 %fusion.9 = bf16[512,256]{0,1:T(8,128)(2,1)S(1)} fusion(bf16[4096,256]{1,0:T(8,128)(2,1)} %all-gather.2.cloned.1.call-done, bf16[512,4096]{1,0:T(8,128)(2,1)} %param.9), kind=kOutput, calls=%fused_computation.22 | convolution fusion | flops 1073872896 | bytes 6553600 | tf_op jit(solution)/shard_map/dot_general | solution.py:72
  62.6 0.1 reshape.157
  62.6 0.2 copy.54
  62.8 0.4 multiply_reduce_fusion
  63.2 0.1 copy.67
  63.2 3.7 %convolution_bitcast_fusion = f32[2048,128]{0,1:T(8,128)S(1)} fusion(bf16[4,256,2048]{1,2,0:T(8,128)(2,1)} %get-tuple-element.8, bf16[4,128,256]{2,1,0:T(8,128)(2,1)S(1)} %copy.54), kind=kOutput, calls=%fused_computation.15 | convolution fusion | flops 536870912 | bytes 5505024 | tf_op jit(solution)/shard_map/gtk,gdt->kd/dot_general | solution.py:91
  66.9 4.6 %multiply_convert_fusion = bf16[4,256,2048]{1,2,0:T(8,128)(2,1)S(1)} fusion(f32[4,256,2048]{1,2,0:T(8,128)} %get-tuple-element.34, bf16[2048,128,1]{1,0,2:T(8,128)(2,1)S(1)} %bitcast.70, bf16[4,128,256]{2,1,0:T(8,128)(2,1)S(1)} %copy.54, f32[4,256]{1,0:T(4,128)S(1)} %copy.67), kind=kOutput, calls=%fused_computation.3 | convolution fusion | flops 545259520 | bytes 13373440 | tf_op jit(solution)/shard_map/gdt,kd->gtk/dot_general | solution.py:81
  71.5 1.5 %convolution_bitcast_fusion.1 = f32[2048,128]{0,1:T(8,128)S(1)} fusion(bf16[4,256,2048]{1,2,0:T(8,128)(2,1)S(1)} %multiply_convert_fusion, bf16[256,4,128]{0,2,1:T(8,128)(2,1)S(1)} %bitcast.74), kind=kOutput, calls=%fused_computation.16 | convolution fusion | flops 536870912 | bytes 5505024 | tf_op jit(solution)/shard_map/gtk,tgd->kd/dot_general | solution.py:90
  73.0 0.1 fusion.8
  73.2 0.1 fusion.23
  73.2 1.3 %collective-permute-start.10 = (bf16[256,256]{0,1:T(8,128)(2,1)S(1)}, bf16[256,256]{0,1:T(8,128)(2,1)S(1)}, u32[]{:S(2)}, u32[]{:S(2)}) collective-permute-start(bf16[256,256]{0,1:T(8,128)(2,1)S(1)} %get-tuple-element.23), channel_id=1, source_target_pairs={{7,0},{8,1},{9,2},{10,3},{11,4},{12,5},{13,6},{14,7},{15,8},{16,9}... | collective-permute-start | bytes 393224 | tf_op jit(solution)/shard_map/ppermute | solution.py:15
  74.5 1.9 %collective-permute-start.4 = (bf16[256,256]{0,1:T(8,128)(2,1)S(1)}, bf16[256,256]{0,1:T(8,128)(2,1)S(1)}, u32[]{:S(2)}, u32[]{:S(2)}) collective-permute-start(bf16[256,256]{0,1:T(8,128)(2,1)S(1)} %get-tuple-element.22), channel_id=1, source_target_pairs={{1,0},{2,1},{3,2},{4,3},{5,4},{6,5},{7,6},{8,7},{9,8},{10,9},{11,1... | collective-permute-start | bytes 393224 | tf_op jit(solution)/shard_map/ppermute | solution.py:15
  76.5 2.8 %collective-permute-start.5 = (bf16[256,256]{0,1:T(8,128)(2,1)S(1)}, bf16[256,256]{0,1:T(8,128)(2,1)}, u32[]{:S(2)}, u32[]{:S(2)}) collective-permute-start(bf16[256,256]{0,1:T(8,128)(2,1)S(1)} %get-tuple-element.28), channel_id=1, source_target_pairs={{2,0},{3,1},{4,2},{5,3},{6,4},{7,5},{8,6},{9,7},{10,8},{11,9},{12,... | collective-permute-start | bytes 393224 | tf_op jit(solution)/shard_map/ppermute | solution.py:15
  79.3 2.6 %collective-permute-start.6 = (bf16[256,256]{0,1:T(8,128)(2,1)S(1)}, bf16[256,256]{0,1:T(8,128)(2,1)}, u32[]{:S(2)}, u32[]{:S(2)}) collective-permute-start(bf16[256,256]{0,1:T(8,128)(2,1)S(1)} %get-tuple-element.27), channel_id=1, source_target_pairs={{3,0},{4,1},{5,2},{6,3},{7,4},{8,5},{9,6},{10,7},{11,8},{12,9},{13... | collective-permute-start | bytes 393224 | tf_op jit(solution)/shard_map/ppermute | solution.py:15
  81.9 1.9 %collective-permute-start.7 = (bf16[256,256]{0,1:T(8,128)(2,1)S(1)}, bf16[256,256]{0,1:T(8,128)(2,1)}, u32[]{:S(2)}, u32[]{:S(2)}) collective-permute-start(bf16[256,256]{0,1:T(8,128)(2,1)S(1)} %get-tuple-element.26), channel_id=1, source_target_pairs={{4,0},{5,1},{6,2},{7,3},{8,4},{9,5},{10,6},{11,7},{12,8},{13,9},{1... | collective-permute-start | bytes 393224 | tf_op jit(solution)/shard_map/ppermute | solution.py:15
  83.9 0.0 collective-permute-done.10
  83.9 0.0 copy-start.1
  83.9 1.9 %collective-permute-start.8 = (bf16[256,256]{0,1:T(8,128)(2,1)S(1)}, bf16[256,256]{0,1:T(8,128)(2,1)}, u32[]{:S(2)}, u32[]{:S(2)}) collective-permute-start(bf16[256,256]{0,1:T(8,128)(2,1)S(1)} %get-tuple-element.25), channel_id=1, source_target_pairs={{5,0},{6,1},{7,2},{8,3},{9,4},{10,5},{11,6},{12,7},{13,8},{14,9},{... | collective-permute-start | bytes 393224 | tf_op jit(solution)/shard_map/ppermute | solution.py:15
  85.8 0.0 collective-permute-done.4
  85.8 0.0 copy-start.2
  85.8 0.0 copy-done.1
  85.8 0.6 copy-done.2
  86.5 1.9 %collective-permute-start.9 = (bf16[256,256]{0,1:T(8,128)(2,1)S(1)}, bf16[256,256]{0,1:T(8,128)(2,1)}, u32[]{:S(2)}, u32[]{:S(2)}) collective-permute-start(bf16[256,256]{0,1:T(8,128)(2,1)S(1)} %get-tuple-element.24), channel_id=1, source_target_pairs={{6,0},{7,1},{8,2},{9,3},{10,4},{11,5},{12,6},{13,7},{14,8},{15,9},... | collective-permute-start | bytes 393224 | tf_op jit(solution)/shard_map/ppermute | solution.py:15
  88.4 0.8 convolution_convert_fusion.2
  89.1 0.8 copy.55
  90.0 0.0 collective-permute-done.5
  90.0 0.0 collective-permute-done.6
  90.0 3.5 %collective-permute-done.7 = bf16[256,256]{0,1:T(8,128)(2,1)} collective-permute-done((bf16[256,256]{0,1:T(8,128)(2,1)S(1)}, bf16[256,256]{0,1:T(8,128)(2,1)}, u32[]{:S(2)}, u32[]{:S(2)}) %collective-permute-start.7) | collective-permute-done | bytes 131104 | tf_op jit(solution)/shard_map/ppermute | solution.py:15
  93.5 1.8 %collective-permute-done.8 = bf16[256,256]{0,1:T(8,128)(2,1)} collective-permute-done((bf16[256,256]{0,1:T(8,128)(2,1)S(1)}, bf16[256,256]{0,1:T(8,128)(2,1)}, u32[]{:S(2)}, u32[]{:S(2)}) %collective-permute-start.8) | collective-permute-done | bytes 131104 | tf_op jit(solution)/shard_map/ppermute | solution.py:15
  95.3 1.6 %collective-permute-done.9 = bf16[256,256]{0,1:T(8,128)(2,1)} collective-permute-done((bf16[256,256]{0,1:T(8,128)(2,1)S(1)}, bf16[256,256]{0,1:T(8,128)(2,1)}, u32[]{:S(2)}, u32[]{:S(2)}) %collective-permute-start.9) | collective-permute-done | bytes 131104 | tf_op jit(solution)/shard_map/ppermute | solution.py:15
  96.8 1.4 %fusion.20 = bf16[256,256]{0,1:T(8,128)(2,1)S(1)} fusion(bf16[256,256]{0,1:T(8,128)(2,1)} %copy-done.1, bf16[256,256]{0,1:T(8,128)(2,1)} %collective-permute-done.9, bf16[256,256]{0,1:T(8,128)(2,1)} %collective-permute-done.8, bf16[256,256]{0,1:T(8,128)(2,1)} %collective-permute-done.7, bf16[256,256]{0,1:T(8,128)(2,1)} %collective-permute-done.6, ...), kind=kLoop, calls=%fused_computation.38 | loop fusion | flops 1048576 | bytes 3145728 | tf_op jit(solution)/shard_map/convert.1
  98.2 0.7 copy.56
  99.0 0.7 copy.57
  99.7 5.4 %reduce-scatter.2.cloned.1.call-done = bf16[512,256]{1,0:T(8,128)(2,1)} async-done(((bf16[4096,256]{1,0:T(8,128)(2,1)}), bf16[512,256]{1,0:T(8,128)(2,1)}) %reduce-scatter.2.cloned.1.call-update) | async-done | bytes 262160 | tf_op jit(solution)/shard_map/reduce_scatter | solution.py:68
  (8 shorter events, 0.2 us)
Async XLA Ops:
  7.2 51.3 %all-gather.2.cloned.1.call-start = ((), (), s32[]{:S(2)}) async-start(), calls=%async_computation.2 | async-start | bytes 2359296 | tf_op jit(solution)/shard_map/all_gather | solution.py:67
  7.9 97.2 %reduce-scatter.2.cloned.1.call-start = ((), (), s32[]{:S(2)}) async-start(), calls=%async_computation.1 | async-start | bytes 2359296 | tf_op jit(solution)/shard_map/reduce_scatter | solution.py:68
  8.8 6.3 %collective-permute-start = (bf16[1,256,256]{2,1,0:T(8,128)(2,1)S(1)}, bf16[1,256,256]{2,1,0:T(8,128)(2,1)S(1)}, u32[]{:S(2)}, u32[]{:S(2)}) collective-permute-start(bf16[1,256,256]{2,1,0:T(8,128)(2,1)S(1)} %maximum_bitcast_fusion), channel_id=1, source_target_pairs={{0,1},{1,2},{2,3},{3,4},{4,5},{5,6},{6,7},{7,8},{8,9},{9,10},{10,1... | collective-permute-start | bytes 393224 | tf_op jit(solution)/shard_map/ppermute | solution.py:15
  15.2 10.2 %collective-permute-start.1 = (bf16[2,256,256]{2,1,0:T(8,128)(2,1)S(1)}, bf16[2,256,256]{2,1,0:T(8,128)(2,1)S(1)}, u32[]{:S(2)}, u32[]{:S(2)}) collective-permute-start(bf16[2,256,256]{2,1,0:T(8,128)(2,1)S(1)} %pad_maximum_fusion.4), channel_id=1, source_target_pairs={{0,2},{1,3},{2,4},{3,5},{4,6},{5,7},{6,8},{7,9},{8,10},{9,11},{10,... | collective-permute-start | bytes 786440 | tf_op jit(solution)/shard_map/ppermute | solution.py:15
  25.5 12.6 %collective-permute-start.3 = (bf16[4,256,128]{2,1,0:T(8,128)(2,1)S(1)}, bf16[4,256,128]{2,1,0:T(8,128)(2,1)S(1)}, u32[]{:S(2)}, u32[]{:S(2)}) collective-permute-start(bf16[4,256,128]{2,1,0:T(8,128)(2,1)S(1)} %get-tuple-element.29), channel_id=1, source_target_pairs={{0,4},{1,5},{2,6},{3,7},{4,8},{5,9},{6,10},{7,11},{8,12},{9,13},{1... | collective-permute-start | bytes 786440 | tf_op jit(solution)/shard_map/ppermute | solution.py:15
  30.3 16.5 %collective-permute-start.2 = (bf16[4,256,128]{2,1,0:T(8,128)(2,1)S(1)}, bf16[4,256,128]{2,1,0:T(8,128)(2,1)S(1)}, u32[]{:S(2)}, u32[]{:S(2)}) collective-permute-start(bf16[4,256,128]{2,1,0:T(8,128)(2,1)S(1)} %get-tuple-element.30), channel_id=1, source_target_pairs={{0,4},{1,5},{2,6},{3,7},{4,8},{5,9},{6,10},{7,11},{8,12},{9,13},{1... | collective-permute-start | bytes 786440 | tf_op jit(solution)/shard_map/ppermute | solution.py:15
  46.8 3.5 %copy-start = (bf16[512,4096]{1,0:T(8,128)(2,1)S(1)}, bf16[512,4096]{1,0:T(8,128)(2,1)}, u32[]{:S(2)}) copy-start(bf16[512,4096]{1,0:T(8,128)(2,1)} %param.9) | copy-start | bytes 12582916
  73.2 10.6 %collective-permute-start.10 = (bf16[256,256]{0,1:T(8,128)(2,1)S(1)}, bf16[256,256]{0,1:T(8,128)(2,1)S(1)}, u32[]{:S(2)}, u32[]{:S(2)}) collective-permute-start(bf16[256,256]{0,1:T(8,128)(2,1)S(1)} %get-tuple-element.23), channel_id=1, source_target_pairs={{7,0},{8,1},{9,2},{10,3},{11,4},{12,5},{13,6},{14,7},{15,8},{16,9}... | collective-permute-start | bytes 393224 | tf_op jit(solution)/shard_map/ppermute | solution.py:15
  74.5 11.3 %collective-permute-start.4 = (bf16[256,256]{0,1:T(8,128)(2,1)S(1)}, bf16[256,256]{0,1:T(8,128)(2,1)S(1)}, u32[]{:S(2)}, u32[]{:S(2)}) collective-permute-start(bf16[256,256]{0,1:T(8,128)(2,1)S(1)} %get-tuple-element.22), channel_id=1, source_target_pairs={{1,0},{2,1},{3,2},{4,3},{5,4},{6,5},{7,6},{8,7},{9,8},{10,9},{11,1... | collective-permute-start | bytes 393224 | tf_op jit(solution)/shard_map/ppermute | solution.py:15
  76.5 13.5 %collective-permute-start.5 = (bf16[256,256]{0,1:T(8,128)(2,1)S(1)}, bf16[256,256]{0,1:T(8,128)(2,1)}, u32[]{:S(2)}, u32[]{:S(2)}) collective-permute-start(bf16[256,256]{0,1:T(8,128)(2,1)S(1)} %get-tuple-element.28), channel_id=1, source_target_pairs={{2,0},{3,1},{4,2},{5,3},{6,4},{7,5},{8,6},{9,7},{10,8},{11,9},{12,... | collective-permute-start | bytes 393224 | tf_op jit(solution)/shard_map/ppermute | solution.py:15
  79.3 10.7 %collective-permute-start.6 = (bf16[256,256]{0,1:T(8,128)(2,1)S(1)}, bf16[256,256]{0,1:T(8,128)(2,1)}, u32[]{:S(2)}, u32[]{:S(2)}) collective-permute-start(bf16[256,256]{0,1:T(8,128)(2,1)S(1)} %get-tuple-element.27), channel_id=1, source_target_pairs={{3,0},{4,1},{5,2},{6,3},{7,4},{8,5},{9,6},{10,7},{11,8},{12,9},{13... | collective-permute-start | bytes 393224 | tf_op jit(solution)/shard_map/ppermute | solution.py:15
  81.9 11.6 %collective-permute-start.7 = (bf16[256,256]{0,1:T(8,128)(2,1)S(1)}, bf16[256,256]{0,1:T(8,128)(2,1)}, u32[]{:S(2)}, u32[]{:S(2)}) collective-permute-start(bf16[256,256]{0,1:T(8,128)(2,1)S(1)} %get-tuple-element.26), channel_id=1, source_target_pairs={{4,0},{5,1},{6,2},{7,3},{8,4},{9,5},{10,6},{11,7},{12,8},{13,9},{1... | collective-permute-start | bytes 393224 | tf_op jit(solution)/shard_map/ppermute | solution.py:15
  83.9 2.0 %copy-start.1 = (bf16[256,256]{0,1:T(8,128)(2,1)}, bf16[256,256]{0,1:T(8,128)(2,1)S(1)}, u32[]{:S(2)}) copy-start(bf16[256,256]{0,1:T(8,128)(2,1)S(1)} %collective-permute-done.10) | copy-start | bytes 393220
  83.9 11.4 %collective-permute-start.8 = (bf16[256,256]{0,1:T(8,128)(2,1)S(1)}, bf16[256,256]{0,1:T(8,128)(2,1)}, u32[]{:S(2)}, u32[]{:S(2)}) collective-permute-start(bf16[256,256]{0,1:T(8,128)(2,1)S(1)} %get-tuple-element.25), channel_id=1, source_target_pairs={{5,0},{6,1},{7,2},{8,3},{9,4},{10,5},{11,6},{12,7},{13,8},{14,9},{... | collective-permute-start | bytes 393224 | tf_op jit(solution)/shard_map/ppermute | solution.py:15
  85.8 0.7 copy-start.2
  86.5 10.4 %collective-permute-start.9 = (bf16[256,256]{0,1:T(8,128)(2,1)S(1)}, bf16[256,256]{0,1:T(8,128)(2,1)}, u32[]{:S(2)}, u32[]{:S(2)}) collective-permute-start(bf16[256,256]{0,1:T(8,128)(2,1)S(1)} %get-tuple-element.24), channel_id=1, source_target_pairs={{6,0},{7,1},{8,2},{9,3},{10,4},{11,5},{12,6},{13,7},{14,8},{15,9},... | collective-permute-start | bytes 393224 | tf_op jit(solution)/shard_map/ppermute | solution.py:15
Sparse Core Ops, SparseCore 0:
  10.1 48.3 all-gather.1
  61.8 43.2 reduce-scatter.1
